TPU v7x, 512 devices: a whole 4x4x16 slice. The times are simulated.
512 devices in a mesh: head: 8 (over x, core), expert: 64 (over z, y).
Axes of the slice: x: 4, y: 4, z: 16, core: 2. Of those that a mesh axis runs over, the one named last changes fastest.
Arguments:
- q_latent: bfloat16 [512, 64, 512], P('expert', 'head'), may hold values from -16 to 16
- q_rotary: bfloat16 [512, 64, 64], P('expert', 'head'), may hold values from -3 to 3
- cache_latent: bfloat16 [512, 128, 512], P('expert'), may hold values from -5 to 5
- cache_rotary: bfloat16 [512, 64, 128], P('expert'), may hold values from -5 to 5
- lengths: int32 [512], P('expert'), may hold values from 16 to 128, as said below
- w_value_out: bfloat16 [32768, 5120], P('head', 'expert'), may hold values from -0.25 to 0.25
- resid: bfloat16 [512, 5120], P('expert'), may hold values from -8 to 8
- norm_gain: float32 [5120], replicated, may hold values from 0.1 to 1.9
- route_ids: int32 [512, 6], P('expert'), may hold values from 0 to 63, as said below
- route_weights: float32 [512, 6], P('expert'), may hold values from 0.1 to 0.6
- w_gate_up: bfloat16 [64, 2, 768, 5120], P('expert', None, 'head'), may hold values from -0.078125 to 0.078125
- w_down: bfloat16 [64, 768, 5120], P('expert', 'head'), may hold values from -0.21875 to 0.21875
Outputs:
- mixed_out: float32 [512, 5120], P('expert', 'head')
Inputs may be any that keep to these rules, and one draw needn't show every extreme that they name: `lengths`: slots at positions below a sequence's length are valid; some sequence has length 128. `route_ids`: each row names 6 different experts. Among the rows of one device (aligned blocks of 8 rows) no expert is named by more than 2 rows, and one expert is named by exactly 2 rows in every block.
All inputs are finite; a program needn't handle non-finite values.
Results may differ from a plain program's by a relative error of at most 0.0046.
Values may be sent and summed in bfloat16 or wider, within the bound.
No kernel may reach another device: no remote copies, remote signals or barrier semaphores. Data moves between devices by JAX's collectives and lax.ppermute only.
A program may use at most 64 MiB of HBM per device.

v0:
```python
import jax
import jax.numpy as jnp
from jax import lax
from jax.sharding import PartitionSpec as P

softmax_scale = 192.0 ** (-0.5)
norm_epsilon = 1e-06


def attend(q_latent, q_rotary, cache_latent, cache_rotary, lengths):
    scores = jnp.einsum("shl,scl->shc", q_latent, cache_latent, preferred_element_type=jnp.float32)
    scores = scores + jnp.einsum(
        "shr,src->shc", q_rotary, cache_rotary, preferred_element_type=jnp.float32
    )
    scores = scores * softmax_scale
    position = lax.broadcasted_iota(jnp.int32, scores.shape, 2)
    scores = jnp.where(position < lengths[:, None, None], scores, -1e30)
    highest = jnp.max(scores, axis=2, keepdims=True)
    weights = jnp.exp(scores - highest)
    probs = (weights / jnp.sum(weights, axis=2, keepdims=True)).astype(jnp.bfloat16)
    return jnp.einsum(
        "shc,scl->shl", probs, cache_latent, preferred_element_type=jnp.float32
    ).astype(jnp.bfloat16)


def on_device(
    q_latent,
    q_rotary,
    cache_latent,
    cache_rotary,
    lengths,
    w_value_out,
    resid,
    norm_gain,
    route_ids,
    route_weights,
    w_gate_up,
    w_down,
):
    seq_local = q_latent.shape[0]
    latent_out = attend(q_latent, q_rotary, cache_latent, cache_rotary, lengths)
    flattened = latent_out.reshape(seq_local, -1)
    column_terms = jnp.dot(
        lax.all_gather(flattened, "expert", axis=0, tiled=True),
        w_value_out,
        preferred_element_type=jnp.float32,
    )
    column_sums = lax.psum(column_terms, "head")
    attention = lax.all_to_all(
        column_sums.astype(jnp.bfloat16), "expert", split_axis=0, concat_axis=1, tiled=True
    )
    stream = resid.astype(jnp.float32) + attention.astype(jnp.float32)
    mean_square = jnp.mean(stream * stream, axis=1, keepdims=True)
    normed = (stream * lax.rsqrt(mean_square + norm_epsilon) * norm_gain).astype(jnp.bfloat16)
    expert_count = lax.axis_size("expert")
    top_count = route_ids.shape[1]
    capacity = max(2, -(-(seq_local * top_count) // expert_count))
    flat_ids = route_ids.reshape(-1)
    one_hot = (flat_ids[:, None] == jnp.arange(expert_count, dtype=jnp.int32)[None, :]).astype(
        jnp.int32
    )
    earlier = jnp.cumsum(one_hot, axis=0) - one_hot
    slot_index = jnp.sum(earlier * one_hot, axis=1)
    target = (flat_ids * capacity + slot_index).reshape(seq_local, top_count)
    places = jnp.arange(expert_count * capacity, dtype=jnp.int32)
    matches = target[None, :, :] == places[:, None, None]
    selector = jnp.sum(matches.astype(jnp.int32), axis=2).astype(jnp.bfloat16)
    blending = jnp.sum(jnp.where(matches, route_weights[None, :, :], 0.0), axis=2)
    outgoing = jnp.dot(selector, normed, preferred_element_type=jnp.float32).astype(jnp.bfloat16)
    outgoing = outgoing.reshape(expert_count, capacity, -1)
    gate_up = w_gate_up[0]
    down_local = w_down[0]
    col_width = stream.shape[1] // lax.axis_size("head")
    offset = lax.axis_index("head") * col_width
    arrived = lax.all_to_all(outgoing, "expert", split_axis=0, concat_axis=0, tiled=True)
    flat_rows = arrived.reshape(-1, arrived.shape[2])
    projected = jnp.einsum("rd,gfd->rgf", flat_rows, gate_up, preferred_element_type=jnp.float32)
    hidden = (jax.nn.silu(projected[:, 0]) * projected[:, 1]).astype(jnp.bfloat16)
    partial_rows = jnp.dot(hidden, down_local, preferred_element_type=jnp.float32)
    expert_terms = partial_rows.reshape(arrived.shape[0], arrived.shape[1], -1)
    summed_rows = lax.psum(expert_terms.astype(jnp.bfloat16), "head")
    returned = lax.all_to_all(summed_rows, "expert", split_axis=0, concat_axis=0, tiled=True)
    back_rows = returned.reshape(expert_count * capacity, -1).astype(jnp.float32)
    mixture = jnp.dot(blending.T, back_rows, precision=lax.Precision.HIGHEST)
    mixed_full = stream + mixture
    return lax.dynamic_slice_in_dim(mixed_full, offset, col_width, 1)


def solution(mesh):
    placed = (
        P("expert", "head", None),
        P("expert", "head", None),
        P("expert", None, None),
        P("expert", None, None),
        P("expert"),
        P("head", "expert"),
        P("expert", None),
        P(),
        P("expert", None),
        P("expert", None),
        P("expert", None, "head", None),
        P("expert", "head", None),
    )
    return jax.shard_map(
        on_device, mesh=mesh, in_specs=placed, out_specs=P("expert", "head"), check_vma=False
    )
```

profile of v0, /device:TPU:6, one launch (start us, length us, event | category | flops | bytes accessed | tf_op | source)
XLA Modules:
  0.0 461.4 jit_solution(11301402010040664374)
XLA Ops:
  6.5 0.0 copy-start
  6.5 0.0 copy-start.1
  6.5 0.0 copy-start.4
  6.5 0.0 all-gather.2.cloned.1.call-start
  6.5 1.8 fusion.17
  8.3 1.1 fusion.7
  9.4 0.2 fusion.16
  9.6 0.0 copy-done.1
  9.6 0.3 fusion.3
  9.9 0.7 copy.32
  10.5 0.0 all-gather.2.cloned.1.call-update
  10.6 0.0 copy-done.4
  10.6 0.1 eq.28
  10.7 0.1 fusion.13
  10.7 0.1 reduce_window_sum.11
  10.8 0.2 select_reduce_fusion.1
  11.0 0.1 reduce_sum.49
  11.1 150.7 %all-gather.2.cloned.1.call-done = bf16[512,4096]{1,0:T(8,128)(2,1)} async-done(((bf16[8,4096]{1,0:T(8,128)(2,1)}), bf16[512,4096]{1,0:T(8,128)(2,1)}) %all-gather.2.cloned.1.call-update) | async-done | bytes 4194320 | tf_op jit(solution)/shard_map/all_gather | solution.py:44
  161.7 3.7 fusion.18
  165.5 0.0 copy-start.2
  165.5 0.0 copy-start.3
  165.5 22.2 %all-reduce.4 = bf16[512,80]{0,1:T(8,128)(2,1)S(1)} all-reduce(f32[512,80]{0,1:T(8,128)S(1)} %fusion.18), channel_id=1, replica_groups=mesh['head'=8,'expert'=64] {'head'}, use_global_device_ids=true, to_apply=%region_2.3 | all-reduce | flops 40960 | bytes 245760 | tf_op jit(solution)/shard_map/psum | solution.py:48
  187.7 0.7 copy.25
  188.5 8.9 %all-to-all-start = ((bf16[64,8,80]{2,1,0:T(8,128)(2,1)}), bf16[64,8,80]{2,1,0:T(8,128)(2,1)S(1)}, u32[]{:S(2)}, u32[]{:S(2)}) async-start(bf16[64,8,80]{2,1,0:T(8,128)(2,1)} %bitcast), calls=%async_computation | async-start | bytes 262144 | tf_op jit(solution)/shard_map/all_to_all | solution.py:49
  197.4 0.0 all-reduce.3.cloned.1.call-start
  197.4 0.1 copy.27
  197.5 0.1 convert_reduce_fusion
  197.6 18.3 %all-to-all-done = bf16[64,8,80]{2,1,0:T(8,128)(2,1)S(1)} async-done(((bf16[64,8,80]{2,1,0:T(8,128)(2,1)}), bf16[64,8,80]{2,1,0:T(8,128)(2,1)S(1)}, u32[]{:S(2)}, u32[]{:S(2)}) %all-to-all-start) | async-done | bytes 81952 | tf_op jit(solution)/shard_map/all_to_all | solution.py:49
  215.9 0.1 copy.26
  216.0 0.2 reshape.47
  216.2 0.0 copy-done.2
  216.2 0.2 multiply_reduce_fusion
  216.3 0.0 copy-done.3
  216.4 0.6 convolution_convert_fusion.1
  216.9 1.4 reshape.44
  218.3 70.5 %all_to_all.23 = bf16[64,2,5120]{2,1,0:T(2,128)(2,1)} all-to-all(bf16[64,2,5120]{2,1,0:T(2,128)(2,1)} %reshape.44), channel_id=1, replica_groups=mesh['head'=8,'expert'=64] {'expert'}, dimensions={0} | all-to-all | bytes 2621440 | tf_op jit(solution)/shard_map/all_to_all | solution.py:75
  288.8 3.1 reshape.48
  291.9 0.0 copy-done
  292.0 0.7 fusion.1
  292.7 0.1 copy.29
  292.8 2.8 convolution_convert_fusion
  295.6 0.0 all-reduce.3.cloned.1.call-update
  295.6 67.7 %all-reduce.3.cloned.1.call-done = bf16[64,2,5120]{2,0,1:T(8,128)(2,1)} async-done(((bf16[64,2,5120]{2,0,1:T(8,128)(2,1)}), bf16[64,2,5120]{2,0,1:T(8,128)(2,1)}) %all-reduce.3.cloned.1.call-update) | async-done | bytes 1310736 | tf_op jit(solution)/shard_map/psum | solution.py:81
  363.3 3.7 copy.31
  367.1 0.0 copy-start.5
  367.1 15.8 %all-to-all-start.2 = ((bf16[64,2,5120]{2,1,0:T(2,128)(2,1)}), bf16[64,2,5120]{2,1,0:T(2,128)(2,1)S(1)}, u32[]{:S(2)}, u32[]{:S(2)}) async-start(bf16[64,2,5120]{2,1,0:T(2,128)(2,1)} %copy.31), calls=%async_computation.2 | async-start | bytes 2621440 | tf_op jit(solution)/shard_map/all_to_all | solution.py:82
  382.9 0.0 copy-done.5
  382.9 0.1 copy.28
  383.0 0.1 select_reduce_fusion
  383.0 67.6 %all-to-all-done.2 = bf16[64,2,5120]{2,1,0:T(2,128)(2,1)S(1)} async-done(((bf16[64,2,5120]{2,1,0:T(2,128)(2,1)}), bf16[64,2,5120]{2,1,0:T(2,128)(2,1)S(1)}, u32[]{:S(2)}, u32[]{:S(2)}) %all-to-all-start.2) | async-done | bytes 1310752 | tf_op jit(solution)/shard_map/all_to_all | solution.py:82
  450.6 1.4 reshape.46
  452.0 1.9 fusion.19
  453.9 0.6 dynamic-slice_add_fusion
  (4 shorter events, 0.1 us)
Async XLA Ops:
  6.5 285.4 %copy-start = (bf16[1,2,96,5120]{3,2,1,0:T(8,128)(2,1)S(1)}, bf16[1,2,96,5120]{3,2,1,0:T(8,128)(2,1)}, u32[]{:S(2)}) copy-start(bf16[1,2,96,5120]{3,2,1,0:T(8,128)(2,1)} %param.22) | copy-start | bytes 5898244
  6.5 3.0 copy-start.1
  6.5 4.0 copy-start.4
  6.5 155.2 %all-gather.2.cloned.1.call-start = ((), (), s32[]{:S(2)}) async-start(), calls=%async_computation.3 | async-start | bytes 4259840 | tf_op jit(solution)/shard_map/all_gather | solution.py:44
  165.5 50.7 %copy-start.2 = (bf16[8,5120]{1,0:T(8,128)(2,1)S(1)}, bf16[8,5120]{1,0:T(8,128)(2,1)}, u32[]{:S(2)}) copy-start(bf16[8,5120]{1,0:T(8,128)(2,1)} %param.18) | copy-start | bytes 245764
  165.5 50.9 %copy-start.3 = (f32[5120]{0:T(1024)S(1)}, f32[5120]{0:T(1024)}, u32[]{:S(2)}) copy-start(f32[5120]{0:T(1024)} %param.19) | copy-start | bytes 61444
  188.5 27.5 %all-to-all-start = ((bf16[64,8,80]{2,1,0:T(8,128)(2,1)}), bf16[64,8,80]{2,1,0:T(8,128)(2,1)S(1)}, u32[]{:S(2)}, u32[]{:S(2)}) async-start(bf16[64,8,80]{2,1,0:T(8,128)(2,1)} %bitcast), calls=%async_computation | async-start | bytes 262144 | tf_op jit(solution)/shard_map/all_to_all | solution.py:49
  197.4 166.0 %all-reduce.3.cloned.1.call-start = ((), (), s32[]{:S(2)}) async-start(), calls=%async_computation.4 | async-start | bytes 2621440 | tf_op jit(solution)/shard_map/psum | solution.py:81
  367.1 15.8 %copy-start.5 = (f32[8,6]{1,0:T(8,128)S(1)}, f32[8,6]{1,0:T(8,128)}, u32[]{:S(2)}) copy-start(f32[8,6]{1,0:T(8,128)} %param.21) | copy-start | bytes 580
  367.1 83.6 %all-to-all-start.2 = ((bf16[64,2,5120]{2,1,0:T(2,128)(2,1)}), bf16[64,2,5120]{2,1,0:T(2,128)(2,1)S(1)}, u32[]{:S(2)}, u32[]{:S(2)}) async-start(bf16[64,2,5120]{2,1,0:T(2,128)(2,1)} %copy.31), calls=%async_computation.2 | async-start | bytes 2621440 | tf_op jit(solution)/shard_map/all_to_all | solution.py:82
Sparse Core Ops, SparseCore 0:
  10.7 151.0 all-gather.1
  295.7 67.5 all-reduce.2
where the time goes:
time: 462 us; the launch traced here: 461 us
  waiting for transfers between devices  304 us (66%)
  blocking collectives  92.7 us (20%)
  starting transfers between devices  24.7 us (5%)
  between operations  13.6 us (3%)
  matrix products  12.8 us (3%)
  local copies, waits for them, and re-layouts  11.7 us (3%)
    all_gather x1, waiting for transfers between devices, on_device(): lax.all_gather(flattened, 'expert', axis=0, tiled=True)  151 us
    all_to_all x1, blocking collectives, on_device(): lax.all_to_all(outgoing, 'expert', split_axis=0, concat_axis=0, tiled=True)  70.5 us
    psum x1, waiting for transfers between devices, on_device(): summed_rows = lax.psum(expert_terms.astype(jnp.bfloat16), 'head')  67.7 us
    all_to_all x1, waiting for transfers between devices, on_device(): lax.all_to_all(summed_rows, 'expert', split_axis=0, concat_axis=0, tiled=...  67.6 us
    psum x1, blocking collectives, on_device(): column_sums = lax.psum(column_terms, 'head')  22.2 us
    all_to_all x1, waiting for transfers between devices, on_device(): lax.all_to_all(column_sums.astype(jnp.bfloat16), 'expert', split_axis=0,...  18.3 us
    all_to_all x1, starting transfers between devices, on_device(): lax.all_to_all(summed_rows, 'expert', split_axis=0, concat_axis=0, tiled=...  15.8 us
  transfers between devices with their start and end apart: 4, of which 4 were waited for; matrix products, arithmetic and copies ran while one was open for 0% of the time, Pallas kernels for 0%

commit v1 on v0

--- a/solution.py
+++ b/solution.py
@@ -66,24 +66,28 @@
     matches = target[None, :, :] == places[:, None, None]
     selector = jnp.sum(matches.astype(jnp.int32), axis=2).astype(jnp.bfloat16)
     blending = jnp.sum(jnp.where(matches, route_weights[None, :, :], 0.0), axis=2)
-    outgoing = jnp.dot(selector, normed, preferred_element_type=jnp.float32).astype(jnp.bfloat16)
-    outgoing = outgoing.reshape(expert_count, capacity, -1)
     gate_up = w_gate_up[0]
     down_local = w_down[0]
     col_width = stream.shape[1] // lax.axis_size("head")
     offset = lax.axis_index("head") * col_width
+    normed_cols = lax.dynamic_slice_in_dim(normed, offset, col_width, 1)
+    outgoing = jnp.dot(selector, normed_cols, preferred_element_type=jnp.float32).astype(jnp.bfloat16)
+    outgoing = outgoing.reshape(expert_count, capacity, -1)
     arrived = lax.all_to_all(outgoing, "expert", split_axis=0, concat_axis=0, tiled=True)
-    flat_rows = arrived.reshape(-1, arrived.shape[2])
+    arrived_cols = arrived.reshape(-1, arrived.shape[2])
+    flat_rows = lax.all_gather(arrived_cols, "head", axis=1, tiled=True)
     projected = jnp.einsum("rd,gfd->rgf", flat_rows, gate_up, preferred_element_type=jnp.float32)
     hidden = (jax.nn.silu(projected[:, 0]) * projected[:, 1]).astype(jnp.bfloat16)
     partial_rows = jnp.dot(hidden, down_local, preferred_element_type=jnp.float32)
-    expert_terms = partial_rows.reshape(arrived.shape[0], arrived.shape[1], -1)
-    summed_rows = lax.psum(expert_terms.astype(jnp.bfloat16), "head")
+    summed_cols = lax.psum_scatter(
+        partial_rows.astype(jnp.bfloat16), "head", scatter_dimension=1, tiled=True
+    )
+    summed_rows = summed_cols.reshape(expert_count, capacity, -1)
     returned = lax.all_to_all(summed_rows, "expert", split_axis=0, concat_axis=0, tiled=True)
     back_rows = returned.reshape(expert_count * capacity, -1).astype(jnp.float32)
     mixture = jnp.dot(blending.T, back_rows, precision=lax.Precision.HIGHEST)
-    mixed_full = stream + mixture
-    return lax.dynamic_slice_in_dim(mixed_full, offset, col_width, 1)
+    stream_cols = lax.dynamic_slice_in_dim(stream, offset, col_width, 1)
+    return stream_cols + mixture
 
 
 def solution(mesh):

time: 462 us -> 350 us (0.76)
  waiting for transfers between devices: 304 us -> 246 us
  blocking collectives: 92.7 us -> 44.8 us
  local copies, waits for them, and re-layouts: 11.7 us -> 6.86 us
    psum x1 -> x0, waiting for transfers between devices: 67.7 us -> none  [on_device(): summed_rows = lax.psum(expert_terms.astype(jnp.bfloat16), 'head')]
    all_to_all x1, waiting for transfers between devices: 67.6 us -> 19 us  [on_device(): lax.all_to_all(summed_rows, 'expert', split_axis=0, concat_axis=0, tiled=...]
    all_to_all x1, blocking collectives: 70.5 us -> 22.6 us  [on_device(): lax.all_to_all(outgoing, 'expert', split_axis=0, concat_axis=0, tiled=True)]
    unnamed x2 -> x4, waiting for transfers between devices: 0.03 us -> 38.3 us
    all_gather x0 -> x1, waiting for transfers between devices: none -> 20 us  [on_device(): flat_rows = lax.all_gather(arrived_cols, 'head', axis=1, tiled=True)]
  transfers between devices with their start and end apart: 4 -> 5, of which waited for: 4 -> 5; matrix products, arithmetic and copies ran while one was open for 0% -> 0% of each run, Pallas kernels for 0% -> 0%
where the time goes in v1:
time: 350 us; the launch traced here: 349 us
  waiting for transfers between devices  246 us (70%)
  blocking collectives  44.8 us (13%)
  starting transfers between devices  24.6 us (7%)
  between operations  13.2 us (4%)
  matrix products  12.8 us (4%)
  local copies, waits for them, and re-layouts  6.86 us (2%)
    all_gather x1, waiting for transfers between devices, on_device(): lax.all_gather(flattened, 'expert', axis=0, tiled=True)  151 us
    unnamed x4, waiting for transfers between devices  38.3 us
    all_to_all x1, blocking collectives, on_device(): lax.all_to_all(outgoing, 'expert', split_axis=0, concat_axis=0, tiled=True)  22.6 us
    psum x1, blocking collectives, on_device(): column_sums = lax.psum(column_terms, 'head')  22.2 us
    all_gather x1, waiting for transfers between devices, on_device(): flat_rows = lax.all_gather(arrived_cols, 'head', axis=1, tiled=True)  20 us
    all_to_all x1, waiting for transfers between devices, on_device(): lax.all_to_all(summed_rows, 'expert', split_axis=0, concat_axis=0, tiled=...  19 us
    all_to_all x1, waiting for transfers between devices, on_device(): lax.all_to_all(column_sums.astype(jnp.bfloat16), 'expert', split_axis=0,...  17.6 us
    all_to_all x1, starting transfers between devices, on_device(): lax.all_to_all(summed_rows, 'expert', split_axis=0, concat_axis=0, tiled=...  15.6 us
  transfers between devices with their start and end apart: 5, of which 5 were waited for; matrix products, arithmetic and copies ran while one was open for 0% of the time, Pallas kernels for 0%

profile of v1, /device:TPU:6, one launch (start us, length us, event | category | flops | bytes accessed | tf_op | source)
XLA Modules:
  0.0 348.7 jit_solution(5322238232163485525)
XLA Ops:
  6.5 0.0 copy-start
  6.5 0.0 copy-start.3
  6.5 0.0 copy-start.1
  6.5 0.0 all-gather.3.cloned.1.call-start
  6.5 1.8 fusion.21
  8.3 1.1 fusion.8
  9.4 0.2 fusion.20
  9.6 1.5 fusion.4
  11.1 0.7 copy.24
  11.8 0.0 all-gather.3.cloned.1.call-update
  11.8 0.0 copy-done.3
  11.8 0.1 eq.28
  11.9 0.1 fusion.13
  12.0 0.1 reduce_window_sum.11
  12.0 0.2 select_reduce_fusion.1
  12.2 0.1 reduce_sum.49
  12.3 150.7 %all-gather.3.cloned.1.call-done = bf16[512,4096]{1,0:T(8,128)(2,1)} async-done(((bf16[8,4096]{1,0:T(8,128)(2,1)}), bf16[512,4096]{1,0:T(8,128)(2,1)}) %all-gather.3.cloned.1.call-update) | async-done | bytes 4194320 | tf_op jit(solution)/shard_map/all_gather | solution.py:44
  163.0 0.0 copy-done.1
  163.0 3.6 %fusion.22 = f32[512,80]{0,1:T(8,128)S(1)} fusion(bf16[512,4096]{1,0:T(8,128)(2,1)} %all-gather.3.cloned.1.call-done, bf16[4096,80]{0,1:T(8,128)(2,1)S(1)} %copy-done.1), kind=kOutput, calls=%fused_computation.40 | convolution fusion | flops 335544320 | bytes 5013504 | tf_op jit(solution)/shard_map/dot_general | solution.py:43
  166.5 0.0 copy-start.2
  166.6 22.2 %all-reduce.1 = bf16[512,80]{0,1:T(8,128)(2,1)S(1)} all-reduce(f32[512,80]{0,1:T(8,128)S(1)} %fusion.22), channel_id=1, replica_groups=mesh['head'=8,'expert'=64] {'head'}, use_global_device_ids=true, to_apply=%region_2.3 | all-reduce | flops 40960 | bytes 245760 | tf_op jit(solution)/shard_map/psum | solution.py:48
  188.8 0.7 copy.18
  189.5 8.9 %all-to-all-start = ((bf16[64,8,80]{2,1,0:T(8,128)(2,1)}), bf16[64,8,80]{2,1,0:T(8,128)(2,1)S(1)}, u32[]{:S(2)}, u32[]{:S(2)}) async-start(bf16[64,8,80]{2,1,0:T(8,128)(2,1)} %bitcast), calls=%async_computation | async-start | bytes 262144 | tf_op jit(solution)/shard_map/all_to_all | solution.py:49
  198.4 0.0 all-gather.5.cloned.1.call-start
  198.5 0.1 copy.20
  198.6 0.8 dynamic-slice
  199.3 0.1 convert_reduce_fusion
  199.4 17.6 %all-to-all-done = bf16[64,8,80]{2,1,0:T(8,128)(2,1)S(1)} async-done(((bf16[64,8,80]{2,1,0:T(8,128)(2,1)}), bf16[64,8,80]{2,1,0:T(8,128)(2,1)S(1)}, u32[]{:S(2)}, u32[]{:S(2)}) %all-to-all-start) | async-done | bytes 81952 | tf_op jit(solution)/shard_map/all_to_all | solution.py:49
  217.0 0.1 copy.19
  217.0 0.2 reshape.47
  217.2 0.0 copy-done.2
  217.2 0.2 multiply_reduce_fusion
  217.4 0.3 convolution_convert_fusion.1
  217.7 0.1 reshape.43
  217.8 22.6 %all_to_all.23 = bf16[64,2,640]{2,1,0:T(2,128)(2,1)S(1)} all-to-all(bf16[64,2,640]{2,1,0:T(2,128)(2,1)S(1)} %reshape.43), channel_id=1, replica_groups=mesh['head'=8,'expert'=64] {'expert'}, dimensions={0} | all-to-all | bytes 327680 | tf_op jit(solution)/shard_map/all_to_all | solution.py:76
  240.4 0.7 reshape.44
  241.1 0.0 all-gather.5.cloned.1.call-update
  241.2 0.0 reduce-scatter.4.cloned.1.call-start
  241.2 20.0 %all-gather.5.cloned.1.call-done = bf16[128,5120]{1,0:T(8,128)(2,1)} async-done(((bf16[128,640]{1,0:T(8,128)(2,1)}), bf16[128,5120]{1,0:T(8,128)(2,1)}) %all-gather.5.cloned.1.call-update) | async-done | bytes 1310736 | tf_op jit(solution)/shard_map/all_gather | solution.py:78
  261.2 0.0 copy-done
  261.2 2.0 fusion.1
  263.2 1.7 convolution_convert_fusion
  265.0 0.0 copy-start.4
  265.0 1.5 copy.22
  266.4 0.0 reduce-scatter.4.cloned.1.call-update
  266.5 38.2 %reduce-scatter.4.cloned.1.call-done = bf16[640,128]{1,0:T(8,128)(2,1)} async-done(((bf16[5120,128]{1,0:T(8,128)(2,1)}), bf16[640,128]{1,0:T(8,128)(2,1)}) %reduce-scatter.4.cloned.1.call-update) | async-done | bytes 163856
  304.7 1.1 copy.23
  305.8 0.7 reshape.45
  306.5 15.6 %all-to-all-start.2 = ((bf16[64,2,640]{2,1,0:T(2,128)(2,1)}), bf16[64,2,640]{2,1,0:T(2,128)(2,1)S(1)}, u32[]{:S(2)}, u32[]{:S(2)}) async-start(bf16[64,2,640]{2,1,0:T(2,128)(2,1)} %reshape.45), calls=%async_computation.2 | async-start | bytes 327680 | tf_op jit(solution)/shard_map/all_to_all | solution.py:86
  322.2 0.0 copy-done.4
  322.2 0.1 copy.21
  322.2 0.1 select_reduce_fusion
  322.3 19.0 %all-to-all-done.2 = bf16[64,2,640]{2,1,0:T(2,128)(2,1)S(1)} async-done(((bf16[64,2,640]{2,1,0:T(2,128)(2,1)}), bf16[64,2,640]{2,1,0:T(2,128)(2,1)S(1)}, u32[]{:S(2)}, u32[]{:S(2)}) %all-to-all-start.2) | async-done | bytes 163872 | tf_op jit(solution)/shard_map/all_to_all | solution.py:86
  341.3 0.1 reshape.46
  341.4 0.8 convolution_add_fusion.1
  (3 shorter events, 0.0 us)
Async XLA Ops:
  6.5 254.7 %copy-start = (bf16[1,2,96,5120]{3,2,1,0:T(8,128)(2,1)S(1)}, bf16[1,2,96,5120]{3,2,1,0:T(8,128)(2,1)}, u32[]{:S(2)}) copy-start(bf16[1,2,96,5120]{3,2,1,0:T(8,128)(2,1)} %param.22) | copy-start | bytes 5898244
  6.5 5.3 %copy-start.3 = (s32[8,6]{1,0:T(8,128)S(1)}, s32[8,6]{1,0:T(8,128)}, u32[]{:S(2)}) copy-start(s32[8,6]{1,0:T(8,128)} %param.20) | copy-start | bytes 580
  6.5 156.4 %copy-start.1 = (bf16[4096,80]{0,1:T(8,128)(2,1)S(1)}, bf16[4096,80]{0,1:T(8,128)(2,1)}, u32[]{:S(2)}) copy-start(bf16[4096,80]{0,1:T(8,128)(2,1)} %param.17) | copy-start | bytes 1966084
  6.5 156.4 %all-gather.3.cloned.1.call-start = ((), (), s32[]{:S(2)}) async-start(), calls=%async_computation.4 | async-start | bytes 4259840 | tf_op jit(solution)/shard_map/all_gather | solution.py:44
  166.5 50.7 %copy-start.2 = (bf16[8,5120]{1,0:T(8,128)(2,1)S(1)}, bf16[8,5120]{1,0:T(8,128)(2,1)}, u32[]{:S(2)}) copy-start(bf16[8,5120]{1,0:T(8,128)(2,1)} %param.18) | copy-start | bytes 245764
  189.5 27.5 %all-to-all-start = ((bf16[64,8,80]{2,1,0:T(8,128)(2,1)}), bf16[64,8,80]{2,1,0:T(8,128)(2,1)S(1)}, u32[]{:S(2)}, u32[]{:S(2)}) async-start(bf16[64,8,80]{2,1,0:T(8,128)(2,1)} %bitcast), calls=%async_computation | async-start | bytes 262144 | tf_op jit(solution)/shard_map/all_to_all | solution.py:49
  198.4 62.8 %all-gather.5.cloned.1.call-start = ((), (), s32[]{:S(2)}) async-start(), calls=%async_computation.5 | async-start | bytes 1474560 | tf_op jit(solution)/shard_map/all_gather | solution.py:78
  241.2 63.6 %reduce-scatter.4.cloned.1.call-start = ((), (), s32[]{:S(2)}) async-start(), calls=%async_computation.6 | async-start | bytes 1474560
  265.0 57.2 %copy-start.4 = (f32[8,6]{1,0:T(8,128)S(1)}, f32[8,6]{1,0:T(8,128)}, u32[]{:S(2)}) copy-start(f32[8,6]{1,0:T(8,128)} %param.21) | copy-start | bytes 580
  306.5 34.8 %all-to-all-start.2 = ((bf16[64,2,640]{2,1,0:T(2,128)(2,1)}), bf16[64,2,640]{2,1,0:T(2,128)(2,1)S(1)}, u32[]{:S(2)}, u32[]{:S(2)}) async-start(bf16[64,2,640]{2,1,0:T(2,128)(2,1)} %reshape.45), calls=%async_computation.2 | async-start | bytes 327680 | tf_op jit(solution)/shard_map/all_to_all | solution.py:86
Sparse Core Ops, SparseCore 0:
  11.9 151.0 all-gather.2
  241.3 19.9 all-gather.4
  266.6 38.0 reduce-scatter.3

commit v2 on v1

--- a/solution.py
+++ b/solution.py
@@ -1,8 +1,10 @@
 import jax
 import jax.numpy as jnp
 from jax import lax
+from jax.sharding import Mesh
 from jax.sharding import PartitionSpec as P
 
+EXPERT = ("ez", "ey")
 softmax_scale = 192.0 ** (-0.5)
 norm_epsilon = 1e-06
 
@@ -40,19 +42,21 @@
     seq_local = q_latent.shape[0]
     latent_out = attend(q_latent, q_rotary, cache_latent, cache_rotary, lengths)
     flattened = latent_out.reshape(seq_local, -1)
+    gathered = lax.all_gather(flattened, "ey", axis=0, tiled=True)
+    gathered = lax.all_gather(gathered, "ez", axis=0, tiled=True)
     column_terms = jnp.dot(
-        lax.all_gather(flattened, "expert", axis=0, tiled=True),
+        gathered,
         w_value_out,
         preferred_element_type=jnp.float32,
     )
     column_sums = lax.psum(column_terms, "head")
     attention = lax.all_to_all(
-        column_sums.astype(jnp.bfloat16), "expert", split_axis=0, concat_axis=1, tiled=True
+        column_sums.astype(jnp.bfloat16), EXPERT, split_axis=0, concat_axis=1, tiled=True
     )
     stream = resid.astype(jnp.float32) + attention.astype(jnp.float32)
     mean_square = jnp.mean(stream * stream, axis=1, keepdims=True)
     normed = (stream * lax.rsqrt(mean_square + norm_epsilon) * norm_gain).astype(jnp.bfloat16)
-    expert_count = lax.axis_size("expert")
+    expert_count = lax.axis_size("ez") * lax.axis_size("ey")
     top_count = route_ids.shape[1]
     capacity = max(2, -(-(seq_local * top_count) // expert_count))
     flat_ids = route_ids.reshape(-1)
@@ -73,7 +77,7 @@
     normed_cols = lax.dynamic_slice_in_dim(normed, offset, col_width, 1)
     outgoing = jnp.dot(selector, normed_cols, preferred_element_type=jnp.float32).astype(jnp.bfloat16)
     outgoing = outgoing.reshape(expert_count, capacity, -1)
-    arrived = lax.all_to_all(outgoing, "expert", split_axis=0, concat_axis=0, tiled=True)
+    arrived = lax.all_to_all(outgoing, EXPERT, split_axis=0, concat_axis=0, tiled=True)
     arrived_cols = arrived.reshape(-1, arrived.shape[2])
     flat_rows = lax.all_gather(arrived_cols, "head", axis=1, tiled=True)
     projected = jnp.einsum("rd,gfd->rgf", flat_rows, gate_up, preferred_element_type=jnp.float32)
@@ -83,7 +87,7 @@
         partial_rows.astype(jnp.bfloat16), "head", scatter_dimension=1, tiled=True
     )
     summed_rows = summed_cols.reshape(expert_count, capacity, -1)
-    returned = lax.all_to_all(summed_rows, "expert", split_axis=0, concat_axis=0, tiled=True)
+    returned = lax.all_to_all(summed_rows, EXPERT, split_axis=0, concat_axis=0, tiled=True)
     back_rows = returned.reshape(expert_count * capacity, -1).astype(jnp.float32)
     mixture = jnp.dot(blending.T, back_rows, precision=lax.Precision.HIGHEST)
     stream_cols = lax.dynamic_slice_in_dim(stream, offset, col_width, 1)
@@ -92,19 +96,24 @@
 
 def solution(mesh):
     placed = (
-        P("expert", "head", None),
-        P("expert", "head", None),
-        P("expert", None, None),
-        P("expert", None, None),
-        P("expert"),
-        P("head", "expert"),
-        P("expert", None),
+        P(EXPERT, "head", None),
+        P(EXPERT, "head", None),
+        P(EXPERT, None, None),
+        P(EXPERT, None, None),
+        P(EXPERT),
+        P("head", EXPERT),
+        P(EXPERT, None),
         P(),
-        P("expert", None),
-        P("expert", None),
-        P("expert", None, "head", None),
-        P("expert", "head", None),
+        P(EXPERT, None),
+        P(EXPERT, None),
+        P(EXPERT, None, "head", None),
+        P(EXPERT, "head", None),
+    )
+    head_count, expert_total = mesh.devices.shape
+    y_count = len({device.coords[1] for device in mesh.devices[0]})
+    split_mesh = Mesh(
+        mesh.devices.reshape(head_count, expert_total // y_count, y_count), ("head",) + EXPERT
     )
     return jax.shard_map(
-        on_device, mesh=mesh, in_specs=placed, out_specs=P("expert", "head"), check_vma=False
+        on_device, mesh=split_mesh, in_specs=placed, out_specs=P(EXPERT, "head"), check_vma=False
     )

time: 350 us -> 296 us (0.85)
  waiting for transfers between devices: 246 us -> 177 us
  blocking collectives: 44.8 us -> 58.4 us
    all_gather x1, waiting for transfers between devices: 151 us -> 82.3 us  [on_device(): gathered = lax.all_gather(gathered, 'ez', axis=0, tiled=True)]
    all_gather x0 -> x1, blocking collectives: none -> 13.5 us  [on_device(): gathered = lax.all_gather(flattened, 'ey', axis=0, tiled=True)]
  transfers between devices with their start and end apart: 5 -> 5, of which waited for: 5 -> 5; matrix products, arithmetic and copies ran while one was open for 0% -> 1% of each run, Pallas kernels for 0% -> 0%
where the time goes in v2:
time: 296 us; the launch traced here: 295 us
  waiting for transfers between devices  177 us (60%)
  blocking collectives  58.4 us (20%)
  starting transfers between devices  26.4 us (9%)
  between operations  13.3 us (4%)
  matrix products  12.8 us (4%)
  local copies, waits for them, and re-layouts  6.22 us (2%)
    all_gather x1, waiting for transfers between devices, on_device(): gathered = lax.all_gather(gathered, 'ez', axis=0, tiled=True)  82.3 us
    unnamed x4, waiting for transfers between devices  38.3 us
    all_to_all x1, blocking collectives, on_device(): lax.all_to_all(outgoing, EXPERT, split_axis=0, concat_axis=0, tiled=True)  22.7 us
    psum x1, blocking collectives, on_device(): column_sums = lax.psum(column_terms, 'head')  22.2 us
    all_gather x1, waiting for transfers between devices, on_device(): flat_rows = lax.all_gather(arrived_cols, 'head', axis=1, tiled=True)  20 us
    all_to_all x1, waiting for transfers between devices, on_device(): lax.all_to_all(summed_rows, EXPERT, split_axis=0, concat_axis=0, tiled=True)  18.9 us
    all_to_all x1, waiting for transfers between devices, on_device(): lax.all_to_all(column_sums.astype(jnp.bfloat16), EXPERT, split_axis=0, co...  17.6 us
    all_to_all x1, starting transfers between devices, on_device(): lax.all_to_all(summed_rows, EXPERT, split_axis=0, concat_axis=0, tiled=True)  15.6 us
  transfers between devices with their start and end apart: 5, of which 5 were waited for; matrix products, arithmetic and copies ran while one was open for 1% of the time, Pallas kernels for 0%

profile of v2, /device:TPU:6, one launch (start us, length us, event | category | flops | bytes accessed | tf_op | source)
XLA Modules:
  0.0 295.0 jit_solution(180812473195348940)
XLA Ops:
  6.5 0.0 copy-start
  6.5 0.0 copy-start.3
  6.5 0.0 copy-start.1
  6.5 0.0 all-gather.3.cloned.1.call-start
  6.5 1.8 fusion.21
  8.3 1.1 fusion.8
  9.4 0.2 fusion.20
  9.6 1.5 fusion.4
  11.1 13.5 %all_gather.9 = bf16[32,4096]{1,0:T(8,128)(2,1)} all-gather(bf16[8,4096]{1,0:T(8,128)(2,1)S(1)} %bitcast.32), channel_id=1, replica_groups=mesh['head'=8,'ez'=16,'ey'=4] {'ey'}, dimensions={0}, use_global_device_ids=true | all-gather | bytes 327680 | tf_op jit(solution)/shard_map/all_gather | solution.py:45
  24.7 0.0 all-gather.3.cloned.1.call-update
  24.7 0.0 copy-done.3
  24.7 0.1 eq.28
  24.8 0.1 fusion.13
  24.8 0.1 reduce_window_sum.11
  24.9 0.2 select_reduce_fusion.1
  25.1 0.1 reduce_sum.49
  25.2 82.3 %all-gather.3.cloned.1.call-done = bf16[512,4096]{1,0:T(8,128)(2,1)} async-done(((bf16[32,4096]{1,0:T(8,128)(2,1)}), bf16[512,4096]{1,0:T(8,128)(2,1)}) %all-gather.3.cloned.1.call-update) | async-done | bytes 4194320 | tf_op jit(solution)/shard_map/all_gather | solution.py:46
  107.5 0.0 copy-done.1
  107.5 3.6 %fusion.22 = f32[512,80]{0,1:T(8,128)S(1)} fusion(bf16[512,4096]{1,0:T(8,128)(2,1)} %all-gather.3.cloned.1.call-done, bf16[4096,80]{0,1:T(8,128)(2,1)S(1)} %copy-done.1), kind=kOutput, calls=%fused_computation.40 | convolution fusion | flops 335544320 | bytes 5013504 | tf_op jit(solution)/shard_map/dot_general | solution.py:47
  111.1 0.0 copy-start.2
  111.1 22.2 %all-reduce.1 = bf16[512,80]{0,1:T(8,128)(2,1)S(1)} all-reduce(f32[512,80]{0,1:T(8,128)S(1)} %fusion.22), channel_id=1, replica_groups=mesh['head'=8,'ez'=16,'ey'=4] {'head'}, use_global_device_ids=true, to_apply=%region_2.3 | all-reduce | flops 40960 | bytes 245760 | tf_op jit(solution)/shard_map/psum | solution.py:52
  133.3 0.7 copy.18
  134.0 10.8 %all-to-all-start = ((bf16[64,8,80]{2,1,0:T(8,128)(2,1)}), bf16[64,8,80]{2,1,0:T(8,128)(2,1)S(1)}, u32[]{:S(2)}, u32[]{:S(2)}) async-start(bf16[64,8,80]{2,1,0:T(8,128)(2,1)} %bitcast), calls=%async_computation | async-start | bytes 262144 | tf_op jit(solution)/shard_map/all_to_all | solution.py:53
  144.8 0.0 all-gather.5.cloned.1.call-start
  144.9 0.1 copy.20
  145.0 0.8 dynamic-slice
  145.8 0.1 convert_reduce_fusion
  145.8 17.6 %all-to-all-done = bf16[64,8,80]{2,1,0:T(8,128)(2,1)S(1)} async-done(((bf16[64,8,80]{2,1,0:T(8,128)(2,1)}), bf16[64,8,80]{2,1,0:T(8,128)(2,1)S(1)}, u32[]{:S(2)}, u32[]{:S(2)}) %all-to-all-start) | async-done | bytes 81952 | tf_op jit(solution)/shard_map/all_to_all | solution.py:53
  163.4 0.1 copy.19
  163.5 0.2 reshape.47
  163.6 0.0 copy-done.2
  163.7 0.2 multiply_reduce_fusion
  163.8 0.3 convolution_convert_fusion.1
  164.1 0.1 reshape.43
  164.2 22.7 %all_to_all.23 = bf16[64,2,640]{2,1,0:T(2,128)(2,1)S(1)} all-to-all(bf16[64,2,640]{2,1,0:T(2,128)(2,1)S(1)} %reshape.43), channel_id=1, replica_groups=mesh['head'=8,'ez'=16,'ey'=4] {'ez','ey'}, dimensions={0} | all-to-all | bytes 327680 | tf_op jit(solution)/shard_map/all_to_all | solution.py:80
  186.9 0.7 reshape.44
  187.6 0.0 all-gather.5.cloned.1.call-update
  187.6 0.0 reduce-scatter.4.cloned.1.call-start
  187.7 20.0 %all-gather.5.cloned.1.call-done = bf16[128,5120]{1,0:T(8,128)(2,1)} async-done(((bf16[128,640]{1,0:T(8,128)(2,1)}), bf16[128,5120]{1,0:T(8,128)(2,1)}) %all-gather.5.cloned.1.call-update) | async-done | bytes 1310736 | tf_op jit(solution)/shard_map/all_gather | solution.py:82
  207.7 0.0 copy-done
  207.7 2.0 fusion.1
  209.6 1.8 convolution_convert_fusion
  211.4 0.0 copy-start.4
  211.4 1.5 copy.22
  212.9 0.0 reduce-scatter.4.cloned.1.call-update
  212.9 38.2 %reduce-scatter.4.cloned.1.call-done = bf16[640,128]{1,0:T(8,128)(2,1)} async-done(((bf16[5120,128]{1,0:T(8,128)(2,1)}), bf16[640,128]{1,0:T(8,128)(2,1)}) %reduce-scatter.4.cloned.1.call-update) | async-done | bytes 163856
  251.1 1.1 copy.23
  252.2 0.7 reshape.45
  252.9 15.6 %all-to-all-start.2 = ((bf16[64,2,640]{2,1,0:T(2,128)(2,1)}), bf16[64,2,640]{2,1,0:T(2,128)(2,1)S(1)}, u32[]{:S(2)}, u32[]{:S(2)}) async-start(bf16[64,2,640]{2,1,0:T(2,128)(2,1)} %reshape.45), calls=%async_computation.2 | async-start | bytes 327680 | tf_op jit(solution)/shard_map/all_to_all | solution.py:90
  268.5 0.0 copy-done.4
  268.5 0.1 copy.21
  268.6 0.1 select_reduce_fusion
  268.7 18.9 %all-to-all-done.2 = bf16[64,2,640]{2,1,0:T(2,128)(2,1)S(1)} async-done(((bf16[64,2,640]{2,1,0:T(2,128)(2,1)}), bf16[64,2,640]{2,1,0:T(2,128)(2,1)S(1)}, u32[]{:S(2)}, u32[]{:S(2)}) %all-to-all-start.2) | async-done | bytes 163872 | tf_op jit(solution)/shard_map/all_to_all | solution.py:90
  287.6 0.1 reshape.46
  287.7 0.8 convolution_add_fusion.1
  (4 shorter events, 0.1 us)
Async XLA Ops:
  6.5 201.1 %copy-start = (bf16[1,2,96,5120]{3,2,1,0:T(8,128)(2,1)S(1)}, bf16[1,2,96,5120]{3,2,1,0:T(8,128)(2,1)}, u32[]{:S(2)}) copy-start(bf16[1,2,96,5120]{3,2,1,0:T(8,128)(2,1)} %param.22) | copy-start | bytes 5898244
  6.5 18.1 %copy-start.3 = (s32[8,6]{1,0:T(8,128)S(1)}, s32[8,6]{1,0:T(8,128)}, u32[]{:S(2)}) copy-start(s32[8,6]{1,0:T(8,128)} %param.20) | copy-start | bytes 580
  6.5 101.0 %copy-start.1 = (bf16[4096,80]{0,1:T(8,128)(2,1)S(1)}, bf16[4096,80]{0,1:T(8,128)(2,1)}, u32[]{:S(2)}) copy-start(bf16[4096,80]{0,1:T(8,128)(2,1)} %param.17) | copy-start | bytes 1966084
  6.5 101.0 %all-gather.3.cloned.1.call-start = ((), (), s32[]{:S(2)}) async-start(), calls=%async_computation.4 | async-start | bytes 4456448 | tf_op jit(solution)/shard_map/all_gather | solution.py:46
  111.1 52.6 %copy-start.2 = (bf16[8,5120]{1,0:T(8,128)(2,1)S(1)}, bf16[8,5120]{1,0:T(8,128)(2,1)}, u32[]{:S(2)}) copy-start(bf16[8,5120]{1,0:T(8,128)(2,1)} %param.18) | copy-start | bytes 245764
  134.0 29.3 %all-to-all-start = ((bf16[64,8,80]{2,1,0:T(8,128)(2,1)}), bf16[64,8,80]{2,1,0:T(8,128)(2,1)S(1)}, u32[]{:S(2)}, u32[]{:S(2)}) async-start(bf16[64,8,80]{2,1,0:T(8,128)(2,1)} %bitcast), calls=%async_computation | async-start | bytes 262144 | tf_op jit(solution)/shard_map/all_to_all | solution.py:53
  144.8 62.8 %all-gather.5.cloned.1.call-start = ((), (), s32[]{:S(2)}) async-start(), calls=%async_computation.5 | async-start | bytes 1474560 | tf_op jit(solution)/shard_map/all_gather | solution.py:82
  187.6 63.5 %reduce-scatter.4.cloned.1.call-start = ((), (), s32[]{:S(2)}) async-start(), calls=%async_computation.6 | async-start | bytes 1474560
  211.4 57.1 %copy-start.4 = (f32[8,6]{1,0:T(8,128)S(1)}, f32[8,6]{1,0:T(8,128)}, u32[]{:S(2)}) copy-start(f32[8,6]{1,0:T(8,128)} %param.21) | copy-start | bytes 580
  252.9 34.7 %all-to-all-start.2 = ((bf16[64,2,640]{2,1,0:T(2,128)(2,1)}), bf16[64,2,640]{2,1,0:T(2,128)(2,1)S(1)}, u32[]{:S(2)}, u32[]{:S(2)}) async-start(bf16[64,2,640]{2,1,0:T(2,128)(2,1)} %reshape.45), calls=%async_computation.2 | async-start | bytes 327680 | tf_op jit(solution)/shard_map/all_to_all | solution.py:90
Sparse Core Ops, SparseCore 0:
  24.8 82.6 all-gather.2
  187.7 19.8 all-gather.4
  213.0 38.0 reduce-scatter.3

commit v3 on v2

--- a/solution.py
+++ b/solution.py
@@ -42,16 +42,12 @@
     seq_local = q_latent.shape[0]
     latent_out = attend(q_latent, q_rotary, cache_latent, cache_rotary, lengths)
     flattened = latent_out.reshape(seq_local, -1)
-    gathered = lax.all_gather(flattened, "ey", axis=0, tiled=True)
-    gathered = lax.all_gather(gathered, "ez", axis=0, tiled=True)
-    column_terms = jnp.dot(
-        gathered,
-        w_value_out,
-        preferred_element_type=jnp.float32,
-    )
+    gathered = lax.all_gather(flattened, "ez", axis=0, tiled=True)
+    value_cols = lax.all_gather(w_value_out, "ey", axis=1, tiled=True)
+    column_terms = jnp.dot(gathered, value_cols, preferred_element_type=jnp.float32)
     column_sums = lax.psum(column_terms, "head")
     attention = lax.all_to_all(
-        column_sums.astype(jnp.bfloat16), EXPERT, split_axis=0, concat_axis=1, tiled=True
+        column_sums.astype(jnp.bfloat16), "ez", split_axis=0, concat_axis=1, tiled=True
     )
     stream = resid.astype(jnp.float32) + attention.astype(jnp.float32)
     mean_square = jnp.mean(stream * stream, axis=1, keepdims=True)

time: 296 us -> 319 us (1.078)
  waiting for transfers between devices: 177 us -> 207 us
  blocking collectives: 58.4 us -> 49.9 us
    all_gather x1 -> x2, waiting for transfers between devices: 82.3 us -> 116 us  [the longest x1 74.3 us: on_device(): gathered = lax.all_gather(flattened, 'ez', axis=0, tiled=True)]
    all_gather x1 -> x0, blocking collectives: 13.5 us -> none  [on_device(): gathered = lax.all_gather(flattened, 'ey', axis=0, tiled=True)]
    all_to_all x1, waiting for transfers between devices: 17.6 us -> 12.5 us  [on_device(): lax.all_to_all(column_sums.astype(jnp.bfloat16), 'ez', split_axis=0, conc...]
    unnamed x4 -> x5, waiting for transfers between devices: 38.3 us -> 39 us
  transfers between devices with their start and end apart: 5 -> 6, of which waited for: 5 -> 6; matrix products, arithmetic and copies ran while one was open for 1% -> 0% of each run, Pallas kernels for 0% -> 0%
where the time goes in v3:
time: 319 us; the launch traced here: 318 us
  waiting for transfers between devices  207 us (65%)
  blocking collectives  49.9 us (16%)
  starting transfers between devices  28.1 us (9%)
  between operations  13.3 us (4%)
  matrix products  12.1 us (4%)
  local copies, waits for them, and re-layouts  6.75 us (2%)
    all_gather x1, waiting for transfers between devices, on_device(): gathered = lax.all_gather(flattened, 'ez', axis=0, tiled=True)  74.3 us
    all_gather x1, waiting for transfers between devices, on_device(): value_cols = lax.all_gather(w_value_out, 'ey', axis=1, tiled=True)  41.9 us
    unnamed x5, waiting for transfers between devices  39 us
    all_to_all x1, blocking collectives, on_device(): lax.all_to_all(outgoing, EXPERT, split_axis=0, concat_axis=0, tiled=True)  25.7 us
    psum x1, blocking collectives, on_device(): column_sums = lax.psum(column_terms, 'head')  24.2 us
    all_gather x1, waiting for transfers between devices, on_device(): flat_rows = lax.all_gather(arrived_cols, 'head', axis=1, tiled=True)  20 us
    all_to_all x1, waiting for transfers between devices, on_device(): lax.all_to_all(summed_rows, EXPERT, split_axis=0, concat_axis=0, tiled=True)  19.1 us
    all_to_all x1, starting transfers between devices, on_device(): lax.all_to_all(summed_rows, EXPERT, split_axis=0, concat_axis=0, tiled=True)  15.7 us
  transfers between devices with their start and end apart: 6, of which 6 were waited for; matrix products, arithmetic and copies ran while one was open for 0% of the time, Pallas kernels for 0%

profile of v3, /device:TPU:6, one launch (start us, length us, event | category | flops | bytes accessed | tf_op | source)
XLA Modules:
  0.0 317.7 jit_solution(12334773724931351285)
XLA Ops:
  6.5 0.0 copy-start
  6.5 0.0 copy-start.2
  6.5 0.0 all-gather.4.cloned.1.call-start
  6.5 1.8 fusion.21
  8.3 1.1 fusion.8
  9.4 0.2 fusion.20
  9.6 1.5 fusion.4
  11.1 0.7 copy.24
  11.7 0.0 all-gather.4.cloned.1.call-update
  11.8 0.0 all-gather.6.cloned.1.call-start
  11.8 0.7 all-gather.6.cloned.1.call-update
  12.5 0.0 copy-done.2
  12.5 0.1 eq.28
  12.6 0.1 fusion.13
  12.7 0.1 reduce_window_sum.11
  12.8 0.2 select_reduce_fusion.1
  13.0 0.1 reduce_sum.49
  13.0 0.0 copy-start.1
  13.0 74.3 %all-gather.4.cloned.1.call-done = bf16[128,4096]{1,0:T(8,128)(2,1)} async-done(((bf16[8,4096]{1,0:T(8,128)(2,1)}), bf16[128,4096]{1,0:T(8,128)(2,1)}) %all-gather.4.cloned.1.call-update) | async-done | bytes 1048592 | tf_op jit(solution)/shard_map/all_gather | solution.py:45
  87.4 41.9 %all-gather.6.cloned.1.call-done = bf16[4096,320]{0,1:T(8,128)(2,1)} async-done(((bf16[4096,80]{0,1:T(8,128)(2,1)}), bf16[4096,320]{0,1:T(8,128)(2,1)}) %all-gather.6.cloned.1.call-update) | async-done | bytes 2621456 | tf_op jit(solution)/shard_map/all_gather | solution.py:46
  129.3 2.9 fusion.22
  132.2 24.2 %all-reduce.1 = bf16[128,320]{0,1:T(8,128)(2,1)S(1)} all-reduce(f32[128,320]{0,1:T(8,128)S(1)} %fusion.22), channel_id=1, replica_groups=mesh['head'=8,'ez'=16,'ey'=4] {'head'}, use_global_device_ids=true, to_apply=%region_2.3 | all-reduce | flops 40960 | bytes 245760 | tf_op jit(solution)/shard_map/psum | solution.py:48
  156.4 0.7 copy.18
  157.1 12.3 %all-to-all-start = ((bf16[16,8,320]{2,1,0:T(8,128)(2,1)}), bf16[16,8,320]{2,1,0:T(8,128)(2,1)S(1)}, u32[]{:S(2)}, u32[]{:S(2)}) async-start(bf16[16,8,320]{2,1,0:T(8,128)(2,1)} %bitcast), calls=%async_computation | async-start | bytes 196608 | tf_op jit(solution)/shard_map/all_to_all | solution.py:49
  169.4 0.0 all-gather.8.cloned.1.call-start
  169.5 0.1 copy.20
  169.6 0.8 dynamic-slice
  170.3 0.1 convert_reduce_fusion
  170.4 12.5 %all-to-all-done = bf16[16,8,320]{2,1,0:T(8,128)(2,1)S(1)} async-done(((bf16[16,8,320]{2,1,0:T(8,128)(2,1)}), bf16[16,8,320]{2,1,0:T(8,128)(2,1)S(1)}, u32[]{:S(2)}, u32[]{:S(2)}) %all-to-all-start) | async-done | bytes 81952 | tf_op jit(solution)/shard_map/all_to_all | solution.py:49
  183.0 0.1 reshape.47
  183.1 0.0 copy-done.1
  183.1 0.2 multiply_reduce_fusion
  183.3 0.3 convolution_convert_fusion.1
  183.6 0.1 reshape.43
  183.6 25.7 %all_to_all.23 = bf16[64,2,640]{2,1,0:T(2,128)(2,1)S(1)} all-to-all(bf16[64,2,640]{2,1,0:T(2,128)(2,1)S(1)} %reshape.43), channel_id=1, replica_groups=mesh['head'=8,'ez'=16,'ey'=4] {'ez','ey'}, dimensions={0} | all-to-all | bytes 327680 | tf_op jit(solution)/shard_map/all_to_all | solution.py:76
  209.3 0.7 reshape.44
  210.0 0.0 all-gather.8.cloned.1.call-update
  210.1 0.0 reduce-scatter.4.cloned.1.call-start
  210.1 20.0 %all-gather.8.cloned.1.call-done = bf16[128,5120]{1,0:T(8,128)(2,1)} async-done(((bf16[128,640]{1,0:T(8,128)(2,1)}), bf16[128,5120]{1,0:T(8,128)(2,1)}) %all-gather.8.cloned.1.call-update) | async-done | bytes 1310736 | tf_op jit(solution)/shard_map/all_gather | solution.py:78
  230.1 0.0 copy-done
  230.1 2.0 fusion.1
  232.1 1.7 convolution_convert_fusion
  233.8 0.0 copy-start.3
  233.9 1.5 copy.22
  235.3 0.0 reduce-scatter.4.cloned.1.call-update
  235.3 38.2 %reduce-scatter.4.cloned.1.call-done = bf16[640,128]{1,0:T(8,128)(2,1)} async-done(((bf16[5120,128]{1,0:T(8,128)(2,1)}), bf16[640,128]{1,0:T(8,128)(2,1)}) %reduce-scatter.4.cloned.1.call-update) | async-done | bytes 163856
  273.6 1.1 copy.23
  274.7 0.7 reshape.45
  275.4 15.7 %all-to-all-start.2 = ((bf16[64,2,640]{2,1,0:T(2,128)(2,1)}), bf16[64,2,640]{2,1,0:T(2,128)(2,1)S(1)}, u32[]{:S(2)}, u32[]{:S(2)}) async-start(bf16[64,2,640]{2,1,0:T(2,128)(2,1)} %reshape.45), calls=%async_computation.2 | async-start | bytes 327680 | tf_op jit(solution)/shard_map/all_to_all | solution.py:86
  291.1 0.0 copy-done.3
  291.1 0.1 copy.21
  291.1 0.1 select_reduce_fusion
  291.2 19.1 %all-to-all-done.2 = bf16[64,2,640]{2,1,0:T(2,128)(2,1)S(1)} async-done(((bf16[64,2,640]{2,1,0:T(2,128)(2,1)}), bf16[64,2,640]{2,1,0:T(2,128)(2,1)S(1)}, u32[]{:S(2)}, u32[]{:S(2)}) %all-to-all-start.2) | async-done | bytes 163872 | tf_op jit(solution)/shard_map/all_to_all | solution.py:86
  310.3 0.1 reshape.46
  310.4 0.8 convolution_add_fusion.1
  (4 shorter events, 0.1 us)
Async XLA Ops:
  6.5 223.6 %copy-start = (bf16[1,2,96,5120]{3,2,1,0:T(8,128)(2,1)S(1)}, bf16[1,2,96,5120]{3,2,1,0:T(8,128)(2,1)}, u32[]{:S(2)}) copy-start(bf16[1,2,96,5120]{3,2,1,0:T(8,128)(2,1)} %param.22) | copy-start | bytes 5898244
  6.5 6.0 %copy-start.2 = (s32[8,6]{1,0:T(8,128)S(1)}, s32[8,6]{1,0:T(8,128)}, u32[]{:S(2)}) copy-start(s32[8,6]{1,0:T(8,128)} %param.20) | copy-start | bytes 580
  6.5 80.8 %all-gather.4.cloned.1.call-start = ((), (), s32[]{:S(2)}) async-start(), calls=%async_computation.4 | async-start | bytes 1114112 | tf_op jit(solution)/shard_map/all_gather | solution.py:45
  11.8 117.5 %all-gather.6.cloned.1.call-start = ((), (), s32[]{:S(2)}) async-start(), calls=%async_computation.5 | async-start | bytes 3276800 | tf_op jit(solution)/shard_map/all_gather | solution.py:46
  13.0 170.0 %copy-start.1 = (bf16[8,5120]{1,0:T(8,128)(2,1)S(1)}, bf16[8,5120]{1,0:T(8,128)(2,1)}, u32[]{:S(2)}) copy-start(bf16[8,5120]{1,0:T(8,128)(2,1)} %param.18) | copy-start | bytes 245764
  157.1 25.8 %all-to-all-start = ((bf16[16,8,320]{2,1,0:T(8,128)(2,1)}), bf16[16,8,320]{2,1,0:T(8,128)(2,1)S(1)}, u32[]{:S(2)}, u32[]{:S(2)}) async-start(bf16[16,8,320]{2,1,0:T(8,128)(2,1)} %bitcast), calls=%async_computation | async-start | bytes 196608 | tf_op jit(solution)/shard_map/all_to_all | solution.py:49
  169.4 60.7 %all-gather.8.cloned.1.call-start = ((), (), s32[]{:S(2)}) async-start(), calls=%async_computation.6 | async-start | bytes 1474560 | tf_op jit(solution)/shard_map/all_gather | solution.py:78
  210.1 63.5 %reduce-scatter.4.cloned.1.call-start = ((), (), s32[]{:S(2)}) async-start(), calls=%async_computation.7 | async-start | bytes 1474560
  233.8 57.2 %copy-start.3 = (f32[8,6]{1,0:T(8,128)S(1)}, f32[8,6]{1,0:T(8,128)}, u32[]{:S(2)}) copy-start(f32[8,6]{1,0:T(8,128)} %param.21) | copy-start | bytes 580
  275.4 34.9 %all-to-all-start.2 = ((bf16[64,2,640]{2,1,0:T(2,128)(2,1)}), bf16[64,2,640]{2,1,0:T(2,128)(2,1)S(1)}, u32[]{:S(2)}, u32[]{:S(2)}) async-start(bf16[64,2,640]{2,1,0:T(2,128)(2,1)} %reshape.45), calls=%async_computation.2 | async-start | bytes 327680 | tf_op jit(solution)/shard_map/all_to_all | solution.py:86
Sparse Core Ops, SparseCore 0:
  11.9 75.4 all-gather.3
  89.4 39.7 all-gather.5
  210.2 19.8 all-gather.7
  235.5 38.0 reduce-scatter.3

commit v4 on v2

--- a/solution.py
+++ b/solution.py
@@ -44,6 +44,11 @@
     flattened = latent_out.reshape(seq_local, -1)
     gathered = lax.all_gather(flattened, "ey", axis=0, tiled=True)
     gathered = lax.all_gather(gathered, "ez", axis=0, tiled=True)
+    head_count = lax.axis_size("head")
+    down_blocks = w_down[0].reshape(w_down.shape[1], head_count, -1)
+    down_cols = lax.all_to_all(down_blocks, "head", split_axis=1, concat_axis=0, tiled=True)
+    down_cols = down_cols.reshape(-1, down_blocks.shape[2])
+    gathered, down_cols = lax.optimization_barrier((gathered, down_cols))
     column_terms = jnp.dot(
         gathered,
         w_value_out,
@@ -71,7 +76,6 @@
     selector = jnp.sum(matches.astype(jnp.int32), axis=2).astype(jnp.bfloat16)
     blending = jnp.sum(jnp.where(matches, route_weights[None, :, :], 0.0), axis=2)
     gate_up = w_gate_up[0]
-    down_local = w_down[0]
     col_width = stream.shape[1] // lax.axis_size("head")
     offset = lax.axis_index("head") * col_width
     normed_cols = lax.dynamic_slice_in_dim(normed, offset, col_width, 1)
@@ -82,10 +86,8 @@
     flat_rows = lax.all_gather(arrived_cols, "head", axis=1, tiled=True)
     projected = jnp.einsum("rd,gfd->rgf", flat_rows, gate_up, preferred_element_type=jnp.float32)
     hidden = (jax.nn.silu(projected[:, 0]) * projected[:, 1]).astype(jnp.bfloat16)
-    partial_rows = jnp.dot(hidden, down_local, preferred_element_type=jnp.float32)
-    summed_cols = lax.psum_scatter(
-        partial_rows.astype(jnp.bfloat16), "head", scatter_dimension=1, tiled=True
-    )
+    hidden_all = lax.all_gather(hidden, "head", axis=1, tiled=True)
+    summed_cols = jnp.dot(hidden_all, down_cols, preferred_element_type=jnp.float32).astype(jnp.bfloat16)
     summed_rows = summed_cols.reshape(expert_count, capacity, -1)
     returned = lax.all_to_all(summed_rows, EXPERT, split_axis=0, concat_axis=0, tiled=True)
     back_rows = returned.reshape(expert_count * capacity, -1).astype(jnp.float32)

time: 296 us -> 268 us (0.905)
  waiting for transfers between devices: 177 us -> 128 us
  blocking collectives: 58.4 us -> 70.9 us
  starting transfers between devices: 26.4 us -> 35.2 us
    unnamed x4 -> x2, waiting for transfers between devices: 38.3 us -> 0.03 us
    all_gather x1, waiting for transfers between devices: 82.3 us -> 58.4 us  [on_device(): gathered = lax.all_gather(gathered, 'ez', axis=0, tiled=True)]
    all_gather x0 -> x1, blocking collectives: none -> 12.8 us  [on_device(): hidden_all = lax.all_gather(hidden, 'head', axis=1, tiled=True)]
    all_to_all x0 -> x1, waiting for transfers between devices: none -> 12.7 us  [on_device(): lax.all_to_all(down_blocks, 'head', split_axis=1, concat_axis=0, tiled=True)]
    all_to_all x0 -> x1, starting transfers between devices: none -> 8.82 us  [on_device(): lax.all_to_all(down_blocks, 'head', split_axis=1, concat_axis=0, tiled=True)]
where the time goes in v4:
time: 268 us; the launch traced here: 267 us
  waiting for transfers between devices  128 us (48%)
  blocking collectives  70.9 us (26%)
  starting transfers between devices  35.2 us (13%)
  between operations  13.5 us (5%)
  matrix products  11.6 us (4%)
  local copies, waits for them, and re-layouts  6.09 us (2%)
    all_gather x1, waiting for transfers between devices, on_device(): gathered = lax.all_gather(gathered, 'ez', axis=0, tiled=True)  58.4 us
    all_to_all x1, blocking collectives, on_device(): lax.all_to_all(outgoing, EXPERT, split_axis=0, concat_axis=0, tiled=True)  22.6 us
    psum x1, blocking collectives, on_device(): column_sums = lax.psum(column_terms, 'head')  22 us
    all_gather x1, waiting for transfers between devices, on_device(): flat_rows = lax.all_gather(arrived_cols, 'head', axis=1, tiled=True)  20.1 us
    all_to_all x1, waiting for transfers between devices, on_device(): lax.all_to_all(summed_rows, EXPERT, split_axis=0, concat_axis=0, tiled=True)  19.3 us
    all_to_all x1, waiting for transfers between devices, on_device(): lax.all_to_all(column_sums.astype(jnp.bfloat16), EXPERT, split_axis=0, co...  17.6 us
    all_to_all x1, starting transfers between devices, on_device(): lax.all_to_all(summed_rows, EXPERT, split_axis=0, concat_axis=0, tiled=True)  15.4 us
    all_gather x1, blocking collectives, on_device(): gathered = lax.all_gather(flattened, 'ey', axis=0, tiled=True)  13.5 us
  transfers between devices with their start and end apart: 5, of which 5 were waited for; matrix products, arithmetic and copies ran while one was open for 1% of the time, Pallas kernels for 0%

profile of v4, /device:TPU:6, one launch (start us, length us, event | category | flops | bytes accessed | tf_op | source)
XLA Modules:
  0.0 267.1 jit_solution(11325874160416129855)
XLA Ops:
  6.5 0.0 copy-start
  6.5 0.0 all-gather.3.cloned.1.call-start
  6.5 1.8 fusion.18
  8.3 1.1 fusion.8
  9.4 0.2 fusion.17
  9.5 1.5 fusion.4
  11.1 13.5 %all_gather.12 = bf16[32,4096]{1,0:T(8,128)(2,1)} all-gather(bf16[8,4096]{1,0:T(8,128)(2,1)S(1)} %bitcast.46), channel_id=1, replica_groups=mesh['head'=8,'ez'=16,'ey'=4] {'ey'}, dimensions={0}, use_global_device_ids=true | all-gather | bytes 327680 | tf_op jit(solution)/shard_map/all_gather | solution.py:45
  24.6 0.0 all-gather.3.cloned.1.call-update
  24.7 1.3 copy.28
  26.0 0.0 copy-start.1
  26.0 1.1 copy.22
  27.1 8.8 %all-to-all-start = ((bf16[96,8,640]{2,0,1:T(8,128)(2,1)}), bf16[96,8,640]{2,0,1:T(8,128)(2,1)S(1)}, u32[]{:S(2)}, u32[]{:S(2)}) async-start(bf16[96,8,640]{2,0,1:T(8,128)(2,1)} %copy.22), calls=%async_computation | async-start | bytes 1966080 | tf_op jit(solution)/shard_map/all_to_all | solution.py:49
  35.9 0.0 copy-done.1
  35.9 0.1 eq.28
  36.0 0.1 fusion.11
  36.1 0.1 reduce_window_sum.11
  36.1 0.2 select_reduce_fusion.1
  36.3 0.1 reduce_sum.49
  36.4 12.7 %all-to-all-done = bf16[96,8,640]{2,0,1:T(8,128)(2,1)S(1)} async-done(((bf16[96,8,640]{2,0,1:T(8,128)(2,1)}), bf16[96,8,640]{2,0,1:T(8,128)(2,1)S(1)}, u32[]{:S(2)}, u32[]{:S(2)}) %all-to-all-start) | async-done | bytes 983072 | tf_op jit(solution)/shard_map/all_to_all | solution.py:49
  49.1 58.4 %all-gather.3.cloned.1.call-done = bf16[512,4096]{1,0:T(8,128)(2,1)} async-done(((bf16[32,4096]{1,0:T(8,128)(2,1)}), bf16[512,4096]{1,0:T(8,128)(2,1)}) %all-gather.3.cloned.1.call-update) | async-done | bytes 4194320 | tf_op jit(solution)/shard_map/all_gather | solution.py:46
  107.5 3.7 %fusion.19 = f32[512,80]{0,1:T(8,128)S(1)} fusion(bf16[512,4096]{1,0:T(8,128)(2,1)} %all-gather.3.cloned.1.call-done, bf16[4096,80]{0,1:T(8,128)(2,1)} %param.17), kind=kOutput, calls=%fused_computation.39 | convolution fusion | flops 335544320 | bytes 5013504 | tf_op jit(solution)/shard_map/dot_general | solution.py:52
  111.2 22.0 %all-reduce.1 = bf16[512,80]{0,1:T(8,128)(2,1)S(1)} all-reduce(f32[512,80]{0,1:T(8,128)S(1)} %fusion.19), channel_id=1, replica_groups=mesh['head'=8,'ez'=16,'ey'=4] {'head'}, use_global_device_ids=true, to_apply=%region_2.3 | all-reduce | flops 40960 | bytes 245760 | tf_op jit(solution)/shard_map/psum | solution.py:57
  133.2 0.7 copy.23
  134.0 10.9 %all-to-all-start.1 = ((bf16[64,8,80]{2,1,0:T(8,128)(2,1)}), bf16[64,8,80]{2,1,0:T(8,128)(2,1)S(1)}, u32[]{:S(2)}, u32[]{:S(2)}) async-start(bf16[64,8,80]{2,1,0:T(8,128)(2,1)} %bitcast.3), calls=%async_computation.1 | async-start | bytes 262144 | tf_op jit(solution)/shard_map/all_to_all | solution.py:58
  144.8 0.0 all-gather.5.cloned.1.call-start
  144.9 0.1 copy.25
  145.0 0.8 dynamic-slice
  145.7 0.1 convert_reduce_fusion
  145.8 17.6 %all-to-all-done.1 = bf16[64,8,80]{2,1,0:T(8,128)(2,1)S(1)} async-done(((bf16[64,8,80]{2,1,0:T(8,128)(2,1)}), bf16[64,8,80]{2,1,0:T(8,128)(2,1)S(1)}, u32[]{:S(2)}, u32[]{:S(2)}) %all-to-all-start.1) | async-done | bytes 81952 | tf_op jit(solution)/shard_map/all_to_all | solution.py:58
  163.4 0.1 copy.24
  163.5 0.2 reshape.51
  163.6 1.0 multiply_reduce_fusion
  164.7 0.3 convolution_convert_fusion.1
  165.0 0.1 reshape.47
  165.1 22.6 %all_to_all.38 = bf16[64,2,640]{2,1,0:T(2,128)(2,1)S(1)} all-to-all(bf16[64,2,640]{2,1,0:T(2,128)(2,1)S(1)} %reshape.47), channel_id=1, replica_groups=mesh['head'=8,'ez'=16,'ey'=4] {'ez','ey'}, dimensions={0} | all-to-all | bytes 327680 | tf_op jit(solution)/shard_map/all_to_all | solution.py:84
  187.7 0.7 reshape.48
  188.4 0.0 all-gather.5.cloned.1.call-update
  188.5 20.1 %all-gather.5.cloned.1.call-done = bf16[128,5120]{1,0:T(8,128)(2,1)} async-done(((bf16[128,640]{1,0:T(8,128)(2,1)}), bf16[128,5120]{1,0:T(8,128)(2,1)}) %all-gather.5.cloned.1.call-update) | async-done | bytes 1310736 | tf_op jit(solution)/shard_map/all_gather | solution.py:86
  208.5 0.0 copy-done
  208.5 2.0 fusion.1
  210.5 0.0 copy-start.2
  210.6 12.8 %all_gather.15 = bf16[128,768]{0,1:T(8,128)(2,1)S(1)} all-gather(bf16[128,96]{0,1:T(8,128)(2,1)S(1)} %fusion.10), channel_id=1, replica_groups=mesh['head'=8,'ez'=16,'ey'=4] {'head'}, dimensions={1}, use_global_device_ids=true | all-gather | bytes 221184 | tf_op jit(solution)/shard_map/all_gather | solution.py:89
  223.4 0.4 convolution_convert_fusion
  223.7 0.7 reshape.49
  224.4 15.4 %all-to-all-start.3 = ((bf16[64,2,640]{2,1,0:T(2,128)(2,1)}), bf16[64,2,640]{2,1,0:T(2,128)(2,1)S(1)}, u32[]{:S(2)}, u32[]{:S(2)}) async-start(bf16[64,2,640]{2,1,0:T(2,128)(2,1)} %reshape.49), calls=%async_computation.3 | async-start | bytes 327680 | tf_op jit(solution)/shard_map/all_to_all | solution.py:92
  239.9 0.0 copy-done.2
  239.9 0.1 copy.26
  240.0 0.1 select_reduce_fusion
  240.1 19.3 %all-to-all-done.3 = bf16[64,2,640]{2,1,0:T(2,128)(2,1)S(1)} async-done(((bf16[64,2,640]{2,1,0:T(2,128)(2,1)}), bf16[64,2,640]{2,1,0:T(2,128)(2,1)S(1)}, u32[]{:S(2)}, u32[]{:S(2)}) %all-to-all-start.3) | async-done | bytes 163872 | tf_op jit(solution)/shard_map/all_to_all | solution.py:92
  259.4 0.1 reshape.50
  259.5 0.8 convolution_add_fusion.1
  (5 shorter events, 0.1 us)
Async XLA Ops:
  6.5 202.0 %copy-start = (bf16[1,2,96,5120]{3,2,1,0:T(8,128)(2,1)S(1)}, bf16[1,2,96,5120]{3,2,1,0:T(8,128)(2,1)}, u32[]{:S(2)}) copy-start(bf16[1,2,96,5120]{3,2,1,0:T(8,128)(2,1)} %param.22) | copy-start | bytes 5898244
  6.5 100.9 %all-gather.3.cloned.1.call-start = ((), (), s32[]{:S(2)}) async-start(), calls=%async_computation.4 | async-start | bytes 4456448 | tf_op jit(solution)/shard_map/all_gather | solution.py:46
  26.0 9.9 %copy-start.1 = (s32[8,6]{1,0:T(8,128)S(1)}, s32[8,6]{1,0:T(8,128)}, u32[]{:S(2)}) copy-start(s32[8,6]{1,0:T(8,128)} %param.20) | copy-start | bytes 580
  27.1 22.0 %all-to-all-start = ((bf16[96,8,640]{2,0,1:T(8,128)(2,1)}), bf16[96,8,640]{2,0,1:T(8,128)(2,1)S(1)}, u32[]{:S(2)}, u32[]{:S(2)}) async-start(bf16[96,8,640]{2,0,1:T(8,128)(2,1)} %copy.22), calls=%async_computation | async-start | bytes 1966080 | tf_op jit(solution)/shard_map/all_to_all | solution.py:49
  134.0 29.4 %all-to-all-start.1 = ((bf16[64,8,80]{2,1,0:T(8,128)(2,1)}), bf16[64,8,80]{2,1,0:T(8,128)(2,1)S(1)}, u32[]{:S(2)}, u32[]{:S(2)}) async-start(bf16[64,8,80]{2,1,0:T(8,128)(2,1)} %bitcast.3), calls=%async_computation.1 | async-start | bytes 262144 | tf_op jit(solution)/shard_map/all_to_all | solution.py:58
  144.8 63.7 %all-gather.5.cloned.1.call-start = ((), (), s32[]{:S(2)}) async-start(), calls=%async_computation.5 | async-start | bytes 1474560 | tf_op jit(solution)/shard_map/all_gather | solution.py:86
  210.5 29.4 %copy-start.2 = (f32[8,6]{1,0:T(8,128)S(1)}, f32[8,6]{1,0:T(8,128)}, u32[]{:S(2)}) copy-start(f32[8,6]{1,0:T(8,128)} %param.21) | copy-start | bytes 580
  224.4 35.0 %all-to-all-start.3 = ((bf16[64,2,640]{2,1,0:T(2,128)(2,1)}), bf16[64,2,640]{2,1,0:T(2,128)(2,1)S(1)}, u32[]{:S(2)}, u32[]{:S(2)}) async-start(bf16[64,2,640]{2,1,0:T(2,128)(2,1)} %reshape.49), calls=%async_computation.3 | async-start | bytes 327680 | tf_op jit(solution)/shard_map/all_to_all | solution.py:92
Sparse Core Ops, SparseCore 0:
  24.8 82.6 all-gather.2
  188.6 19.9 all-gather.4

commit v5 on v4

--- a/solution.py
+++ b/solution.py
@@ -42,21 +42,21 @@
     seq_local = q_latent.shape[0]
     latent_out = attend(q_latent, q_rotary, cache_latent, cache_rotary, lengths)
     flattened = latent_out.reshape(seq_local, -1)
-    gathered = lax.all_gather(flattened, "ey", axis=0, tiled=True)
-    gathered = lax.all_gather(gathered, "ez", axis=0, tiled=True)
+    gathered = lax.all_gather(flattened, "ez", axis=0, tiled=True)
+    y_count = lax.axis_size("ey")
+    value_copies = jnp.broadcast_to(w_value_out[None], (y_count,) + w_value_out.shape)
+    value_blocks = lax.all_to_all(value_copies, "ey", split_axis=0, concat_axis=0, tiled=True)
     head_count = lax.axis_size("head")
     down_blocks = w_down[0].reshape(w_down.shape[1], head_count, -1)
     down_cols = lax.all_to_all(down_blocks, "head", split_axis=1, concat_axis=0, tiled=True)
     down_cols = down_cols.reshape(-1, down_blocks.shape[2])
-    gathered, down_cols = lax.optimization_barrier((gathered, down_cols))
-    column_terms = jnp.dot(
-        gathered,
-        w_value_out,
-        preferred_element_type=jnp.float32,
-    )
+    gathered, value_blocks, down_cols = lax.optimization_barrier((gathered, value_blocks, down_cols))
+    column_terms = jnp.einsum(
+        "sk,jkc->sjc", gathered, value_blocks, preferred_element_type=jnp.float32
+    ).reshape(gathered.shape[0], -1)
     column_sums = lax.psum(column_terms, "head")
     attention = lax.all_to_all(
-        column_sums.astype(jnp.bfloat16), EXPERT, split_axis=0, concat_axis=1, tiled=True
+        column_sums.astype(jnp.bfloat16), "ez", split_axis=0, concat_axis=1, tiled=True
     )
     stream = resid.astype(jnp.float32) + attention.astype(jnp.float32)
     mean_square = jnp.mean(stream * stream, axis=1, keepdims=True)

time: 268 us -> 249 us (0.929)
  waiting for transfers between devices: 128 us -> 115 us
  blocking collectives: 70.9 us -> 62.9 us
  matrix products: 11.6 us -> 8.62 us
  local copies, waits for them, and re-layouts: 6.09 us -> 8.99 us
  starting transfers between devices: 35.2 us -> 38.1 us
    all_gather x1 -> x0, blocking collectives: 13.5 us -> none  [on_device(): gathered = lax.all_gather(flattened, 'ey', axis=0, tiled=True)]
    all_gather x1, waiting for transfers between devices: 58.4 us -> 51.9 us  [on_device(): gathered = lax.all_gather(flattened, 'ez', axis=0, tiled=True)]
    all_to_all x1 -> x2, waiting for transfers between devices: 17.6 us -> 12.4 us  [the longest x1 12.4 us: on_device(): lax.all_to_all(column_sums.astype(jnp.bfloat16), 'ez', split_axis=0, conc...]
    all_to_all x1, blocking collectives: 22.6 us -> 27.2 us  [on_device(): lax.all_to_all(outgoing, EXPERT, split_axis=0, concat_axis=0, tiled=True)]
    dot_general x1 -> x0, matrix products: 3.74 us -> none  [on_device(): jnp.dot(gathered, w_value_out, preferred_element_type=jnp.float32)]
    reshape x0 -> x1, matrix products: none -> 3.15 us  [on_device(): column_terms = jnp.einsum('sk,jkc->sjc', gathered, value_blocks, preferre...]
    broadcast_in_dim x0 -> x1, local copies, waits for them, and re-layouts: none -> 2.92 us  [on_device(): jnp.broadcast_to(w_value_out[None], (y_count,) + w_value_out.shape)]
    all_to_all x1 -> x2, starting transfers between devices: 10.9 us -> 12.5 us  [the longest x1 7.85 us: on_device(): lax.all_to_all(column_sums.astype(jnp.bfloat16), 'ez', split_axis=0, conc...]
  transfers between devices with their start and end apart: 5 -> 6, of which waited for: 5 -> 5; matrix products, arithmetic and copies ran while one was open for 1% -> 2% of each run, Pallas kernels for 0% -> 0%
where the time goes in v5:
time: 249 us; the launch traced here: 248 us
  waiting for transfers between devices  115 us (46%)
  blocking collectives  62.9 us (25%)
  starting transfers between devices  38.1 us (15%)
  between operations  13.6 us (5%)
  local copies, waits for them, and re-layouts  8.99 us (4%)
  matrix products  8.62 us (3%)
    all_gather x1, waiting for transfers between devices, on_device(): gathered = lax.all_gather(flattened, 'ez', axis=0, tiled=True)  51.9 us
    all_to_all x1, blocking collectives, on_device(): lax.all_to_all(outgoing, EXPERT, split_axis=0, concat_axis=0, tiled=True)  27.2 us
    psum x1, blocking collectives, on_device(): column_sums = lax.psum(column_terms, 'head')  22.9 us
    all_gather x1, waiting for transfers between devices, on_device(): flat_rows = lax.all_gather(arrived_cols, 'head', axis=1, tiled=True)  20 us
    all_to_all x1, waiting for transfers between devices, on_device(): lax.all_to_all(summed_rows, EXPERT, split_axis=0, concat_axis=0, tiled=True)  19.3 us
    all_to_all x1, starting transfers between devices, on_device(): lax.all_to_all(summed_rows, EXPERT, split_axis=0, concat_axis=0, tiled=True)  15.4 us
    all_gather x1, blocking collectives, on_device(): hidden_all = lax.all_gather(hidden, 'head', axis=1, tiled=True)  12.8 us
    all_to_all x1, waiting for transfers between devices, on_device(): lax.all_to_all(column_sums.astype(jnp.bfloat16), 'ez', split_axis=0, conc...  12.4 us
  transfers between devices with their start and end apart: 6, of which 5 were waited for; matrix products, arithmetic and copies ran while one was open for 2% of the time, Pallas kernels for 0%

profile of v5, /device:TPU:6, one launch (start us, length us, event | category | flops | bytes accessed | tf_op | source)
XLA Modules:
  0.0 248.3 jit_solution(1763339786226493249)
XLA Ops:
  6.5 0.0 copy-start
  6.5 1.5 copy.28
  8.0 0.0 copy-start.1
  8.0 0.0 copy-start.4
  8.1 1.1 copy.22
  9.1 0.0 copy-start.2
  9.1 0.0 copy-start.6
  9.1 0.0 copy-start.8
  9.1 10.1 %all-to-all-start.1 = ((bf16[96,8,640]{2,0,1:T(8,128)(2,1)}), bf16[96,8,640]{2,0,1:T(8,128)(2,1)}, u32[]{:S(2)}, u32[]{:S(2)}) async-start(bf16[96,8,640]{2,0,1:T(8,128)(2,1)} %copy.22), calls=%async_computation.1 | async-start | bytes 1966080 | tf_op jit(solution)/shard_map/all_to_all | solution.py:51
  19.2 0.0 all-gather.3.cloned.1.call-start
  19.2 0.0 copy-done.1
  19.3 0.0 copy-done.4
  19.3 0.4 fusion.18
  19.6 0.0 copy-done.2
  19.6 0.0 copy-done.6
  19.6 0.0 copy-done.8
  19.6 0.2 fusion.8
  19.8 0.2 fusion.17
  20.0 0.3 fusion.4
  20.3 0.7 copy.27
  20.9 0.0 all-gather.3.cloned.1.call-update
  21.0 11.6 %all-to-all-done.1 = bf16[96,8,640]{2,0,1:T(8,128)(2,1)} async-done(((bf16[96,8,640]{2,0,1:T(8,128)(2,1)}), bf16[96,8,640]{2,0,1:T(8,128)(2,1)}, u32[]{:S(2)}, u32[]{:S(2)}) %all-to-all-start.1) | async-done | bytes 983072 | tf_op jit(solution)/shard_map/all_to_all | solution.py:51
  32.5 2.9 %broadcast_in_dim.15 = bf16[4,4096,80]{1,2,0:T(8,128)(2,1)} broadcast(bf16[4096,80]{0,1:T(8,128)(2,1)} %param.17), dimensions={1,2} | broadcast | bytes 3276800 | tf_op jit(solution)/shard_map/broadcast_in_dim | solution.py:47
  35.4 0.0 copy-start.5
  35.4 4.7 %all-to-all-start = ((bf16[4,4096,80]{1,2,0:T(8,128)(2,1)}), bf16[4,4096,80]{1,2,0:T(8,128)(2,1)}, u32[]{:S(2)}, u32[]{:S(2)}) async-start(bf16[4,4096,80]{1,2,0:T(8,128)(2,1)} %broadcast_in_dim.15), calls=%async_computation | async-start | bytes 5242880 | tf_op jit(solution)/shard_map/all_to_all | solution.py:48
  40.1 0.0 copy-done.5
  40.1 0.1 eq.28
  40.2 0.1 fusion.11
  40.3 0.1 reduce_window_sum.11
  40.4 0.2 select_reduce_fusion.1
  40.6 0.1 reduce_sum.49
  40.6 51.9 %all-gather.3.cloned.1.call-done = bf16[128,4096]{1,0:T(8,128)(2,1)} async-done(((bf16[8,4096]{1,0:T(8,128)(2,1)}), bf16[128,4096]{1,0:T(8,128)(2,1)}) %all-gather.3.cloned.1.call-update) | async-done | bytes 1048592 | tf_op jit(solution)/shard_map/all_gather | solution.py:45
  92.5 0.0 all-to-all-done
  92.5 0.0 copy-start.3
  92.5 3.1 %fusion.19 = f32[128,320]{1,0:T(8,128)S(1)} fusion(bf16[128,4096]{1,0:T(8,128)(2,1)} %all-gather.3.cloned.1.call-done, bf16[4096,320]{0,1:T(8,128)(2,1)} %bitcast.4), kind=kOutput, calls=%fused_computation.40 | convolution fusion | flops 335544320 | bytes 3833856 | tf_op jit(solution)/shard_map/reshape | solution.py:56
  95.7 22.9 %all-reduce.1 = bf16[128,320]{1,0:T(8,128)(2,1)} all-reduce(f32[128,320]{1,0:T(8,128)S(1)} %fusion.19), channel_id=1, replica_groups=mesh['head'=8,'ez'=16,'ey'=4] {'head'}, use_global_device_ids=true, to_apply=%region_2.3 | all-reduce | flops 40960 | bytes 245760 | tf_op jit(solution)/shard_map/psum | solution.py:57
  118.5 7.9 %all-to-all-start.2 = ((bf16[16,8,320]{2,1,0:T(8,128)(2,1)}), bf16[16,8,320]{2,1,0:T(8,128)(2,1)S(1)}, u32[]{:S(2)}, u32[]{:S(2)}) async-start(bf16[16,8,320]{2,1,0:T(8,128)(2,1)} %bitcast.37), calls=%async_computation.2 | async-start | bytes 196608 | tf_op jit(solution)/shard_map/all_to_all | solution.py:58
  126.4 0.0 all-gather.5.cloned.1.call-start
  126.5 0.1 copy.25
  126.5 0.8 dynamic-slice
  127.3 0.1 convert_reduce_fusion
  127.4 12.4 %all-to-all-done.2 = bf16[16,8,320]{2,1,0:T(8,128)(2,1)S(1)} async-done(((bf16[16,8,320]{2,1,0:T(8,128)(2,1)}), bf16[16,8,320]{2,1,0:T(8,128)(2,1)S(1)}, u32[]{:S(2)}, u32[]{:S(2)}) %all-to-all-start.2) | async-done | bytes 81952 | tf_op jit(solution)/shard_map/all_to_all | solution.py:58
  139.9 0.1 reshape.56
  140.0 0.0 copy-done.3
  140.0 0.2 multiply_reduce_fusion
  140.2 0.3 convolution_convert_fusion.1
  140.5 0.1 reshape.52
  140.5 27.2 %all_to_all.43 = bf16[64,2,640]{2,1,0:T(2,128)(2,1)S(1)} all-to-all(bf16[64,2,640]{2,1,0:T(2,128)(2,1)S(1)} %reshape.52), channel_id=1, replica_groups=mesh['head'=8,'ez'=16,'ey'=4] {'ez','ey'}, dimensions={0} | all-to-all | bytes 327680 | tf_op jit(solution)/shard_map/all_to_all | solution.py:84
  167.7 0.7 reshape.53
  168.4 0.0 all-gather.5.cloned.1.call-update
  168.5 20.0 %all-gather.5.cloned.1.call-done = bf16[128,5120]{1,0:T(8,128)(2,1)} async-done(((bf16[128,640]{1,0:T(8,128)(2,1)}), bf16[128,5120]{1,0:T(8,128)(2,1)}) %all-gather.5.cloned.1.call-update) | async-done | bytes 1310736 | tf_op jit(solution)/shard_map/all_gather | solution.py:86
  188.5 0.0 copy-done
  188.5 2.0 fusion.1
  190.5 0.0 copy-start.7
  190.5 12.8 %all_gather.11 = bf16[128,768]{0,1:T(8,128)(2,1)S(1)} all-gather(bf16[128,96]{0,1:T(8,128)(2,1)S(1)} %fusion.10), channel_id=1, replica_groups=mesh['head'=8,'ez'=16,'ey'=4] {'head'}, dimensions={1}, use_global_device_ids=true | all-gather | bytes 221184 | tf_op jit(solution)/shard_map/all_gather | solution.py:89
  203.3 1.5 convolution_convert_fusion
  204.9 0.7 reshape.54
  205.6 15.4 %all-to-all-start.4 = ((bf16[64,2,640]{2,1,0:T(2,128)(2,1)}), bf16[64,2,640]{2,1,0:T(2,128)(2,1)S(1)}, u32[]{:S(2)}, u32[]{:S(2)}) async-start(bf16[64,2,640]{2,1,0:T(2,128)(2,1)} %reshape.54), calls=%async_computation.4 | async-start | bytes 327680 | tf_op jit(solution)/shard_map/all_to_all | solution.py:92
  221.1 0.0 copy-done.7
  221.1 0.1 copy.26
  221.1 0.1 select_reduce_fusion
  221.2 19.3 %all-to-all-done.4 = bf16[64,2,640]{2,1,0:T(2,128)(2,1)S(1)} async-done(((bf16[64,2,640]{2,1,0:T(2,128)(2,1)}), bf16[64,2,640]{2,1,0:T(2,128)(2,1)S(1)}, u32[]{:S(2)}, u32[]{:S(2)}) %all-to-all-start.4) | async-done | bytes 163872 | tf_op jit(solution)/shard_map/all_to_all | solution.py:92
  240.6 0.1 reshape.55
  240.6 0.8 convolution_add_fusion.1
  (5 shorter events, 0.1 us)
Async XLA Ops:
  6.5 182.0 %copy-start = (bf16[1,2,96,5120]{3,2,1,0:T(8,128)(2,1)S(1)}, bf16[1,2,96,5120]{3,2,1,0:T(8,128)(2,1)}, u32[]{:S(2)}) copy-start(bf16[1,2,96,5120]{3,2,1,0:T(8,128)(2,1)} %param.22) | copy-start | bytes 5898244
  8.0 11.2 %copy-start.1 = (bf16[8,128,512]{2,1,0:T(8,128)(2,1)S(1)}, bf16[8,128,512]{2,1,0:T(8,128)(2,1)}, u32[]{:S(2)}) copy-start(bf16[8,128,512]{2,1,0:T(8,128)(2,1)} %param.14) | copy-start | bytes 3145732
  8.0 11.2 %copy-start.4 = (bf16[8,8,512]{2,1,0:T(8,128)(2,1)S(1)}, bf16[8,8,512]{2,1,0:T(8,128)(2,1)}, u32[]{:S(2)}) copy-start(bf16[8,8,512]{2,1,0:T(8,128)(2,1)} %param.12) | copy-start | bytes 196612
  9.1 10.5 %copy-start.2 = (bf16[8,64,128]{2,1,0:T(8,128)(2,1)S(1)}, bf16[8,64,128]{2,1,0:T(8,128)(2,1)}, u32[]{:S(2)}) copy-start(bf16[8,64,128]{2,1,0:T(8,128)(2,1)} %param.15) | copy-start | bytes 393220
  9.1 10.5 %copy-start.6 = (bf16[8,8,64]{2,1,0:T(8,128)(2,1)S(1)}, bf16[8,8,64]{2,1,0:T(8,128)(2,1)}, u32[]{:S(2)}) copy-start(bf16[8,8,64]{2,1,0:T(8,128)(2,1)} %param.13) | copy-start | bytes 24580
  9.1 10.5 %copy-start.8 = (s32[8]{0:T(128)S(1)}, s32[8]{0:T(128)}, u32[]{:S(2)}) copy-start(s32[8]{0:T(128)} %param.16) | copy-start | bytes 100
  9.1 23.4 %all-to-all-start.1 = ((bf16[96,8,640]{2,0,1:T(8,128)(2,1)}), bf16[96,8,640]{2,0,1:T(8,128)(2,1)}, u32[]{:S(2)}, u32[]{:S(2)}) async-start(bf16[96,8,640]{2,0,1:T(8,128)(2,1)} %copy.22), calls=%async_computation.1 | async-start | bytes 1966080 | tf_op jit(solution)/shard_map/all_to_all | solution.py:51
  19.2 73.3 %all-gather.3.cloned.1.call-start = ((), (), s32[]{:S(2)}) async-start(), calls=%async_computation.5 | async-start | bytes 1114112 | tf_op jit(solution)/shard_map/all_gather | solution.py:45
  35.4 4.7 %copy-start.5 = (s32[8,6]{1,0:T(8,128)S(1)}, s32[8,6]{1,0:T(8,128)}, u32[]{:S(2)}) copy-start(s32[8,6]{1,0:T(8,128)} %param.20) | copy-start | bytes 580
  35.4 57.1 %all-to-all-start = ((bf16[4,4096,80]{1,2,0:T(8,128)(2,1)}), bf16[4,4096,80]{1,2,0:T(8,128)(2,1)}, u32[]{:S(2)}, u32[]{:S(2)}) async-start(bf16[4,4096,80]{1,2,0:T(8,128)(2,1)} %broadcast_in_dim.15), calls=%async_computation | async-start | bytes 5242880 | tf_op jit(solution)/shard_map/all_to_all | solution.py:48
  92.5 47.5 %copy-start.3 = (bf16[8,5120]{1,0:T(8,128)(2,1)S(1)}, bf16[8,5120]{1,0:T(8,128)(2,1)}, u32[]{:S(2)}) copy-start(bf16[8,5120]{1,0:T(8,128)(2,1)} %param.18) | copy-start | bytes 245764
  118.5 21.3 %all-to-all-start.2 = ((bf16[16,8,320]{2,1,0:T(8,128)(2,1)}), bf16[16,8,320]{2,1,0:T(8,128)(2,1)S(1)}, u32[]{:S(2)}, u32[]{:S(2)}) async-start(bf16[16,8,320]{2,1,0:T(8,128)(2,1)} %bitcast.37), calls=%async_computation.2 | async-start | bytes 196608 | tf_op jit(solution)/shard_map/all_to_all | solution.py:58
  126.4 62.1 %all-gather.5.cloned.1.call-start = ((), (), s32[]{:S(2)}) async-start(), calls=%async_computation.6 | async-start | bytes 1474560 | tf_op jit(solution)/shard_map/all_gather | solution.py:86
  190.5 30.6 %copy-start.7 = (f32[8,6]{1,0:T(8,128)S(1)}, f32[8,6]{1,0:T(8,128)}, u32[]{:S(2)}) copy-start(f32[8,6]{1,0:T(8,128)} %param.21) | copy-start | bytes 580
  205.6 35.0 %all-to-all-start.4 = ((bf16[64,2,640]{2,1,0:T(2,128)(2,1)}), bf16[64,2,640]{2,1,0:T(2,128)(2,1)S(1)}, u32[]{:S(2)}, u32[]{:S(2)}) async-start(bf16[64,2,640]{2,1,0:T(2,128)(2,1)} %reshape.54), calls=%async_computation.4 | async-start | bytes 327680 | tf_op jit(solution)/shard_map/all_to_all | solution.py:92
Sparse Core Ops, SparseCore 0:
  22.1 70.3 all-gather.2
  168.6 19.8 all-gather.4

commit v6 on v5

--- a/solution.py
+++ b/solution.py
@@ -42,15 +42,11 @@
     seq_local = q_latent.shape[0]
     latent_out = attend(q_latent, q_rotary, cache_latent, cache_rotary, lengths)
     flattened = latent_out.reshape(seq_local, -1)
-    gathered = lax.all_gather(flattened, "ez", axis=0, tiled=True)
-    y_count = lax.axis_size("ey")
-    value_copies = jnp.broadcast_to(w_value_out[None], (y_count,) + w_value_out.shape)
-    value_blocks = lax.all_to_all(value_copies, "ey", split_axis=0, concat_axis=0, tiled=True)
-    head_count = lax.axis_size("head")
-    down_blocks = w_down[0].reshape(w_down.shape[1], head_count, -1)
-    down_cols = lax.all_to_all(down_blocks, "head", split_axis=1, concat_axis=0, tiled=True)
-    down_cols = down_cols.reshape(-1, down_blocks.shape[2])
-    gathered, value_blocks, down_cols = lax.optimization_barrier((gathered, value_blocks, down_cols))
+    z_count = lax.axis_size("ez")
+    latent_copies = jnp.broadcast_to(flattened[None], (z_count,) + flattened.shape)
+    gathered = lax.all_to_all(latent_copies, "ez", split_axis=0, concat_axis=0, tiled=True)
+    gathered = gathered.reshape(-1, flattened.shape[1])
+    value_blocks = lax.all_gather(w_value_out, "ey", axis=0, tiled=False)
     column_terms = jnp.einsum(
         "sk,jkc->sjc", gathered, value_blocks, preferred_element_type=jnp.float32
     ).reshape(gathered.shape[0], -1)
@@ -83,6 +79,11 @@
     outgoing = outgoing.reshape(expert_count, capacity, -1)
     arrived = lax.all_to_all(outgoing, EXPERT, split_axis=0, concat_axis=0, tiled=True)
     arrived_cols = arrived.reshape(-1, arrived.shape[2])
+    head_count = lax.axis_size("head")
+    down_blocks = w_down[0].reshape(w_down.shape[1], head_count, -1)
+    arrived_cols, down_blocks = lax.optimization_barrier((arrived_cols, down_blocks))
+    down_cols = lax.all_to_all(down_blocks, "head", split_axis=1, concat_axis=0, tiled=True)
+    down_cols = down_cols.reshape(-1, down_blocks.shape[2])
     flat_rows = lax.all_gather(arrived_cols, "head", axis=1, tiled=True)
     projected = jnp.einsum("rd,gfd->rgf", flat_rows, gate_up, preferred_element_type=jnp.float32)
     hidden = (jax.nn.silu(projected[:, 0]) * projected[:, 1]).astype(jnp.bfloat16)

time: 249 us -> 235 us (0.944)
  blocking collectives: 62.9 us -> 34.8 us
  starting transfers between devices: 38.1 us -> 50.8 us
  local copies, waits for them, and re-layouts: 8.99 us -> 18 us
  waiting for transfers between devices: 115 us -> 107 us
    all_to_all x1 -> x2, waiting for transfers between devices: 0.01 us -> 27.6 us  [the longest x1 17.8 us: on_device(): lax.all_to_all(outgoing, EXPERT, split_axis=0, concat_axis=0, tiled=True)]
    all_to_all x1 -> x0, blocking collectives: 27.2 us -> none  [on_device(): lax.all_to_all(outgoing, EXPERT, split_axis=0, concat_axis=0, tiled=True)]
    all_gather x1, waiting for transfers between devices: 51.9 us -> 29.5 us  [on_device(): value_blocks = lax.all_gather(w_value_out, 'ey', axis=0, tiled=False)]
    all_to_all x1 -> x2, starting transfers between devices: 4.67 us -> 23.2 us  [the longest x1 15.2 us: on_device(): lax.all_to_all(latent_copies, 'ez', split_axis=0, concat_axis=0, tiled=True)]
    all_to_all x1, waiting for transfers between devices: 11.6 us -> 0.01 us  [on_device(): lax.all_to_all(down_blocks, 'head', split_axis=1, concat_axis=0, tiled=True)]
    all_to_all x1, starting transfers between devices: 10.1 us -> 4.51 us  [on_device(): lax.all_to_all(down_blocks, 'head', split_axis=1, concat_axis=0, tiled=True)]
    all_gather x0 -> x1, local copies, waits for them, and re-layouts: none -> 5.53 us  [on_device(): value_blocks = lax.all_gather(w_value_out, 'ey', axis=0, tiled=False)]
    dot_general x0 -> x1, local copies, waits for them, and re-layouts: none -> 4.68 us  [on_device(): jnp.einsum('sk,jkc->sjc', gathered, value_blocks, preferred_element_type=...]
  transfers between devices with their start and end apart: 6 -> 7, of which waited for: 5 -> 6; matrix products, arithmetic and copies ran while one was open for 2% -> 9% of each run, Pallas kernels for 0% -> 0%
where the time goes in v6:
time: 235 us; the launch traced here: 234 us
  waiting for transfers between devices  107 us (46%)
  starting transfers between devices  50.8 us (22%)
  blocking collectives  34.8 us (15%)
  local copies, waits for them, and re-layouts  18 us (8%)
  between operations  13.6 us (6%)
  matrix products  9.05 us (4%)
    all_gather x1, waiting for transfers between devices, on_device(): value_blocks = lax.all_gather(w_value_out, 'ey', axis=0, tiled=False)  29.5 us
    psum x1, blocking collectives, on_device(): column_sums = lax.psum(column_terms, 'head')  22 us
    all_to_all x1, waiting for transfers between devices, on_device(): lax.all_to_all(summed_rows, EXPERT, split_axis=0, concat_axis=0, tiled=True)  19.3 us
    all_to_all x1, waiting for transfers between devices, on_device(): lax.all_to_all(outgoing, EXPERT, split_axis=0, concat_axis=0, tiled=True)  17.8 us
    all_gather x1, waiting for transfers between devices, on_device(): flat_rows = lax.all_gather(arrived_cols, 'head', axis=1, tiled=True)  17.1 us
    all_to_all x1, starting transfers between devices, on_device(): lax.all_to_all(latent_copies, 'ez', split_axis=0, concat_axis=0, tiled=True)  15.2 us
    all_to_all x1, starting transfers between devices, on_device(): lax.all_to_all(summed_rows, EXPERT, split_axis=0, concat_axis=0, tiled=True)  12.8 us
    all_gather x1, blocking collectives, on_device(): hidden_all = lax.all_gather(hidden, 'head', axis=1, tiled=True)  12.8 us
  transfers between devices with their start and end apart: 7, of which 6 were waited for; matrix products, arithmetic and copies ran while one was open for 9% of the time, Pallas kernels for 0%

profile of v6, /device:TPU:6, one launch (start us, length us, event | category | flops | bytes accessed | tf_op | source)
XLA Modules:
  0.0 233.9 jit_solution(10736050746131402408)
XLA Ops:
  6.5 0.0 copy-start
  6.5 0.0 copy-start.1
  6.5 0.0 all-gather.6.cloned.1.call-start
  6.5 0.7 all-gather.6.cloned.1.call-update
  7.3 1.6 fusion.20
  8.9 1.1 fusion.8
  10.0 0.2 fusion.19
  10.1 0.0 copy-done.1
  10.1 0.3 fusion.4
  10.4 0.0 copy-start.3
  10.5 1.1 broadcast_in_dim.33
  11.6 15.2 %all-to-all-start = ((bf16[16,8,4096]{2,1,0:T(8,128)(2,1)}), bf16[16,8,4096]{2,1,0:T(8,128)(2,1)S(1)}, u32[]{:S(2)}, u32[]{:S(2)}) async-start(bf16[16,8,4096]{2,1,0:T(8,128)(2,1)} %broadcast_in_dim.33), calls=%async_computation | async-start | bytes 2097152 | tf_op jit(solution)/shard_map/all_to_all | solution.py:47
  26.8 0.0 copy-done.3
  26.8 0.1 eq.28
  26.9 0.1 fusion.13
  27.0 0.1 reduce_window_sum.11
  27.1 0.2 select_reduce_fusion.1
  27.2 0.1 reduce_sum.49
  27.3 29.5 %all-gather.6.cloned.1.call-done = bf16[16384,80]{0,1:T(8,128)(2,1)} async-done(((bf16[4096,80]{0,1:T(8,128)(2,1)}), bf16[16384,80]{0,1:T(8,128)(2,1)}) %all-gather.6.cloned.1.call-update) | async-done | bytes 2621456 | tf_op jit(solution)/shard_map/all_gather | solution.py:49
  56.8 5.5 %reshape.55 = bf16[4,4096,80]{1,0,2:T(4,128)(2,1)} reshape(bf16[16384,80]{0,1:T(8,128)(2,1)} %all-gather.6.cloned.1.call-done) | data formatting | bytes 5242880 | tf_op jit(solution)/shard_map/all_gather | solution.py:49
  62.3 4.7 %copy.24 = bf16[4,80,4096]{2,1,0:T(8,128)(2,1)} copy(bf16[4,80,4096]{2,0,1:T(4,128)(2,1)} %bitcast.50) | data formatting | bytes 5242880 | tf_op jit(solution)/shard_map/sk,jkc->sjc/dot_general | solution.py:50
  67.0 9.8 %all-to-all-done = bf16[16,8,4096]{2,1,0:T(8,128)(2,1)S(1)} async-done(((bf16[16,8,4096]{2,1,0:T(8,128)(2,1)}), bf16[16,8,4096]{2,1,0:T(8,128)(2,1)S(1)}, u32[]{:S(2)}, u32[]{:S(2)}) %all-to-all-start) | async-done | bytes 1048608 | tf_op jit(solution)/shard_map/all_to_all | solution.py:47
  76.8 0.0 copy-start.2
  76.8 2.6 %fusion.9 = f32[128,320]{0,1:T(8,128)S(1)} fusion(bf16[320,4096]{1,0:T(8,128)(2,1)} %bitcast.49, bf16[16,8,4096]{2,1,0:T(8,128)(2,1)S(1)} %all-to-all-done), kind=kOutput, calls=%fused_computation.14 | convolution fusion | flops 335544320 | bytes 3833856 | tf_op jit(solution)/shard_map/sk,jkc->sjc/dot_general | solution.py:50
  79.4 22.0 %all-reduce.1 = bf16[128,320]{0,1:T(8,128)(2,1)S(1)} all-reduce(f32[128,320]{0,1:T(8,128)S(1)} %fusion.9), channel_id=1, replica_groups=mesh['head'=8,'ez'=16,'ey'=4] {'head'}, use_global_device_ids=true, to_apply=%region_2.3 | all-reduce | flops 40960 | bytes 245760 | tf_op jit(solution)/shard_map/psum | solution.py:53
  101.4 0.7 copy.25
  102.2 10.2 %all-to-all-start.1 = ((bf16[16,8,320]{2,1,0:T(8,128)(2,1)}), bf16[16,8,320]{2,1,0:T(8,128)(2,1)S(1)}, u32[]{:S(2)}, u32[]{:S(2)}) async-start(bf16[16,8,320]{2,1,0:T(8,128)(2,1)} %bitcast.3), calls=%async_computation.1 | async-start | bytes 196608 | tf_op jit(solution)/shard_map/all_to_all | solution.py:54
  112.4 0.1 copy.27
  112.5 0.8 dynamic-slice
  113.3 0.1 convert_reduce_fusion
  113.3 12.6 %all-to-all-done.1 = bf16[16,8,320]{2,1,0:T(8,128)(2,1)S(1)} async-done(((bf16[16,8,320]{2,1,0:T(8,128)(2,1)}), bf16[16,8,320]{2,1,0:T(8,128)(2,1)S(1)}, u32[]{:S(2)}, u32[]{:S(2)}) %all-to-all-start.1) | async-done | bytes 81952 | tf_op jit(solution)/shard_map/all_to_all | solution.py:54
  126.0 0.1 reshape.54
  126.1 0.0 copy-done.2
  126.1 0.2 multiply_reduce_fusion
  126.2 0.3 convolution_convert_fusion.1
  126.6 0.7 reshape.49
  127.3 8.0 %all-to-all-start.2 = ((bf16[64,2,640]{2,1,0:T(2,128)(2,1)}), bf16[64,2,640]{2,1,0:T(2,128)(2,1)S(1)}, u32[]{:S(2)}, u32[]{:S(2)}) async-start(bf16[64,2,640]{2,1,0:T(2,128)(2,1)} %reshape.49), calls=%async_computation.2 | async-start | bytes 327680 | tf_op jit(solution)/shard_map/all_to_all | solution.py:80
  135.3 0.0 all-gather.4.cloned.1.call-start
  135.4 1.3 copy.31
  136.7 17.8 %all-to-all-done.2 = bf16[64,2,640]{2,1,0:T(2,128)(2,1)S(1)} async-done(((bf16[64,2,640]{2,1,0:T(2,128)(2,1)}), bf16[64,2,640]{2,1,0:T(2,128)(2,1)S(1)}, u32[]{:S(2)}, u32[]{:S(2)}) %all-to-all-start.2) | async-done | bytes 163872 | tf_op jit(solution)/shard_map/all_to_all | solution.py:80
  154.5 0.7 reshape.50
  155.3 0.0 all-gather.4.cloned.1.call-update
  155.3 1.1 copy.29
  156.4 4.5 %all-to-all-start.3 = ((bf16[96,8,640]{2,0,1:T(8,128)(2,1)}), bf16[96,8,640]{2,0,1:T(8,128)(2,1)S(1)}, u32[]{:S(2)}, u32[]{:S(2)}) async-start(bf16[96,8,640]{2,0,1:T(8,128)(2,1)} %copy.29), calls=%async_computation.3 | async-start | bytes 1966080 | tf_op jit(solution)/shard_map/all_to_all | solution.py:85
  160.9 17.1 %all-gather.4.cloned.1.call-done = bf16[128,5120]{1,0:T(8,128)(2,1)} async-done(((bf16[128,640]{1,0:T(8,128)(2,1)}), bf16[128,5120]{1,0:T(8,128)(2,1)}) %all-gather.4.cloned.1.call-update) | async-done | bytes 1310736 | tf_op jit(solution)/shard_map/all_gather | solution.py:87
  177.9 0.0 copy-done
  177.9 2.0 fusion.1
  179.9 0.0 copy-start.4
  180.0 12.8 %all_gather.15 = bf16[128,768]{0,1:T(8,128)(2,1)S(1)} all-gather(bf16[128,96]{0,1:T(8,128)(2,1)S(1)} %fusion.12), channel_id=1, replica_groups=mesh['head'=8,'ez'=16,'ey'=4] {'head'}, dimensions={1}, use_global_device_ids=true | all-gather | bytes 221184 | tf_op jit(solution)/shard_map/all_gather | solution.py:90
  192.8 0.0 all-to-all-done.3
  192.8 0.3 convolution_convert_fusion
  193.1 0.7 reshape.52
  193.9 12.8 %all-to-all-start.4 = ((bf16[64,2,640]{2,1,0:T(2,128)(2,1)}), bf16[64,2,640]{2,1,0:T(2,128)(2,1)S(1)}, u32[]{:S(2)}, u32[]{:S(2)}) async-start(bf16[64,2,640]{2,1,0:T(2,128)(2,1)} %reshape.52), calls=%async_computation.4 | async-start | bytes 327680 | tf_op jit(solution)/shard_map/all_to_all | solution.py:93
  206.7 0.0 copy-done.4
  206.7 0.1 copy.28
  206.8 0.1 select_reduce_fusion
  206.8 19.3 %all-to-all-done.4 = bf16[64,2,640]{2,1,0:T(2,128)(2,1)S(1)} async-done(((bf16[64,2,640]{2,1,0:T(2,128)(2,1)}), bf16[64,2,640]{2,1,0:T(2,128)(2,1)S(1)}, u32[]{:S(2)}, u32[]{:S(2)}) %all-to-all-start.4) | async-done | bytes 163872 | tf_op jit(solution)/shard_map/all_to_all | solution.py:93
  226.2 0.1 reshape.53
  226.2 0.8 convolution_add_fusion.1
  (6 shorter events, 0.1 us)
Async XLA Ops:
  6.5 171.4 %copy-start = (bf16[1,2,96,5120]{3,2,1,0:T(8,128)(2,1)S(1)}, bf16[1,2,96,5120]{3,2,1,0:T(8,128)(2,1)}, u32[]{:S(2)}) copy-start(bf16[1,2,96,5120]{3,2,1,0:T(8,128)(2,1)} %param.22) | copy-start | bytes 5898244
  6.5 3.6 %copy-start.1 = (bf16[8,128,512]{2,1,0:T(8,128)(2,1)S(1)}, bf16[8,128,512]{2,1,0:T(8,128)(2,1)}, u32[]{:S(2)}) copy-start(bf16[8,128,512]{2,1,0:T(8,128)(2,1)} %param.14) | copy-start | bytes 3145732
  6.5 50.3 %all-gather.6.cloned.1.call-start = ((), (), s32[]{:S(2)}) async-start(), calls=%async_computation.6 | async-start | bytes 3276800 | tf_op jit(solution)/shard_map/all_gather | solution.py:49
  10.4 16.4 %copy-start.3 = (s32[8,6]{1,0:T(8,128)S(1)}, s32[8,6]{1,0:T(8,128)}, u32[]{:S(2)}) copy-start(s32[8,6]{1,0:T(8,128)} %param.20) | copy-start | bytes 580
  11.6 65.2 %all-to-all-start = ((bf16[16,8,4096]{2,1,0:T(8,128)(2,1)}), bf16[16,8,4096]{2,1,0:T(8,128)(2,1)S(1)}, u32[]{:S(2)}, u32[]{:S(2)}) async-start(bf16[16,8,4096]{2,1,0:T(8,128)(2,1)} %broadcast_in_dim.33), calls=%async_computation | async-start | bytes 2097152 | tf_op jit(solution)/shard_map/all_to_all | solution.py:47
  76.8 49.3 %copy-start.2 = (bf16[8,5120]{1,0:T(8,128)(2,1)S(1)}, bf16[8,5120]{1,0:T(8,128)(2,1)}, u32[]{:S(2)}) copy-start(bf16[8,5120]{1,0:T(8,128)(2,1)} %param.18) | copy-start | bytes 245764
  102.2 23.7 %all-to-all-start.1 = ((bf16[16,8,320]{2,1,0:T(8,128)(2,1)}), bf16[16,8,320]{2,1,0:T(8,128)(2,1)S(1)}, u32[]{:S(2)}, u32[]{:S(2)}) async-start(bf16[16,8,320]{2,1,0:T(8,128)(2,1)} %bitcast.3), calls=%async_computation.1 | async-start | bytes 196608 | tf_op jit(solution)/shard_map/all_to_all | solution.py:54
  127.3 27.3 %all-to-all-start.2 = ((bf16[64,2,640]{2,1,0:T(2,128)(2,1)}), bf16[64,2,640]{2,1,0:T(2,128)(2,1)S(1)}, u32[]{:S(2)}, u32[]{:S(2)}) async-start(bf16[64,2,640]{2,1,0:T(2,128)(2,1)} %reshape.49), calls=%async_computation.2 | async-start | bytes 327680 | tf_op jit(solution)/shard_map/all_to_all | solution.py:80
  135.3 42.6 %all-gather.4.cloned.1.call-start = ((), (), s32[]{:S(2)}) async-start(), calls=%async_computation.5 | async-start | bytes 1474560 | tf_op jit(solution)/shard_map/all_gather | solution.py:87
  156.4 36.4 %all-to-all-start.3 = ((bf16[96,8,640]{2,0,1:T(8,128)(2,1)}), bf16[96,8,640]{2,0,1:T(8,128)(2,1)S(1)}, u32[]{:S(2)}, u32[]{:S(2)}) async-start(bf16[96,8,640]{2,0,1:T(8,128)(2,1)} %copy.29), calls=%async_computation.3 | async-start | bytes 1966080 | tf_op jit(solution)/shard_map/all_to_all | solution.py:85
  179.9 26.7 %copy-start.4 = (f32[8,6]{1,0:T(8,128)S(1)}, f32[8,6]{1,0:T(8,128)}, u32[]{:S(2)}) copy-start(f32[8,6]{1,0:T(8,128)} %param.21) | copy-start | bytes 580
  193.9 32.3 %all-to-all-start.4 = ((bf16[64,2,640]{2,1,0:T(2,128)(2,1)}), bf16[64,2,640]{2,1,0:T(2,128)(2,1)S(1)}, u32[]{:S(2)}, u32[]{:S(2)}) async-start(bf16[64,2,640]{2,1,0:T(2,128)(2,1)} %reshape.52), calls=%async_computation.4 | async-start | bytes 327680 | tf_op jit(solution)/shard_map/all_to_all | solution.py:93
Sparse Core Ops, SparseCore 0:
  9.5 47.2 all-gather.5
  155.4 22.4 all-gather.3

commit v7 on v6

--- a/solution.py
+++ b/solution.py
@@ -46,10 +46,8 @@
     latent_copies = jnp.broadcast_to(flattened[None], (z_count,) + flattened.shape)
     gathered = lax.all_to_all(latent_copies, "ez", split_axis=0, concat_axis=0, tiled=True)
     gathered = gathered.reshape(-1, flattened.shape[1])
-    value_blocks = lax.all_gather(w_value_out, "ey", axis=0, tiled=False)
-    column_terms = jnp.einsum(
-        "sk,jkc->sjc", gathered, value_blocks, preferred_element_type=jnp.float32
-    ).reshape(gathered.shape[0], -1)
+    value_cols = lax.all_gather(w_value_out, "ey", axis=1, tiled=True)
+    column_terms = jnp.dot(gathered, value_cols, preferred_element_type=jnp.float32)
     column_sums = lax.psum(column_terms, "head")
     attention = lax.all_to_all(
         column_sums.astype(jnp.bfloat16), "ez", split_axis=0, concat_axis=1, tiled=True

time: 235 us -> 236 us (level)
  local copies, waits for them, and re-layouts: 18 us -> 7.78 us
  waiting for transfers between devices: 107 us -> 116 us
    all_to_all x1, waiting for transfers between devices: 9.78 us -> 48.7 us  [on_device(): lax.all_to_all(latent_copies, 'ez', split_axis=0, concat_axis=0, tiled=True)]
    all_gather x1, waiting for transfers between devices: 29.5 us -> 0.01 us  [on_device(): value_cols = lax.all_gather(w_value_out, 'ey', axis=1, tiled=True)]
    all_gather x1 -> x0, local copies, waits for them, and re-layouts: 5.53 us -> none  [on_device(): value_blocks = lax.all_gather(w_value_out, 'ey', axis=0, tiled=False)]
    dot_general x1 -> x0, local copies, waits for them, and re-layouts: 4.68 us -> none  [on_device(): jnp.einsum('sk,jkc->sjc', gathered, value_blocks, preferred_element_type=...]
  transfers between devices with their start and end apart: 7 -> 7, of which waited for: 6 -> 5; matrix products, arithmetic and copies ran while one was open for 9% -> 3% of each run, Pallas kernels for 0% -> 0%
where the time goes in v7:
time: 236 us; the launch traced here: 235 us
  waiting for transfers between devices  116 us (49%)
  starting transfers between devices  50.9 us (22%)
  blocking collectives  34.8 us (15%)
  between operations  13.6 us (6%)
  matrix products  10.4 us (4%)
  local copies, waits for them, and re-layouts  7.78 us (3%)
    all_to_all x1, waiting for transfers between devices, on_device(): lax.all_to_all(latent_copies, 'ez', split_axis=0, concat_axis=0, tiled=True)  48.7 us
    psum x1, blocking collectives, on_device(): column_sums = lax.psum(column_terms, 'head')  22 us
    all_to_all x1, waiting for transfers between devices, on_device(): lax.all_to_all(summed_rows, EXPERT, split_axis=0, concat_axis=0, tiled=True)  19.3 us
    all_to_all x1, waiting for transfers between devices, on_device(): lax.all_to_all(outgoing, EXPERT, split_axis=0, concat_axis=0, tiled=True)  17.8 us
    all_gather x1, waiting for transfers between devices, on_device(): flat_rows = lax.all_gather(arrived_cols, 'head', axis=1, tiled=True)  17.1 us
    all_to_all x1, starting transfers between devices, on_device(): lax.all_to_all(latent_copies, 'ez', split_axis=0, concat_axis=0, tiled=True)  15.2 us
    all_to_all x1, starting transfers between devices, on_device(): lax.all_to_all(summed_rows, EXPERT, split_axis=0, concat_axis=0, tiled=True)  12.8 us
    all_gather x1, blocking collectives, on_device(): hidden_all = lax.all_gather(hidden, 'head', axis=1, tiled=True)  12.8 us
  transfers between devices with their start and end apart: 7, of which 5 were waited for; matrix products, arithmetic and copies ran while one was open for 3% of the time, Pallas kernels for 0%

profile of v7, /device:TPU:6, one launch (start us, length us, event | category | flops | bytes accessed | tf_op | source)
XLA Modules:
  0.0 234.6 jit_solution(13916893692590816185)
XLA Ops:
  6.5 0.0 copy-start
  6.5 1.8 fusion.20
  8.3 1.1 fusion.8
  9.4 0.2 fusion.19
  9.5 1.5 fusion.4
  11.1 0.0 copy-start.2
  11.1 1.1 broadcast_in_dim.33
  12.2 15.2 %all-to-all-start = ((bf16[16,8,4096]{2,1,0:T(8,128)(2,1)}), bf16[16,8,4096]{2,1,0:T(8,128)(2,1)S(1)}, u32[]{:S(2)}, u32[]{:S(2)}) async-start(bf16[16,8,4096]{2,1,0:T(8,128)(2,1)} %broadcast_in_dim.33), calls=%async_computation | async-start | bytes 2097152 | tf_op jit(solution)/shard_map/all_to_all | solution.py:47
  27.4 0.0 all-gather.3.cloned.1.call-start
  27.5 0.7 all-gather.3.cloned.1.call-update
  28.2 0.0 copy-done.2
  28.2 0.1 eq.28
  28.3 0.1 fusion.13
  28.3 0.1 reduce_window_sum.11
  28.4 0.2 select_reduce_fusion.1
  28.6 0.1 reduce_sum.49
  28.7 0.0 copy-start.1
  28.7 48.7 %all-to-all-done = bf16[16,8,4096]{2,1,0:T(8,128)(2,1)S(1)} async-done(((bf16[16,8,4096]{2,1,0:T(8,128)(2,1)}), bf16[16,8,4096]{2,1,0:T(8,128)(2,1)S(1)}, u32[]{:S(2)}, u32[]{:S(2)}) %all-to-all-start) | async-done | bytes 1048608 | tf_op jit(solution)/shard_map/all_to_all | solution.py:47
  77.4 0.0 all-gather.3.cloned.1.call-done
  77.4 2.6 %fusion.9 = f32[128,320]{0,1:T(8,128)S(1)} fusion(bf16[4096,320]{0,1:T(8,128)(2,1)} %all-gather.3.cloned.1.call-done, bf16[16,8,4096]{2,1,0:T(8,128)(2,1)S(1)} %all-to-all-done), kind=kOutput, calls=%fused_computation.14 | convolution fusion | flops 335544320 | bytes 3833856 | tf_op jit(solution)/shard_map/dot_general | solution.py:50
  80.0 22.0 %all-reduce.1 = bf16[128,320]{0,1:T(8,128)(2,1)S(1)} all-reduce(f32[128,320]{0,1:T(8,128)S(1)} %fusion.9), channel_id=1, replica_groups=mesh['head'=8,'ez'=16,'ey'=4] {'head'}, use_global_device_ids=true, to_apply=%region_2.3 | all-reduce | flops 40960 | bytes 245760 | tf_op jit(solution)/shard_map/psum | solution.py:51
  102.0 0.7 copy.22
  102.7 11.6 %all-to-all-start.1 = ((bf16[16,8,320]{2,1,0:T(8,128)(2,1)}), bf16[16,8,320]{2,1,0:T(8,128)(2,1)S(1)}, u32[]{:S(2)}, u32[]{:S(2)}) async-start(bf16[16,8,320]{2,1,0:T(8,128)(2,1)} %bitcast.1), calls=%async_computation.1 | async-start | bytes 196608 | tf_op jit(solution)/shard_map/all_to_all | solution.py:52
  114.3 0.1 copy.24
  114.4 0.8 dynamic-slice
  115.2 0.1 convert_reduce_fusion
  115.3 12.6 %all-to-all-done.1 = bf16[16,8,320]{2,1,0:T(8,128)(2,1)S(1)} async-done(((bf16[16,8,320]{2,1,0:T(8,128)(2,1)}), bf16[16,8,320]{2,1,0:T(8,128)(2,1)S(1)}, u32[]{:S(2)}, u32[]{:S(2)}) %all-to-all-start.1) | async-done | bytes 81952 | tf_op jit(solution)/shard_map/all_to_all | solution.py:52
  127.9 0.1 reshape.52
  128.0 0.0 copy-done.1
  128.0 0.2 multiply_reduce_fusion
  128.2 0.3 convolution_convert_fusion.1
  128.5 0.7 reshape.47
  129.2 6.8 %all-to-all-start.2 = ((bf16[64,2,640]{2,1,0:T(2,128)(2,1)}), bf16[64,2,640]{2,1,0:T(2,128)(2,1)S(1)}, u32[]{:S(2)}, u32[]{:S(2)}) async-start(bf16[64,2,640]{2,1,0:T(2,128)(2,1)} %reshape.47), calls=%async_computation.2 | async-start | bytes 327680 | tf_op jit(solution)/shard_map/all_to_all | solution.py:78
  136.0 0.0 all-gather.5.cloned.1.call-start
  136.0 1.3 copy.28
  137.4 17.8 %all-to-all-done.2 = bf16[64,2,640]{2,1,0:T(2,128)(2,1)S(1)} async-done(((bf16[64,2,640]{2,1,0:T(2,128)(2,1)}), bf16[64,2,640]{2,1,0:T(2,128)(2,1)S(1)}, u32[]{:S(2)}, u32[]{:S(2)}) %all-to-all-start.2) | async-done | bytes 163872 | tf_op jit(solution)/shard_map/all_to_all | solution.py:78
  155.2 0.7 reshape.48
  155.9 0.0 all-gather.5.cloned.1.call-update
  156.0 1.1 copy.26
  157.0 4.5 %all-to-all-start.3 = ((bf16[96,8,640]{2,0,1:T(8,128)(2,1)}), bf16[96,8,640]{2,0,1:T(8,128)(2,1)S(1)}, u32[]{:S(2)}, u32[]{:S(2)}) async-start(bf16[96,8,640]{2,0,1:T(8,128)(2,1)} %copy.26), calls=%async_computation.3 | async-start | bytes 1966080 | tf_op jit(solution)/shard_map/all_to_all | solution.py:83
  161.6 17.1 %all-gather.5.cloned.1.call-done = bf16[128,5120]{1,0:T(8,128)(2,1)} async-done(((bf16[128,640]{1,0:T(8,128)(2,1)}), bf16[128,5120]{1,0:T(8,128)(2,1)}) %all-gather.5.cloned.1.call-update) | async-done | bytes 1310736 | tf_op jit(solution)/shard_map/all_gather | solution.py:85
  178.6 0.0 copy-done
  178.6 2.0 fusion.1
  180.6 0.0 copy-start.3
  180.7 12.8 %all_gather.11 = bf16[128,768]{0,1:T(8,128)(2,1)S(1)} all-gather(bf16[128,96]{0,1:T(8,128)(2,1)S(1)} %fusion.12), channel_id=1, replica_groups=mesh['head'=8,'ez'=16,'ey'=4] {'head'}, dimensions={1}, use_global_device_ids=true | all-gather | bytes 221184 | tf_op jit(solution)/shard_map/all_gather | solution.py:88
  193.5 0.0 all-to-all-done.3
  193.5 0.3 convolution_convert_fusion
  193.8 0.7 reshape.50
  194.5 12.8 %all-to-all-start.4 = ((bf16[64,2,640]{2,1,0:T(2,128)(2,1)}), bf16[64,2,640]{2,1,0:T(2,128)(2,1)S(1)}, u32[]{:S(2)}, u32[]{:S(2)}) async-start(bf16[64,2,640]{2,1,0:T(2,128)(2,1)} %reshape.50), calls=%async_computation.4 | async-start | bytes 327680 | tf_op jit(solution)/shard_map/all_to_all | solution.py:91
  207.3 0.0 copy-done.3
  207.3 0.1 copy.25
  207.4 0.1 select_reduce_fusion
  207.5 19.3 %all-to-all-done.4 = bf16[64,2,640]{2,1,0:T(2,128)(2,1)S(1)} async-done(((bf16[64,2,640]{2,1,0:T(2,128)(2,1)}), bf16[64,2,640]{2,1,0:T(2,128)(2,1)S(1)}, u32[]{:S(2)}, u32[]{:S(2)}) %all-to-all-start.4) | async-done | bytes 163872 | tf_op jit(solution)/shard_map/all_to_all | solution.py:91
  226.8 0.1 reshape.51
  226.9 0.8 convolution_add_fusion.1
  (6 shorter events, 0.1 us)
Async XLA Ops:
  6.5 172.1 %copy-start = (bf16[1,2,96,5120]{3,2,1,0:T(8,128)(2,1)S(1)}, bf16[1,2,96,5120]{3,2,1,0:T(8,128)(2,1)}, u32[]{:S(2)}) copy-start(bf16[1,2,96,5120]{3,2,1,0:T(8,128)(2,1)} %param.22) | copy-start | bytes 5898244
  11.1 17.1 %copy-start.2 = (s32[8,6]{1,0:T(8,128)S(1)}, s32[8,6]{1,0:T(8,128)}, u32[]{:S(2)}) copy-start(s32[8,6]{1,0:T(8,128)} %param.20) | copy-start | bytes 580
  12.2 65.2 %all-to-all-start = ((bf16[16,8,4096]{2,1,0:T(8,128)(2,1)}), bf16[16,8,4096]{2,1,0:T(8,128)(2,1)S(1)}, u32[]{:S(2)}, u32[]{:S(2)}) async-start(bf16[16,8,4096]{2,1,0:T(8,128)(2,1)} %broadcast_in_dim.33), calls=%async_computation | async-start | bytes 2097152 | tf_op jit(solution)/shard_map/all_to_all | solution.py:47
  27.4 50.0 %all-gather.3.cloned.1.call-start = ((), (), s32[]{:S(2)}) async-start(), calls=%async_computation.5 | async-start | bytes 3276800 | tf_op jit(solution)/shard_map/all_gather | solution.py:49
  28.7 99.3 %copy-start.1 = (bf16[8,5120]{1,0:T(8,128)(2,1)S(1)}, bf16[8,5120]{1,0:T(8,128)(2,1)}, u32[]{:S(2)}) copy-start(bf16[8,5120]{1,0:T(8,128)(2,1)} %param.18) | copy-start | bytes 245764
  102.7 25.1 %all-to-all-start.1 = ((bf16[16,8,320]{2,1,0:T(8,128)(2,1)}), bf16[16,8,320]{2,1,0:T(8,128)(2,1)S(1)}, u32[]{:S(2)}, u32[]{:S(2)}) async-start(bf16[16,8,320]{2,1,0:T(8,128)(2,1)} %bitcast.1), calls=%async_computation.1 | async-start | bytes 196608 | tf_op jit(solution)/shard_map/all_to_all | solution.py:52
  129.2 26.0 %all-to-all-start.2 = ((bf16[64,2,640]{2,1,0:T(2,128)(2,1)}), bf16[64,2,640]{2,1,0:T(2,128)(2,1)S(1)}, u32[]{:S(2)}, u32[]{:S(2)}) async-start(bf16[64,2,640]{2,1,0:T(2,128)(2,1)} %reshape.47), calls=%async_computation.2 | async-start | bytes 327680 | tf_op jit(solution)/shard_map/all_to_all | solution.py:78
  136.0 42.6 %all-gather.5.cloned.1.call-start = ((), (), s32[]{:S(2)}) async-start(), calls=%async_computation.6 | async-start | bytes 1474560 | tf_op jit(solution)/shard_map/all_gather | solution.py:85
  157.0 36.4 %all-to-all-start.3 = ((bf16[96,8,640]{2,0,1:T(8,128)(2,1)}), bf16[96,8,640]{2,0,1:T(8,128)(2,1)S(1)}, u32[]{:S(2)}, u32[]{:S(2)}) async-start(bf16[96,8,640]{2,0,1:T(8,128)(2,1)} %copy.26), calls=%async_computation.3 | async-start | bytes 1966080 | tf_op jit(solution)/shard_map/all_to_all | solution.py:83
  180.6 26.7 %copy-start.3 = (f32[8,6]{1,0:T(8,128)S(1)}, f32[8,6]{1,0:T(8,128)}, u32[]{:S(2)}) copy-start(f32[8,6]{1,0:T(8,128)} %param.21) | copy-start | bytes 580
  194.5 32.3 %all-to-all-start.4 = ((bf16[64,2,640]{2,1,0:T(2,128)(2,1)}), bf16[64,2,640]{2,1,0:T(2,128)(2,1)S(1)}, u32[]{:S(2)}, u32[]{:S(2)}) async-start(bf16[64,2,640]{2,1,0:T(2,128)(2,1)} %reshape.50), calls=%async_computation.4 | async-start | bytes 327680 | tf_op jit(solution)/shard_map/all_to_all | solution.py:91
Sparse Core Ops, SparseCore 0:
  30.4 44.1 all-gather.2
  156.1 22.4 all-gather.4

commit v8 on v7

--- a/solution.py
+++ b/solution.py
@@ -43,11 +43,23 @@
     latent_out = attend(q_latent, q_rotary, cache_latent, cache_rotary, lengths)
     flattened = latent_out.reshape(seq_local, -1)
     z_count = lax.axis_size("ez")
-    latent_copies = jnp.broadcast_to(flattened[None], (z_count,) + flattened.shape)
-    gathered = lax.all_to_all(latent_copies, "ez", split_axis=0, concat_axis=0, tiled=True)
-    gathered = gathered.reshape(-1, flattened.shape[1])
+    forward = [(i, (i + 1) % z_count) for i in range(z_count)]
+    backward = [(i, (i - 1) % z_count) for i in range(z_count)]
+    ahead, behind = [], []
+    moving_fwd, moving_bwd = flattened, flattened
+    for step in range(1, z_count // 2 + 1):
+        moving_fwd = lax.ppermute(moving_fwd, "ez", forward)
+        behind.append(moving_fwd)
+        if step < z_count - step:
+            moving_bwd = lax.ppermute(moving_bwd, "ez", backward)
+            ahead.append(moving_bwd)
+    relative = [flattened] + ahead + behind[len(ahead):] + behind[: len(ahead)][::-1]
+    gathered = jnp.concatenate(relative, axis=0)
     value_cols = lax.all_gather(w_value_out, "ey", axis=1, tiled=True)
     column_terms = jnp.dot(gathered, value_cols, preferred_element_type=jnp.float32)
+    column_terms = column_terms.reshape(z_count, seq_local, -1)
+    column_terms = jnp.roll(column_terms, lax.axis_index("ez"), axis=0)
+    column_terms = column_terms.reshape(z_count * seq_local, -1)
     column_sums = lax.psum(column_terms, "head")
     attention = lax.all_to_all(
         column_sums.astype(jnp.bfloat16), "ez", split_axis=0, concat_axis=1, tiled=True

time: 236 us -> 237 us (level)
  starting transfers between devices: 50.9 us -> 90.2 us
  waiting for transfers between devices: 116 us -> 78.1 us
    ppermute x0 -> x15, starting transfers between devices: none -> 58.8 us  [the longest x7 43.5 us: on_device(): moving_bwd = lax.ppermute(moving_bwd, 'ez', backward)]
    all_to_all x1 -> x0, waiting for transfers between devices: 48.7 us -> none  [on_device(): lax.all_to_all(latent_copies, 'ez', split_axis=0, concat_axis=0, tiled=True)]
    all_to_all x1 -> x0, starting transfers between devices: 15.2 us -> none  [on_device(): lax.all_to_all(latent_copies, 'ez', split_axis=0, concat_axis=0, tiled=True)]
    ppermute x0 -> x15, waiting for transfers between devices: none -> 11.4 us  [the longest x8 11.4 us: on_device(): moving_fwd = lax.ppermute(moving_fwd, 'ez', forward)]
    all_to_all x1, starting transfers between devices: 11.6 us -> 5.4 us  [on_device(): lax.all_to_all(column_sums.astype(jnp.bfloat16), 'ez', split_axis=0, conc...]
  transfers between devices with their start and end apart: 7 -> 21, of which waited for: 5 -> 6; matrix products, arithmetic and copies ran while one was open for 3% -> 3% of each run, Pallas kernels for 0% -> 0%
where the time goes in v8:
time: 237 us; the launch traced here: 235 us
  starting transfers between devices  90.2 us (38%)
  waiting for transfers between devices  78.1 us (33%)
  blocking collectives  35.7 us (15%)
  between operations  13.9 us (6%)
  matrix products  10.6 us (4%)
  local copies, waits for them, and re-layouts  6.06 us (3%)
    ppermute x7, starting transfers between devices, on_device(): moving_bwd = lax.ppermute(moving_bwd, 'ez', backward)  43.5 us
    psum x1, blocking collectives, on_device(): column_sums = lax.psum(column_terms, 'head')  22.9 us
    all_to_all x1, waiting for transfers between devices, on_device(): lax.all_to_all(summed_rows, EXPERT, split_axis=0, concat_axis=0, tiled=True)  19.3 us
    all_to_all x1, waiting for transfers between devices, on_device(): lax.all_to_all(outgoing, EXPERT, split_axis=0, concat_axis=0, tiled=True)  17.8 us
    all_gather x1, waiting for transfers between devices, on_device(): flat_rows = lax.all_gather(arrived_cols, 'head', axis=1, tiled=True)  17.1 us
    ppermute x8, starting transfers between devices, on_device(): moving_fwd = lax.ppermute(moving_fwd, 'ez', forward)  15.3 us
    all_to_all x1, starting transfers between devices, on_device(): lax.all_to_all(summed_rows, EXPERT, split_axis=0, concat_axis=0, tiled=True)  12.8 us
    all_gather x1, blocking collectives, on_device(): hidden_all = lax.all_gather(hidden, 'head', axis=1, tiled=True)  12.8 us
  transfers between devices with their start and end apart: 21, of which 6 were waited for; matrix products, arithmetic and copies ran while one was open for 3% of the time, Pallas kernels for 0%

profile of v8, /device:TPU:6, one launch (start us, length us, event | category | flops | bytes accessed | tf_op | source)
XLA Modules:
  0.0 235.4 jit_solution(239215114262492398)
XLA Ops:
  6.5 1.8 fusion.20
  8.3 1.1 fusion.8
  9.4 0.2 fusion.19
  9.6 1.5 fusion.4
  11.1 11.4 %collective-permute-start = (bf16[8,4096]{1,0:T(8,128)(2,1)S(1)}, bf16[8,4096]{1,0:T(8,128)(2,1)S(1)}, u32[]{:S(2)}, u32[]{:S(2)}) collective-permute-start(bf16[8,4096]{1,0:T(8,128)(2,1)S(1)} %bitcast.52), channel_id=1, source_target_pairs={{0,60},{4,0},{8,4},{12,8},{16,12},{20,16},{24,20},{28,24},{32,28},... | collective-permute-start | bytes 196616 | tf_op jit(solution)/shard_map/ppermute | solution.py:54
  22.5 1.9 collective-permute-start.7
  24.5 0.0 all-gather.3.cloned.1.call-update
  24.6 0.1 eq.31
  24.6 0.1 fusion.13
  24.7 0.1 reduce_window_sum.11
  24.8 0.2 select_reduce_fusion.1
  25.0 0.1 reduce_sum.49
  25.0 5.1 %collective-permute-start.1 = (bf16[8,4096]{1,0:T(8,128)(2,1)S(1)}, bf16[8,4096]{1,0:T(8,128)(2,1)S(1)}, u32[]{:S(2)}, u32[]{:S(2)}) collective-permute-start(bf16[8,4096]{1,0:T(8,128)(2,1)S(1)} %collective-permute-done), channel_id=1, source_target_pairs={{0,60},{4,0},{8,4},{12,8},{16,12},{20,16},{24,20},{28,24},{32,28},... | collective-permute-start | bytes 196616 | tf_op jit(solution)/shard_map/ppermute | solution.py:54
  30.2 1.9 collective-permute-start.8
  32.2 5.4 %collective-permute-start.2 = (bf16[8,4096]{1,0:T(8,128)(2,1)S(1)}, bf16[8,4096]{1,0:T(8,128)(2,1)S(1)}, u32[]{:S(2)}, u32[]{:S(2)}) collective-permute-start(bf16[8,4096]{1,0:T(8,128)(2,1)S(1)} %collective-permute-done.1), channel_id=1, source_target_pairs={{0,60},{4,0},{8,4},{12,8},{16,12},{20,16},{24,20},{28,24},{32,28},... | collective-permute-start | bytes 196616 | tf_op jit(solution)/shard_map/ppermute | solution.py:54
  37.6 0.0 collective-permute-done.8
  37.6 1.9 collective-permute-start.9
  39.5 5.4 %collective-permute-start.3 = (bf16[8,4096]{1,0:T(8,128)(2,1)S(1)}, bf16[8,4096]{1,0:T(8,128)(2,1)S(1)}, u32[]{:S(2)}, u32[]{:S(2)}) collective-permute-start(bf16[8,4096]{1,0:T(8,128)(2,1)S(1)} %collective-permute-done.2), channel_id=1, source_target_pairs={{0,60},{4,0},{8,4},{12,8},{16,12},{20,16},{24,20},{28,24},{32,28},... | collective-permute-start | bytes 196616 | tf_op jit(solution)/shard_map/ppermute | solution.py:54
  44.9 0.0 collective-permute-done.9
  44.9 1.9 collective-permute-start.10
  46.9 5.4 %collective-permute-start.4 = (bf16[8,4096]{1,0:T(8,128)(2,1)S(1)}, bf16[8,4096]{1,0:T(8,128)(2,1)S(1)}, u32[]{:S(2)}, u32[]{:S(2)}) collective-permute-start(bf16[8,4096]{1,0:T(8,128)(2,1)S(1)} %collective-permute-done.3), channel_id=1, source_target_pairs={{0,60},{4,0},{8,4},{12,8},{16,12},{20,16},{24,20},{28,24},{32,28},... | collective-permute-start | bytes 196616 | tf_op jit(solution)/shard_map/ppermute | solution.py:54
  52.3 0.0 collective-permute-done.10
  52.3 1.9 collective-permute-start.11
  54.2 5.4 %collective-permute-start.5 = (bf16[8,4096]{1,0:T(8,128)(2,1)S(1)}, bf16[8,4096]{1,0:T(8,128)(2,1)S(1)}, u32[]{:S(2)}, u32[]{:S(2)}) collective-permute-start(bf16[8,4096]{1,0:T(8,128)(2,1)S(1)} %collective-permute-done.4), channel_id=1, source_target_pairs={{0,60},{4,0},{8,4},{12,8},{16,12},{20,16},{24,20},{28,24},{32,28},... | collective-permute-start | bytes 196616 | tf_op jit(solution)/shard_map/ppermute | solution.py:54
  59.6 0.0 collective-permute-done.11
  59.7 1.9 collective-permute-start.12
  61.6 5.4 %collective-permute-start.6 = (bf16[8,4096]{1,0:T(8,128)(2,1)S(1)}, bf16[8,4096]{1,0:T(8,128)(2,1)S(1)}, u32[]{:S(2)}, u32[]{:S(2)}) collective-permute-start(bf16[8,4096]{1,0:T(8,128)(2,1)S(1)} %collective-permute-done.5), channel_id=1, source_target_pairs={{0,60},{4,0},{8,4},{12,8},{16,12},{20,16},{24,20},{28,24},{32,28},... | collective-permute-start | bytes 196616 | tf_op jit(solution)/shard_map/ppermute | solution.py:54
  67.0 0.0 collective-permute-done.12
  67.0 1.9 collective-permute-start.13
  68.9 5.9 %collective-permute-done.13 = bf16[8,4096]{1,0:T(8,128)(2,1)S(1)} collective-permute-done((bf16[8,4096]{1,0:T(8,128)(2,1)S(1)}, bf16[8,4096]{1,0:T(8,128)(2,1)S(1)}, u32[]{:S(2)}, u32[]{:S(2)}) %collective-permute-start.13) | collective-permute-done | bytes 65568 | tf_op jit(solution)/shard_map/ppermute | solution.py:51
  74.8 1.9 collective-permute-start.14
  76.7 5.4 %collective-permute-done.14 = bf16[8,4096]{1,0:T(8,128)(2,1)S(1)} collective-permute-done((bf16[8,4096]{1,0:T(8,128)(2,1)S(1)}, bf16[8,4096]{1,0:T(8,128)(2,1)S(1)}, u32[]{:S(2)}, u32[]{:S(2)}) %collective-permute-start.14) | collective-permute-done | bytes 65568 | tf_op jit(solution)/shard_map/ppermute | solution.py:51
  82.3 0.0 all-gather.3.cloned.1.call-done
  82.3 2.8 %convolution_bitcast_fusion = f32[16,8,320]{2,1,0:T(8,128)S(1)} fusion(bf16[128,4096]{1,0:T(8,128)(2,1)S(1)} %constant_dynamic-update-slice_fusion, bf16[4096,320]{0,1:T(8,128)(2,1)} %all-gather.3.cloned.1.call-done), kind=kOutput, calls=%fused_computation.6 | convolution fusion | flops 335544320 | bytes 3833856 | tf_op jit(solution)/shard_map/dot_general | solution.py:59
  85.1 0.1 fusion.10
  85.2 22.9 %all-reduce.1 = bf16[128,320]{1,0:T(8,128)(2,1)} all-reduce(f32[128,320]{1,0:T(8,128)S(1)} %fusion.10), channel_id=1, replica_groups=mesh['head'=8,'ez'=16,'ey'=4] {'head'}, use_global_device_ids=true, to_apply=%region_2.3 | all-reduce | flops 40960 | bytes 245760 | tf_op jit(solution)/shard_map/psum | solution.py:63
  108.1 5.4 %all-to-all-start = ((bf16[16,8,320]{2,1,0:T(8,128)(2,1)}), bf16[16,8,320]{2,1,0:T(8,128)(2,1)S(1)}, u32[]{:S(2)}, u32[]{:S(2)}) async-start(bf16[16,8,320]{2,1,0:T(8,128)(2,1)} %bitcast.35), calls=%async_computation | async-start | bytes 196608 | tf_op jit(solution)/shard_map/all_to_all | solution.py:64
  113.5 0.1 copy.23
  113.6 0.8 dynamic-slice
  114.3 0.1 convert_reduce_fusion
  114.4 12.5 %all-to-all-done = bf16[16,8,320]{2,1,0:T(8,128)(2,1)S(1)} async-done(((bf16[16,8,320]{2,1,0:T(8,128)(2,1)}), bf16[16,8,320]{2,1,0:T(8,128)(2,1)S(1)}, u32[]{:S(2)}, u32[]{:S(2)}) %all-to-all-start) | async-done | bytes 81952 | tf_op jit(solution)/shard_map/all_to_all | solution.py:64
  126.9 0.1 reshape.59
  127.1 0.2 multiply_reduce_fusion
  127.2 0.3 convolution_convert_fusion.1
  127.5 0.7 reshape.54
  128.3 8.6 %all-to-all-start.1 = ((bf16[64,2,640]{2,1,0:T(2,128)(2,1)}), bf16[64,2,640]{2,1,0:T(2,128)(2,1)S(1)}, u32[]{:S(2)}, u32[]{:S(2)}) async-start(bf16[64,2,640]{2,1,0:T(2,128)(2,1)} %reshape.54), calls=%async_computation.1 | async-start | bytes 327680 | tf_op jit(solution)/shard_map/all_to_all | solution.py:90
  136.9 0.0 all-gather.5.cloned.1.call-start
  136.9 1.3 copy.28
  138.3 17.8 %all-to-all-done.1 = bf16[64,2,640]{2,1,0:T(2,128)(2,1)S(1)} async-done(((bf16[64,2,640]{2,1,0:T(2,128)(2,1)}), bf16[64,2,640]{2,1,0:T(2,128)(2,1)S(1)}, u32[]{:S(2)}, u32[]{:S(2)}) %all-to-all-start.1) | async-done | bytes 163872 | tf_op jit(solution)/shard_map/all_to_all | solution.py:90
  156.1 0.7 reshape.55
  156.8 0.0 all-gather.5.cloned.1.call-update
  156.8 1.1 copy.25
  157.9 4.5 %all-to-all-start.2 = ((bf16[96,8,640]{2,0,1:T(8,128)(2,1)}), bf16[96,8,640]{2,0,1:T(8,128)(2,1)S(1)}, u32[]{:S(2)}, u32[]{:S(2)}) async-start(bf16[96,8,640]{2,0,1:T(8,128)(2,1)} %copy.25), calls=%async_computation.2 | async-start | bytes 1966080 | tf_op jit(solution)/shard_map/all_to_all | solution.py:95
  162.4 17.1 %all-gather.5.cloned.1.call-done = bf16[128,5120]{1,0:T(8,128)(2,1)} async-done(((bf16[128,640]{1,0:T(8,128)(2,1)}), bf16[128,5120]{1,0:T(8,128)(2,1)}) %all-gather.5.cloned.1.call-update) | async-done | bytes 1310736 | tf_op jit(solution)/shard_map/all_gather | solution.py:97
  179.5 2.0 fusion.1
  181.5 12.8 %all_gather.11 = bf16[128,768]{0,1:T(8,128)(2,1)S(1)} all-gather(bf16[128,96]{0,1:T(8,128)(2,1)S(1)} %fusion.12), channel_id=1, replica_groups=mesh['head'=8,'ez'=16,'ey'=4] {'head'}, dimensions={1}, use_global_device_ids=true | all-gather | bytes 221184 | tf_op jit(solution)/shard_map/all_gather | solution.py:100
  194.3 0.3 convolution_convert_fusion
  194.7 0.7 reshape.57
  195.4 12.8 %all-to-all-start.3 = ((bf16[64,2,640]{2,1,0:T(2,128)(2,1)}), bf16[64,2,640]{2,1,0:T(2,128)(2,1)S(1)}, u32[]{:S(2)}, u32[]{:S(2)}) async-start(bf16[64,2,640]{2,1,0:T(2,128)(2,1)} %reshape.57), calls=%async_computation.3 | async-start | bytes 327680 | tf_op jit(solution)/shard_map/all_to_all | solution.py:103
  208.2 0.1 copy.24
  208.3 0.1 select_reduce_fusion
  208.4 19.3 %all-to-all-done.3 = bf16[64,2,640]{2,1,0:T(2,128)(2,1)S(1)} async-done(((bf16[64,2,640]{2,1,0:T(2,128)(2,1)}), bf16[64,2,640]{2,1,0:T(2,128)(2,1)S(1)}, u32[]{:S(2)}, u32[]{:S(2)}) %all-to-all-start.3) | async-done | bytes 163872 | tf_op jit(solution)/shard_map/all_to_all | solution.py:103
  227.7 0.1 reshape.58
  227.8 0.8 convolution_add_fusion.1
  (40 shorter events, 0.3 us)
Async XLA Ops:
  6.5 172.9 %copy-start = (bf16[1,2,96,5120]{3,2,1,0:T(8,128)(2,1)S(1)}, bf16[1,2,96,5120]{3,2,1,0:T(8,128)(2,1)}, u32[]{:S(2)}) copy-start(bf16[1,2,96,5120]{3,2,1,0:T(8,128)(2,1)} %param.22) | copy-start | bytes 5898244
  6.5 18.0 %copy-start.2 = (s32[8,6]{1,0:T(8,128)S(1)}, s32[8,6]{1,0:T(8,128)}, u32[]{:S(2)}) copy-start(s32[8,6]{1,0:T(8,128)} %param.20) | copy-start | bytes 580
  6.5 75.8 %all-gather.3.cloned.1.call-start = ((), (), s32[]{:S(2)}) async-start(), calls=%async_computation.4 | async-start | bytes 3276800 | tf_op jit(solution)/shard_map/all_gather | solution.py:58
  11.1 13.9 %collective-permute-start = (bf16[8,4096]{1,0:T(8,128)(2,1)S(1)}, bf16[8,4096]{1,0:T(8,128)(2,1)S(1)}, u32[]{:S(2)}, u32[]{:S(2)}) collective-permute-start(bf16[8,4096]{1,0:T(8,128)(2,1)S(1)} %bitcast.52), channel_id=1, source_target_pairs={{0,60},{4,0},{8,4},{12,8},{16,12},{20,16},{24,20},{28,24},{32,28},... | collective-permute-start | bytes 196616 | tf_op jit(solution)/shard_map/ppermute | solution.py:54
  22.5 7.7 %collective-permute-start.7 = (bf16[8,4096]{1,0:T(8,128)(2,1)S(1)}, bf16[8,4096]{1,0:T(8,128)(2,1)S(1)}, u32[]{:S(2)}, u32[]{:S(2)}) collective-permute-start(bf16[8,4096]{1,0:T(8,128)(2,1)S(1)} %bitcast.53), channel_id=1, source_target_pairs={{0,4},{4,8},{8,12},{12,16},{16,20},{20,24},{24,28},{28,32},{32,36}... | collective-permute-start | bytes 196616 | tf_op jit(solution)/shard_map/ppermute | solution.py:51
  25.0 7.1 %collective-permute-start.1 = (bf16[8,4096]{1,0:T(8,128)(2,1)S(1)}, bf16[8,4096]{1,0:T(8,128)(2,1)S(1)}, u32[]{:S(2)}, u32[]{:S(2)}) collective-permute-start(bf16[8,4096]{1,0:T(8,128)(2,1)S(1)} %collective-permute-done), channel_id=1, source_target_pairs={{0,60},{4,0},{8,4},{12,8},{16,12},{20,16},{24,20},{28,24},{32,28},... | collective-permute-start | bytes 196616 | tf_op jit(solution)/shard_map/ppermute | solution.py:54
  30.2 7.4 %collective-permute-start.8 = (bf16[8,4096]{1,0:T(8,128)(2,1)S(1)}, bf16[8,4096]{1,0:T(8,128)(2,1)S(1)}, u32[]{:S(2)}, u32[]{:S(2)}) collective-permute-start(bf16[8,4096]{1,0:T(8,128)(2,1)S(1)} %collective-permute-done.7), channel_id=1, source_target_pairs={{0,4},{4,8},{8,12},{12,16},{16,20},{20,24},{24,28},{28,32},{32,36}... | collective-permute-start | bytes 196616 | tf_op jit(solution)/shard_map/ppermute | solution.py:51
  32.2 7.4 %collective-permute-start.2 = (bf16[8,4096]{1,0:T(8,128)(2,1)S(1)}, bf16[8,4096]{1,0:T(8,128)(2,1)S(1)}, u32[]{:S(2)}, u32[]{:S(2)}) collective-permute-start(bf16[8,4096]{1,0:T(8,128)(2,1)S(1)} %collective-permute-done.1), channel_id=1, source_target_pairs={{0,60},{4,0},{8,4},{12,8},{16,12},{20,16},{24,20},{28,24},{32,28},... | collective-permute-start | bytes 196616 | tf_op jit(solution)/shard_map/ppermute | solution.py:54
  37.6 7.4 %collective-permute-start.9 = (bf16[8,4096]{1,0:T(8,128)(2,1)S(1)}, bf16[8,4096]{1,0:T(8,128)(2,1)S(1)}, u32[]{:S(2)}, u32[]{:S(2)}) collective-permute-start(bf16[8,4096]{1,0:T(8,128)(2,1)S(1)} %collective-permute-done.8), channel_id=1, source_target_pairs={{0,4},{4,8},{8,12},{12,16},{16,20},{20,24},{24,28},{28,32},{32,36}... | collective-permute-start | bytes 196616 | tf_op jit(solution)/shard_map/ppermute | solution.py:51
  39.5 7.4 %collective-permute-start.3 = (bf16[8,4096]{1,0:T(8,128)(2,1)S(1)}, bf16[8,4096]{1,0:T(8,128)(2,1)S(1)}, u32[]{:S(2)}, u32[]{:S(2)}) collective-permute-start(bf16[8,4096]{1,0:T(8,128)(2,1)S(1)} %collective-permute-done.2), channel_id=1, source_target_pairs={{0,60},{4,0},{8,4},{12,8},{16,12},{20,16},{24,20},{28,24},{32,28},... | collective-permute-start | bytes 196616 | tf_op jit(solution)/shard_map/ppermute | solution.py:54
  44.9 7.4 %collective-permute-start.10 = (bf16[8,4096]{1,0:T(8,128)(2,1)S(1)}, bf16[8,4096]{1,0:T(8,128)(2,1)S(1)}, u32[]{:S(2)}, u32[]{:S(2)}) collective-permute-start(bf16[8,4096]{1,0:T(8,128)(2,1)S(1)} %collective-permute-done.9), channel_id=1, source_target_pairs={{0,4},{4,8},{8,12},{12,16},{16,20},{20,24},{24,28},{28,32},{32,36}... | collective-permute-start | bytes 196616 | tf_op jit(solution)/shard_map/ppermute | solution.py:51
  46.9 7.4 %collective-permute-start.4 = (bf16[8,4096]{1,0:T(8,128)(2,1)S(1)}, bf16[8,4096]{1,0:T(8,128)(2,1)S(1)}, u32[]{:S(2)}, u32[]{:S(2)}) collective-permute-start(bf16[8,4096]{1,0:T(8,128)(2,1)S(1)} %collective-permute-done.3), channel_id=1, source_target_pairs={{0,60},{4,0},{8,4},{12,8},{16,12},{20,16},{24,20},{28,24},{32,28},... | collective-permute-start | bytes 196616 | tf_op jit(solution)/shard_map/ppermute | solution.py:54
  52.3 7.4 %collective-permute-start.11 = (bf16[8,4096]{1,0:T(8,128)(2,1)S(1)}, bf16[8,4096]{1,0:T(8,128)(2,1)S(1)}, u32[]{:S(2)}, u32[]{:S(2)}) collective-permute-start(bf16[8,4096]{1,0:T(8,128)(2,1)S(1)} %collective-permute-done.10), channel_id=1, source_target_pairs={{0,4},{4,8},{8,12},{12,16},{16,20},{20,24},{24,28},{28,32},{32,36}... | collective-permute-start | bytes 196616 | tf_op jit(solution)/shard_map/ppermute | solution.py:51
  54.2 7.4 %collective-permute-start.5 = (bf16[8,4096]{1,0:T(8,128)(2,1)S(1)}, bf16[8,4096]{1,0:T(8,128)(2,1)S(1)}, u32[]{:S(2)}, u32[]{:S(2)}) collective-permute-start(bf16[8,4096]{1,0:T(8,128)(2,1)S(1)} %collective-permute-done.4), channel_id=1, source_target_pairs={{0,60},{4,0},{8,4},{12,8},{16,12},{20,16},{24,20},{28,24},{32,28},... | collective-permute-start | bytes 196616 | tf_op jit(solution)/shard_map/ppermute | solution.py:54
  59.7 7.4 %collective-permute-start.12 = (bf16[8,4096]{1,0:T(8,128)(2,1)S(1)}, bf16[8,4096]{1,0:T(8,128)(2,1)S(1)}, u32[]{:S(2)}, u32[]{:S(2)}) collective-permute-start(bf16[8,4096]{1,0:T(8,128)(2,1)S(1)} %collective-permute-done.11), channel_id=1, source_target_pairs={{0,4},{4,8},{8,12},{12,16},{16,20},{20,24},{24,28},{28,32},{32,36}... | collective-permute-start | bytes 196616 | tf_op jit(solution)/shard_map/ppermute | solution.py:51
  61.6 15.1 %collective-permute-start.6 = (bf16[8,4096]{1,0:T(8,128)(2,1)S(1)}, bf16[8,4096]{1,0:T(8,128)(2,1)S(1)}, u32[]{:S(2)}, u32[]{:S(2)}) collective-permute-start(bf16[8,4096]{1,0:T(8,128)(2,1)S(1)} %collective-permute-done.5), channel_id=1, source_target_pairs={{0,60},{4,0},{8,4},{12,8},{16,12},{20,16},{24,20},{28,24},{32,28},... | collective-permute-start | bytes 196616 | tf_op jit(solution)/shard_map/ppermute | solution.py:54
  67.0 7.8 %collective-permute-start.13 = (bf16[8,4096]{1,0:T(8,128)(2,1)S(1)}, bf16[8,4096]{1,0:T(8,128)(2,1)S(1)}, u32[]{:S(2)}, u32[]{:S(2)}) collective-permute-start(bf16[8,4096]{1,0:T(8,128)(2,1)S(1)} %collective-permute-done.12), channel_id=1, source_target_pairs={{0,4},{4,8},{8,12},{12,16},{16,20},{20,24},{24,28},{28,32},{32,36}... | collective-permute-start | bytes 196616 | tf_op jit(solution)/shard_map/ppermute | solution.py:51
  74.8 7.4 %collective-permute-start.14 = (bf16[8,4096]{1,0:T(8,128)(2,1)S(1)}, bf16[8,4096]{1,0:T(8,128)(2,1)S(1)}, u32[]{:S(2)}, u32[]{:S(2)}) collective-permute-start(bf16[8,4096]{1,0:T(8,128)(2,1)S(1)} %collective-permute-done.13), channel_id=1, source_target_pairs={{0,4},{4,8},{8,12},{12,16},{16,20},{20,24},{24,28},{28,32},{32,36}... | collective-permute-start | bytes 196616 | tf_op jit(solution)/shard_map/ppermute | solution.py:51
  82.3 44.8 %copy-start.1 = (bf16[8,5120]{1,0:T(8,128)(2,1)S(1)}, bf16[8,5120]{1,0:T(8,128)(2,1)}, u32[]{:S(2)}) copy-start(bf16[8,5120]{1,0:T(8,128)(2,1)} %param.18) | copy-start | bytes 245764
  108.1 18.8 %all-to-all-start = ((bf16[16,8,320]{2,1,0:T(8,128)(2,1)}), bf16[16,8,320]{2,1,0:T(8,128)(2,1)S(1)}, u32[]{:S(2)}, u32[]{:S(2)}) async-start(bf16[16,8,320]{2,1,0:T(8,128)(2,1)} %bitcast.35), calls=%async_computation | async-start | bytes 196608 | tf_op jit(solution)/shard_map/all_to_all | solution.py:64
  128.3 27.8 %all-to-all-start.1 = ((bf16[64,2,640]{2,1,0:T(2,128)(2,1)}), bf16[64,2,640]{2,1,0:T(2,128)(2,1)S(1)}, u32[]{:S(2)}, u32[]{:S(2)}) async-start(bf16[64,2,640]{2,1,0:T(2,128)(2,1)} %reshape.54), calls=%async_computation.1 | async-start | bytes 327680 | tf_op jit(solution)/shard_map/all_to_all | solution.py:90
  136.9 42.6 %all-gather.5.cloned.1.call-start = ((), (), s32[]{:S(2)}) async-start(), calls=%async_computation.5 | async-start | bytes 1474560 | tf_op jit(solution)/shard_map/all_gather | solution.py:97
  157.9 36.4 %all-to-all-start.2 = ((bf16[96,8,640]{2,0,1:T(8,128)(2,1)}), bf16[96,8,640]{2,0,1:T(8,128)(2,1)S(1)}, u32[]{:S(2)}, u32[]{:S(2)}) async-start(bf16[96,8,640]{2,0,1:T(8,128)(2,1)} %copy.25), calls=%async_computation.2 | async-start | bytes 1966080 | tf_op jit(solution)/shard_map/all_to_all | solution.py:95
  181.5 26.7 %copy-start.3 = (f32[8,6]{1,0:T(8,128)S(1)}, f32[8,6]{1,0:T(8,128)}, u32[]{:S(2)}) copy-start(f32[8,6]{1,0:T(8,128)} %param.21) | copy-start | bytes 580
  195.4 32.3 %all-to-all-start.3 = ((bf16[64,2,640]{2,1,0:T(2,128)(2,1)}), bf16[64,2,640]{2,1,0:T(2,128)(2,1)S(1)}, u32[]{:S(2)}, u32[]{:S(2)}) async-start(bf16[64,2,640]{2,1,0:T(2,128)(2,1)} %reshape.57), calls=%async_computation.3 | async-start | bytes 327680 | tf_op jit(solution)/shard_map/all_to_all | solution.py:103
Sparse Core Ops, SparseCore 0:
  24.6 39.8 all-gather.2
  157.0 22.4 all-gather.4

commit v9 on v8

--- a/solution.py
+++ b/solution.py
@@ -54,6 +54,7 @@
             moving_bwd = lax.ppermute(moving_bwd, "ez", backward)
             ahead.append(moving_bwd)
     relative = [flattened] + ahead + behind[len(ahead):] + behind[: len(ahead)][::-1]
+    relative = list(lax.optimization_barrier(tuple(relative)))
     gathered = jnp.concatenate(relative, axis=0)
     value_cols = lax.all_gather(w_value_out, "ey", axis=1, tiled=True)
     column_terms = jnp.dot(gathered, value_cols, preferred_element_type=jnp.float32)

time: 237 us -> 260 us (1.097)
  waiting for transfers between devices: 78.1 us -> 87.7 us
  local copies, waits for them, and re-layouts: 6.06 us -> 13.4 us
  starting transfers between devices: 90.2 us -> 94 us
    all_gather x1, waiting for transfers between devices: 0.02 us -> 14.6 us  [on_device(): value_cols = lax.all_gather(w_value_out, 'ey', axis=1, tiled=True)]
    unnamed x26 -> x40, local copies, waits for them, and re-layouts: 1.58 us -> 8.92 us
    all_to_all x1, starting transfers between devices: 5.4 us -> 12.3 us  [on_device(): lax.all_to_all(column_sums.astype(jnp.bfloat16), 'ez', split_axis=0, conc...]
    ppermute x8, waiting for transfers between devices: 11.4 us -> 6.38 us  [on_device(): moving_fwd = lax.ppermute(moving_fwd, 'ez', forward)]
    ppermute x7, starting transfers between devices: 43.5 us -> 40.3 us  [on_device(): moving_bwd = lax.ppermute(moving_bwd, 'ez', backward)]
  transfers between devices with their start and end apart: 21 -> 21, of which waited for: 6 -> 13; matrix products, arithmetic and copies ran while one was open for 3% -> 5% of each run, Pallas kernels for 0% -> 0%
where the time goes in v9:
time: 260 us; the launch traced here: 258 us
  starting transfers between devices  94 us (36%)
  waiting for transfers between devices  87.7 us (34%)
  blocking collectives  37.9 us (15%)
  between operations  13.8 us (5%)
  local copies, waits for them, and re-layouts  13.4 us (5%)
  matrix products  10.6 us (4%)
    ppermute x7, starting transfers between devices, on_device(): moving_bwd = lax.ppermute(moving_bwd, 'ez', backward)  40.3 us
    psum x1, blocking collectives, on_device(): column_sums = lax.psum(column_terms, 'head')  25.1 us
    all_to_all x1, waiting for transfers between devices, on_device(): lax.all_to_all(summed_rows, EXPERT, split_axis=0, concat_axis=0, tiled=True)  19.3 us
    all_to_all x1, waiting for transfers between devices, on_device(): lax.all_to_all(outgoing, EXPERT, split_axis=0, concat_axis=0, tiled=True)  17.8 us
    ppermute x8, starting transfers between devices, on_device(): moving_fwd = lax.ppermute(moving_fwd, 'ez', forward)  17.2 us
    all_gather x1, waiting for transfers between devices, on_device(): flat_rows = lax.all_gather(arrived_cols, 'head', axis=1, tiled=True)  17.1 us
    all_gather x1, waiting for transfers between devices, on_device(): value_cols = lax.all_gather(w_value_out, 'ey', axis=1, tiled=True)  14.6 us
    all_to_all x1, starting transfers between devices, on_device(): lax.all_to_all(summed_rows, EXPERT, split_axis=0, concat_axis=0, tiled=True)  12.8 us
  transfers between devices with their start and end apart: 21, of which 13 were waited for; matrix products, arithmetic and copies ran while one was open for 5% of the time, Pallas kernels for 0%

profile of v9, /device:TPU:6, one launch (start us, length us, event | category | flops | bytes accessed | tf_op | source)
XLA Modules:
  0.0 258.4 jit_solution(12614081506461023291)
XLA Ops:
  6.5 1.8 fusion.20
  8.3 1.1 fusion.8
  9.4 0.2 fusion.19
  9.6 1.5 fusion.4
  11.1 3.8 %collective-permute-start.7 = (bf16[8,4096]{1,0:T(8,128)(2,1)S(1)}, bf16[8,4096]{1,0:T(8,128)(2,1)S(1)}, u32[]{:S(2)}, u32[]{:S(2)}) collective-permute-start(bf16[8,4096]{1,0:T(8,128)(2,1)S(1)} %bitcast.52), channel_id=1, source_target_pairs={{0,4},{4,8},{8,12},{12,16},{16,20},{20,24},{24,28},{28,32},{32,36}... | collective-permute-start | bytes 196616 | tf_op jit(solution)/shard_map/ppermute | solution.py:51
  15.0 9.5 %collective-permute-start = (bf16[8,4096]{1,0:T(8,128)(2,1)S(1)}, bf16[8,4096]{1,0:T(8,128)(2,1)S(1)}, u32[]{:S(2)}, u32[]{:S(2)}) collective-permute-start(bf16[8,4096]{1,0:T(8,128)(2,1)S(1)} %bitcast.53), channel_id=1, source_target_pairs={{0,60},{4,0},{8,4},{12,8},{16,12},{20,16},{24,20},{28,24},{32,28},... | collective-permute-start | bytes 196616 | tf_op jit(solution)/shard_map/ppermute | solution.py:54
  24.5 0.3 collective-permute-done.7
  24.8 1.9 collective-permute-start.8
  26.7 5.1 %collective-permute-start.1 = (bf16[8,4096]{1,0:T(8,128)(2,1)S(1)}, bf16[8,4096]{1,0:T(8,128)(2,1)S(1)}, u32[]{:S(2)}, u32[]{:S(2)}) collective-permute-start(bf16[8,4096]{1,0:T(8,128)(2,1)S(1)} %collective-permute-done), channel_id=1, source_target_pairs={{0,60},{4,0},{8,4},{12,8},{16,12},{20,16},{24,20},{28,24},{32,28},... | collective-permute-start | bytes 196616 | tf_op jit(solution)/shard_map/ppermute | solution.py:54
  31.8 0.3 collective-permute-done.8
  32.1 1.9 collective-permute-start.9
  34.1 5.1 %collective-permute-start.2 = (bf16[8,4096]{1,0:T(8,128)(2,1)S(1)}, bf16[8,4096]{1,0:T(8,128)(2,1)S(1)}, u32[]{:S(2)}, u32[]{:S(2)}) collective-permute-start(bf16[8,4096]{1,0:T(8,128)(2,1)S(1)} %collective-permute-done.1), channel_id=1, source_target_pairs={{0,60},{4,0},{8,4},{12,8},{16,12},{20,16},{24,20},{28,24},{32,28},... | collective-permute-start | bytes 196616 | tf_op jit(solution)/shard_map/ppermute | solution.py:54
  39.2 0.3 collective-permute-done.9
  39.5 1.9 collective-permute-start.10
  41.4 5.1 %collective-permute-start.3 = (bf16[8,4096]{1,0:T(8,128)(2,1)S(1)}, bf16[8,4096]{1,0:T(8,128)(2,1)S(1)}, u32[]{:S(2)}, u32[]{:S(2)}) collective-permute-start(bf16[8,4096]{1,0:T(8,128)(2,1)S(1)} %collective-permute-done.2), channel_id=1, source_target_pairs={{0,60},{4,0},{8,4},{12,8},{16,12},{20,16},{24,20},{28,24},{32,28},... | collective-permute-start | bytes 196616 | tf_op jit(solution)/shard_map/ppermute | solution.py:54
  46.6 0.3 collective-permute-done.10
  46.8 1.9 collective-permute-start.11
  48.8 5.1 %collective-permute-start.4 = (bf16[8,4096]{1,0:T(8,128)(2,1)S(1)}, bf16[8,4096]{1,0:T(8,128)(2,1)S(1)}, u32[]{:S(2)}, u32[]{:S(2)}) collective-permute-start(bf16[8,4096]{1,0:T(8,128)(2,1)S(1)} %collective-permute-done.3), channel_id=1, source_target_pairs={{0,60},{4,0},{8,4},{12,8},{16,12},{20,16},{24,20},{28,24},{32,28},... | collective-permute-start | bytes 196616 | tf_op jit(solution)/shard_map/ppermute | solution.py:54
  53.9 0.3 collective-permute-done.11
  54.2 1.9 collective-permute-start.12
  56.3 5.1 %collective-permute-start.5 = (bf16[8,4096]{1,0:T(8,128)(2,1)S(1)}, bf16[8,4096]{1,0:T(8,128)(2,1)S(1)}, u32[]{:S(2)}, u32[]{:S(2)}) collective-permute-start(bf16[8,4096]{1,0:T(8,128)(2,1)S(1)} %collective-permute-done.4), channel_id=1, source_target_pairs={{0,60},{4,0},{8,4},{12,8},{16,12},{20,16},{24,20},{28,24},{32,28},... | collective-permute-start | bytes 196616 | tf_op jit(solution)/shard_map/ppermute | solution.py:54
  61.4 0.2 collective-permute-done.12
  61.6 1.9 collective-permute-start.13
  63.7 5.1 %collective-permute-start.6 = (bf16[8,4096]{1,0:T(8,128)(2,1)S(1)}, bf16[8,4096]{1,0:T(8,128)(2,1)S(1)}, u32[]{:S(2)}, u32[]{:S(2)}) collective-permute-start(bf16[8,4096]{1,0:T(8,128)(2,1)S(1)} %collective-permute-done.5), channel_id=1, source_target_pairs={{0,60},{4,0},{8,4},{12,8},{16,12},{20,16},{24,20},{28,24},{32,28},... | collective-permute-start | bytes 196616 | tf_op jit(solution)/shard_map/ppermute | solution.py:54
  68.8 0.1 collective-permute-done.13
  68.9 1.9 collective-permute-start.14
  70.9 0.2 select_reduce_fusion.1
  71.2 0.6 copy-done.8
  71.8 4.6 %collective-permute-done.14 = bf16[8,4096]{1,0:T(8,128)(2,1)} collective-permute-done((bf16[8,4096]{1,0:T(8,128)(2,1)S(1)}, bf16[8,4096]{1,0:T(8,128)(2,1)}, u32[]{:S(2)}, u32[]{:S(2)}) %collective-permute-start.14) | collective-permute-done | bytes 65568 | tf_op jit(solution)/shard_map/ppermute | solution.py:51
  76.4 0.8 constant_dynamic-update-slice_fusion.12
  77.3 0.8 constant_dynamic-update-slice_fusion.11
  78.1 0.8 constant_dynamic-update-slice_fusion.10
  79.0 0.8 constant_dynamic-update-slice_fusion.9
  79.8 0.8 constant_dynamic-update-slice_fusion.8
  80.7 0.8 constant_dynamic-update-slice_fusion.7
  81.5 0.8 constant_dynamic-update-slice_fusion.6
  82.3 0.8 constant_dynamic-update-slice_fusion.5
  83.3 14.6 %all-gather.3.cloned.1.call-done = bf16[4096,320]{0,1:T(8,128)(2,1)} async-done(((bf16[4096,80]{0,1:T(8,128)(2,1)}), bf16[4096,320]{0,1:T(8,128)(2,1)}) %all-gather.3.cloned.1.call-update) | async-done | bytes 2621456 | tf_op jit(solution)/shard_map/all_gather | solution.py:59
  97.9 2.8 %convolution_bitcast_fusion = f32[16,8,320]{2,1,0:T(8,128)S(1)} fusion(bf16[128,4096]{1,0:T(8,128)(2,1)S(1)} %constant_dynamic-update-slice_fusion, bf16[4096,320]{0,1:T(8,128)(2,1)} %all-gather.3.cloned.1.call-done), kind=kOutput, calls=%fused_computation.6 | convolution fusion | flops 335544320 | bytes 3833856 | tf_op jit(solution)/shard_map/dot_general | solution.py:60
  100.8 25.1 %all-reduce.1 = bf16[128,320]{1,0:T(8,128)(2,1)} all-reduce(f32[128,320]{1,0:T(8,128)S(1)} %fusion.10), channel_id=1, replica_groups=mesh['head'=8,'ez'=16,'ey'=4] {'head'}, use_global_device_ids=true, to_apply=%region_2.3 | all-reduce | flops 40960 | bytes 245760 | tf_op jit(solution)/shard_map/psum | solution.py:64
  125.9 12.3 %all-to-all-start = ((bf16[16,8,320]{2,1,0:T(8,128)(2,1)}), bf16[16,8,320]{2,1,0:T(8,128)(2,1)S(1)}, u32[]{:S(2)}, u32[]{:S(2)}) async-start(bf16[16,8,320]{2,1,0:T(8,128)(2,1)} %bitcast.35), calls=%async_computation | async-start | bytes 196608 | tf_op jit(solution)/shard_map/all_to_all | solution.py:65
  138.2 0.1 copy.23
  138.3 0.8 dynamic-slice
  139.1 12.5 %all-to-all-done = bf16[16,8,320]{2,1,0:T(8,128)(2,1)S(1)} async-done(((bf16[16,8,320]{2,1,0:T(8,128)(2,1)}), bf16[16,8,320]{2,1,0:T(8,128)(2,1)S(1)}, u32[]{:S(2)}, u32[]{:S(2)}) %all-to-all-start) | async-done | bytes 81952 | tf_op jit(solution)/shard_map/all_to_all | solution.py:65
  151.7 0.1 reshape.59
  151.8 0.2 multiply_reduce_fusion
  152.0 0.3 convolution_convert_fusion.1
  152.3 0.7 reshape.54
  153.0 6.8 %all-to-all-start.1 = ((bf16[64,2,640]{2,1,0:T(2,128)(2,1)}), bf16[64,2,640]{2,1,0:T(2,128)(2,1)S(1)}, u32[]{:S(2)}, u32[]{:S(2)}) async-start(bf16[64,2,640]{2,1,0:T(2,128)(2,1)} %reshape.54), calls=%async_computation.1 | async-start | bytes 327680 | tf_op jit(solution)/shard_map/all_to_all | solution.py:91
  159.8 1.3 copy.28
  161.2 17.8 %all-to-all-done.1 = bf16[64,2,640]{2,1,0:T(2,128)(2,1)S(1)} async-done(((bf16[64,2,640]{2,1,0:T(2,128)(2,1)}), bf16[64,2,640]{2,1,0:T(2,128)(2,1)S(1)}, u32[]{:S(2)}, u32[]{:S(2)}) %all-to-all-start.1) | async-done | bytes 163872 | tf_op jit(solution)/shard_map/all_to_all | solution.py:91
  179.0 0.7 reshape.55
  179.7 1.0 copy.25
  180.8 4.5 %all-to-all-start.2 = ((bf16[96,8,640]{2,0,1:T(8,128)(2,1)}), bf16[96,8,640]{2,0,1:T(8,128)(2,1)S(1)}, u32[]{:S(2)}, u32[]{:S(2)}) async-start(bf16[96,8,640]{2,0,1:T(8,128)(2,1)} %copy.25), calls=%async_computation.2 | async-start | bytes 1966080 | tf_op jit(solution)/shard_map/all_to_all | solution.py:96
  185.3 17.1 %all-gather.5.cloned.1.call-done = bf16[128,5120]{1,0:T(8,128)(2,1)} async-done(((bf16[128,640]{1,0:T(8,128)(2,1)}), bf16[128,5120]{1,0:T(8,128)(2,1)}) %all-gather.5.cloned.1.call-update) | async-done | bytes 1310736 | tf_op jit(solution)/shard_map/all_gather | solution.py:98
  202.4 2.0 fusion.1
  204.4 12.8 %all_gather.11 = bf16[128,768]{0,1:T(8,128)(2,1)S(1)} all-gather(bf16[128,96]{0,1:T(8,128)(2,1)S(1)} %fusion.12), channel_id=1, replica_groups=mesh['head'=8,'ez'=16,'ey'=4] {'head'}, dimensions={1}, use_global_device_ids=true | all-gather | bytes 221184 | tf_op jit(solution)/shard_map/all_gather | solution.py:101
  217.2 0.3 convolution_convert_fusion
  217.6 0.7 reshape.57
  218.3 12.8 %all-to-all-start.3 = ((bf16[64,2,640]{2,1,0:T(2,128)(2,1)}), bf16[64,2,640]{2,1,0:T(2,128)(2,1)S(1)}, u32[]{:S(2)}, u32[]{:S(2)}) async-start(bf16[64,2,640]{2,1,0:T(2,128)(2,1)} %reshape.57), calls=%async_computation.3 | async-start | bytes 327680 | tf_op jit(solution)/shard_map/all_to_all | solution.py:104
  231.1 0.1 copy.24
  231.2 0.1 select_reduce_fusion
  231.3 19.3 %all-to-all-done.3 = bf16[64,2,640]{2,1,0:T(2,128)(2,1)S(1)} async-done(((bf16[64,2,640]{2,1,0:T(2,128)(2,1)}), bf16[64,2,640]{2,1,0:T(2,128)(2,1)S(1)}, u32[]{:S(2)}, u32[]{:S(2)}) %all-to-all-start.3) | async-done | bytes 163872 | tf_op jit(solution)/shard_map/all_to_all | solution.py:104
  250.7 0.8 convolution_add_fusion.1
  (54 shorter events, 0.8 us)
Async XLA Ops:
  6.5 195.9 %copy-start = (bf16[1,2,96,5120]{3,2,1,0:T(8,128)(2,1)S(1)}, bf16[1,2,96,5120]{3,2,1,0:T(8,128)(2,1)}, u32[]{:S(2)}) copy-start(bf16[1,2,96,5120]{3,2,1,0:T(8,128)(2,1)} %param.22) | copy-start | bytes 5898244
  6.5 49.6 %copy-start.9 = (s32[8,6]{1,0:T(8,128)S(1)}, s32[8,6]{1,0:T(8,128)}, u32[]{:S(2)}) copy-start(s32[8,6]{1,0:T(8,128)} %param.20) | copy-start | bytes 580
  6.5 91.4 %all-gather.3.cloned.1.call-start = ((), (), s32[]{:S(2)}) async-start(), calls=%async_computation.4 | async-start | bytes 3276800 | tf_op jit(solution)/shard_map/all_gather | solution.py:59
  11.1 13.6 %collective-permute-start.7 = (bf16[8,4096]{1,0:T(8,128)(2,1)S(1)}, bf16[8,4096]{1,0:T(8,128)(2,1)S(1)}, u32[]{:S(2)}, u32[]{:S(2)}) collective-permute-start(bf16[8,4096]{1,0:T(8,128)(2,1)S(1)} %bitcast.52), channel_id=1, source_target_pairs={{0,4},{4,8},{8,12},{12,16},{16,20},{20,24},{24,28},{28,32},{32,36}... | collective-permute-start | bytes 196616 | tf_op jit(solution)/shard_map/ppermute | solution.py:51
  15.0 11.7 %collective-permute-start = (bf16[8,4096]{1,0:T(8,128)(2,1)S(1)}, bf16[8,4096]{1,0:T(8,128)(2,1)S(1)}, u32[]{:S(2)}, u32[]{:S(2)}) collective-permute-start(bf16[8,4096]{1,0:T(8,128)(2,1)S(1)} %bitcast.53), channel_id=1, source_target_pairs={{0,60},{4,0},{8,4},{12,8},{16,12},{20,16},{24,20},{28,24},{32,28},... | collective-permute-start | bytes 196616 | tf_op jit(solution)/shard_map/ppermute | solution.py:54
  24.8 7.4 %collective-permute-start.8 = (bf16[8,4096]{1,0:T(8,128)(2,1)S(1)}, bf16[8,4096]{1,0:T(8,128)(2,1)S(1)}, u32[]{:S(2)}, u32[]{:S(2)}) collective-permute-start(bf16[8,4096]{1,0:T(8,128)(2,1)S(1)} %collective-permute-done.7), channel_id=1, source_target_pairs={{0,4},{4,8},{8,12},{12,16},{16,20},{20,24},{24,28},{28,32},{32,36}... | collective-permute-start | bytes 196616 | tf_op jit(solution)/shard_map/ppermute | solution.py:51
  26.7 7.4 %collective-permute-start.1 = (bf16[8,4096]{1,0:T(8,128)(2,1)S(1)}, bf16[8,4096]{1,0:T(8,128)(2,1)S(1)}, u32[]{:S(2)}, u32[]{:S(2)}) collective-permute-start(bf16[8,4096]{1,0:T(8,128)(2,1)S(1)} %collective-permute-done), channel_id=1, source_target_pairs={{0,60},{4,0},{8,4},{12,8},{16,12},{20,16},{24,20},{28,24},{32,28},... | collective-permute-start | bytes 196616 | tf_op jit(solution)/shard_map/ppermute | solution.py:54
  32.1 7.4 %collective-permute-start.9 = (bf16[8,4096]{1,0:T(8,128)(2,1)S(1)}, bf16[8,4096]{1,0:T(8,128)(2,1)S(1)}, u32[]{:S(2)}, u32[]{:S(2)}) collective-permute-start(bf16[8,4096]{1,0:T(8,128)(2,1)S(1)} %collective-permute-done.8), channel_id=1, source_target_pairs={{0,4},{4,8},{8,12},{12,16},{16,20},{20,24},{24,28},{28,32},{32,36}... | collective-permute-start | bytes 196616 | tf_op jit(solution)/shard_map/ppermute | solution.py:51
  34.1 7.4 %collective-permute-start.2 = (bf16[8,4096]{1,0:T(8,128)(2,1)S(1)}, bf16[8,4096]{1,0:T(8,128)(2,1)S(1)}, u32[]{:S(2)}, u32[]{:S(2)}) collective-permute-start(bf16[8,4096]{1,0:T(8,128)(2,1)S(1)} %collective-permute-done.1), channel_id=1, source_target_pairs={{0,60},{4,0},{8,4},{12,8},{16,12},{20,16},{24,20},{28,24},{32,28},... | collective-permute-start | bytes 196616 | tf_op jit(solution)/shard_map/ppermute | solution.py:54
  39.5 7.4 %collective-permute-start.10 = (bf16[8,4096]{1,0:T(8,128)(2,1)S(1)}, bf16[8,4096]{1,0:T(8,128)(2,1)S(1)}, u32[]{:S(2)}, u32[]{:S(2)}) collective-permute-start(bf16[8,4096]{1,0:T(8,128)(2,1)S(1)} %collective-permute-done.9), channel_id=1, source_target_pairs={{0,4},{4,8},{8,12},{12,16},{16,20},{20,24},{24,28},{28,32},{32,36}... | collective-permute-start | bytes 196616 | tf_op jit(solution)/shard_map/ppermute | solution.py:51
  41.4 12.8 %copy-start.2 = (bf16[8,4096]{1,0:T(8,128)(2,1)}, bf16[8,4096]{1,0:T(8,128)(2,1)S(1)}, u32[]{:S(2)}) copy-start(bf16[8,4096]{1,0:T(8,128)(2,1)S(1)} %collective-permute-done.2) | copy-start | bytes 196612
  41.4 7.3 %collective-permute-start.3 = (bf16[8,4096]{1,0:T(8,128)(2,1)S(1)}, bf16[8,4096]{1,0:T(8,128)(2,1)S(1)}, u32[]{:S(2)}, u32[]{:S(2)}) collective-permute-start(bf16[8,4096]{1,0:T(8,128)(2,1)S(1)} %collective-permute-done.2), channel_id=1, source_target_pairs={{0,60},{4,0},{8,4},{12,8},{16,12},{20,16},{24,20},{28,24},{32,28},... | collective-permute-start | bytes 196616 | tf_op jit(solution)/shard_map/ppermute | solution.py:54
  46.8 7.4 %collective-permute-start.11 = (bf16[8,4096]{1,0:T(8,128)(2,1)S(1)}, bf16[8,4096]{1,0:T(8,128)(2,1)S(1)}, u32[]{:S(2)}, u32[]{:S(2)}) collective-permute-start(bf16[8,4096]{1,0:T(8,128)(2,1)S(1)} %collective-permute-done.10), channel_id=1, source_target_pairs={{0,4},{4,8},{8,12},{12,16},{16,20},{20,24},{24,28},{28,32},{32,36}... | collective-permute-start | bytes 196616 | tf_op jit(solution)/shard_map/ppermute | solution.py:51
  48.8 12.8 %copy-start.3 = (bf16[8,4096]{1,0:T(8,128)(2,1)}, bf16[8,4096]{1,0:T(8,128)(2,1)S(1)}, u32[]{:S(2)}) copy-start(bf16[8,4096]{1,0:T(8,128)(2,1)S(1)} %collective-permute-done.3) | copy-start | bytes 196612
  48.8 7.5 %collective-permute-start.4 = (bf16[8,4096]{1,0:T(8,128)(2,1)S(1)}, bf16[8,4096]{1,0:T(8,128)(2,1)S(1)}, u32[]{:S(2)}, u32[]{:S(2)}) collective-permute-start(bf16[8,4096]{1,0:T(8,128)(2,1)S(1)} %collective-permute-done.3), channel_id=1, source_target_pairs={{0,60},{4,0},{8,4},{12,8},{16,12},{20,16},{24,20},{28,24},{32,28},... | collective-permute-start | bytes 196616 | tf_op jit(solution)/shard_map/ppermute | solution.py:54
  54.2 7.4 %collective-permute-start.12 = (bf16[8,4096]{1,0:T(8,128)(2,1)S(1)}, bf16[8,4096]{1,0:T(8,128)(2,1)S(1)}, u32[]{:S(2)}, u32[]{:S(2)}) collective-permute-start(bf16[8,4096]{1,0:T(8,128)(2,1)S(1)} %collective-permute-done.11), channel_id=1, source_target_pairs={{0,4},{4,8},{8,12},{12,16},{16,20},{20,24},{24,28},{28,32},{32,36}... | collective-permute-start | bytes 196616 | tf_op jit(solution)/shard_map/ppermute | solution.py:51
  56.2 14.9 %copy-start.5 = (bf16[8,4096]{1,0:T(8,128)(2,1)}, bf16[8,4096]{1,0:T(8,128)(2,1)S(1)}, u32[]{:S(2)}) copy-start(bf16[8,4096]{1,0:T(8,128)(2,1)S(1)} %collective-permute-done.4) | copy-start | bytes 196612
  56.3 7.4 %collective-permute-start.5 = (bf16[8,4096]{1,0:T(8,128)(2,1)S(1)}, bf16[8,4096]{1,0:T(8,128)(2,1)S(1)}, u32[]{:S(2)}, u32[]{:S(2)}) collective-permute-start(bf16[8,4096]{1,0:T(8,128)(2,1)S(1)} %collective-permute-done.4), channel_id=1, source_target_pairs={{0,60},{4,0},{8,4},{12,8},{16,12},{20,16},{24,20},{28,24},{32,28},... | collective-permute-start | bytes 196616 | tf_op jit(solution)/shard_map/ppermute | solution.py:54
  61.6 9.6 %copy-start.4 = (bf16[8,4096]{1,0:T(8,128)(2,1)}, bf16[8,4096]{1,0:T(8,128)(2,1)S(1)}, u32[]{:S(2)}) copy-start(bf16[8,4096]{1,0:T(8,128)(2,1)S(1)} %collective-permute-done.12) | copy-start | bytes 196612
  61.6 7.4 %collective-permute-start.13 = (bf16[8,4096]{1,0:T(8,128)(2,1)S(1)}, bf16[8,4096]{1,0:T(8,128)(2,1)S(1)}, u32[]{:S(2)}, u32[]{:S(2)}) collective-permute-start(bf16[8,4096]{1,0:T(8,128)(2,1)S(1)} %collective-permute-done.12), channel_id=1, source_target_pairs={{0,4},{4,8},{8,12},{12,16},{16,20},{20,24},{24,28},{28,32},{32,36}... | collective-permute-start | bytes 196616 | tf_op jit(solution)/shard_map/ppermute | solution.py:51
  63.6 7.5 %copy-start.7 = (bf16[8,4096]{1,0:T(8,128)(2,1)}, bf16[8,4096]{1,0:T(8,128)(2,1)S(1)}, u32[]{:S(2)}) copy-start(bf16[8,4096]{1,0:T(8,128)(2,1)S(1)} %collective-permute-done.5) | copy-start | bytes 196612
  63.7 7.5 %collective-permute-start.6 = (bf16[8,4096]{1,0:T(8,128)(2,1)S(1)}, bf16[8,4096]{1,0:T(8,128)(2,1)S(1)}, u32[]{:S(2)}, u32[]{:S(2)}) collective-permute-start(bf16[8,4096]{1,0:T(8,128)(2,1)S(1)} %collective-permute-done.5), channel_id=1, source_target_pairs={{0,60},{4,0},{8,4},{12,8},{16,12},{20,16},{24,20},{28,24},{32,28},... | collective-permute-start | bytes 196616 | tf_op jit(solution)/shard_map/ppermute | solution.py:54
  68.9 2.2 copy-start.6
  68.9 7.5 %collective-permute-start.14 = (bf16[8,4096]{1,0:T(8,128)(2,1)S(1)}, bf16[8,4096]{1,0:T(8,128)(2,1)}, u32[]{:S(2)}, u32[]{:S(2)}) collective-permute-start(bf16[8,4096]{1,0:T(8,128)(2,1)S(1)} %collective-permute-done.13), channel_id=1, source_target_pairs={{0,4},{4,8},{8,12},{12,16},{16,20},{20,24},{24,28},{28,32},{32,36}... | collective-permute-start | bytes 196616 | tf_op jit(solution)/shard_map/ppermute | solution.py:51
  71.2 0.6 copy-start.8
  83.3 68.5 %copy-start.1 = (bf16[8,5120]{1,0:T(8,128)(2,1)S(1)}, bf16[8,5120]{1,0:T(8,128)(2,1)}, u32[]{:S(2)}) copy-start(bf16[8,5120]{1,0:T(8,128)(2,1)} %param.18) | copy-start | bytes 245764
  125.9 25.7 %all-to-all-start = ((bf16[16,8,320]{2,1,0:T(8,128)(2,1)}), bf16[16,8,320]{2,1,0:T(8,128)(2,1)S(1)}, u32[]{:S(2)}, u32[]{:S(2)}) async-start(bf16[16,8,320]{2,1,0:T(8,128)(2,1)} %bitcast.35), calls=%async_computation | async-start | bytes 196608 | tf_op jit(solution)/shard_map/all_to_all | solution.py:65
  153.0 26.0 %all-to-all-start.1 = ((bf16[64,2,640]{2,1,0:T(2,128)(2,1)}), bf16[64,2,640]{2,1,0:T(2,128)(2,1)S(1)}, u32[]{:S(2)}, u32[]{:S(2)}) async-start(bf16[64,2,640]{2,1,0:T(2,128)(2,1)} %reshape.54), calls=%async_computation.1 | async-start | bytes 327680 | tf_op jit(solution)/shard_map/all_to_all | solution.py:91
  159.8 42.6 %all-gather.5.cloned.1.call-start = ((), (), s32[]{:S(2)}) async-start(), calls=%async_computation.5 | async-start | bytes 1474560 | tf_op jit(solution)/shard_map/all_gather | solution.py:98
  180.8 36.4 %all-to-all-start.2 = ((bf16[96,8,640]{2,0,1:T(8,128)(2,1)}), bf16[96,8,640]{2,0,1:T(8,128)(2,1)S(1)}, u32[]{:S(2)}, u32[]{:S(2)}) async-start(bf16[96,8,640]{2,0,1:T(8,128)(2,1)} %copy.25), calls=%async_computation.2 | async-start | bytes 1966080 | tf_op jit(solution)/shard_map/all_to_all | solution.py:96
  204.4 26.8 %copy-start.10 = (f32[8,6]{1,0:T(8,128)S(1)}, f32[8,6]{1,0:T(8,128)}, u32[]{:S(2)}) copy-start(f32[8,6]{1,0:T(8,128)} %param.21) | copy-start | bytes 580
  218.3 32.3 %all-to-all-start.3 = ((bf16[64,2,640]{2,1,0:T(2,128)(2,1)}), bf16[64,2,640]{2,1,0:T(2,128)(2,1)S(1)}, u32[]{:S(2)}, u32[]{:S(2)}) async-start(bf16[64,2,640]{2,1,0:T(2,128)(2,1)} %reshape.57), calls=%async_computation.3 | async-start | bytes 327680 | tf_op jit(solution)/shard_map/all_to_all | solution.py:104
Sparse Core Ops, SparseCore 0:
  56.3 41.5 all-gather.2
  179.9 22.4 all-gather.4

commit v10 on v7

--- a/solution.py
+++ b/solution.py
@@ -48,13 +48,32 @@
     gathered = gathered.reshape(-1, flattened.shape[1])
     value_cols = lax.all_gather(w_value_out, "ey", axis=1, tiled=True)
     column_terms = jnp.dot(gathered, value_cols, preferred_element_type=jnp.float32)
-    column_sums = lax.psum(column_terms, "head")
-    attention = lax.all_to_all(
-        column_sums.astype(jnp.bfloat16), "ez", split_axis=0, concat_axis=1, tiled=True
+    head_count = lax.axis_size("head")
+    head_index = lax.axis_index("head")
+    z_count = lax.axis_size("ez")
+    width = resid.shape[1]
+    block = column_terms.shape[1]
+    piece = block // head_count
+    sending = column_terms.reshape(z_count, seq_local, head_count, piece)
+    sending = sending.transpose(2, 0, 1, 3).reshape(head_count * z_count, seq_local, piece)
+    received = lax.all_to_all(sending, ("head", "ez"), split_axis=0, concat_axis=0, tiled=True)
+    received = received.reshape(head_count, z_count, seq_local, piece)
+    attention = jnp.sum(received, axis=0).astype(jnp.bfloat16)
+    attention = attention.transpose(1, 0, 2).reshape(seq_local, -1)
+    strided = lambda values: lax.dynamic_index_in_dim(
+        values.reshape(values.shape[:-1] + (width // block, head_count, piece)),
+        head_index, axis=values.ndim, keepdims=False,
+    ).reshape(values.shape[:-1] + (-1,))
+    stream_part = strided(resid).astype(jnp.float32) + attention.astype(jnp.float32)
+    square_sum = lax.psum(jnp.sum(stream_part * stream_part, axis=1, keepdims=True), "head")
+    mean_square = square_sum / width
+    normed_part = (stream_part * lax.rsqrt(mean_square + norm_epsilon) * strided(norm_gain)).astype(
+        jnp.bfloat16
     )
-    stream = resid.astype(jnp.float32) + attention.astype(jnp.float32)
-    mean_square = jnp.mean(stream * stream, axis=1, keepdims=True)
-    normed = (stream * lax.rsqrt(mean_square + norm_epsilon) * norm_gain).astype(jnp.bfloat16)
+    halves = width // (head_count * block)
+    to_heads = stream_part.reshape(seq_local, head_count, halves, piece).transpose(1, 0, 2, 3)
+    from_heads = lax.all_to_all(to_heads, "head", split_axis=0, concat_axis=0, tiled=True)
+    stream_cols = from_heads.transpose(1, 2, 0, 3).reshape(seq_local, -1)
     expert_count = lax.axis_size("ez") * lax.axis_size("ey")
     top_count = route_ids.shape[1]
     capacity = max(2, -(-(seq_local * top_count) // expert_count))
@@ -69,11 +88,11 @@
     matches = target[None, :, :] == places[:, None, None]
     selector = jnp.sum(matches.astype(jnp.int32), axis=2).astype(jnp.bfloat16)
     blending = jnp.sum(jnp.where(matches, route_weights[None, :, :], 0.0), axis=2)
-    gate_up = w_gate_up[0]
-    col_width = stream.shape[1] // lax.axis_size("head")
-    offset = lax.axis_index("head") * col_width
-    normed_cols = lax.dynamic_slice_in_dim(normed, offset, col_width, 1)
-    outgoing = jnp.dot(selector, normed_cols, preferred_element_type=jnp.float32).astype(jnp.bfloat16)
+    gate_up = w_gate_up[0].reshape(
+        w_gate_up.shape[1], w_gate_up.shape[2], width // block, head_count, piece
+    )
+    gate_up = gate_up.transpose(0, 1, 3, 2, 4).reshape(w_gate_up.shape[1], w_gate_up.shape[2], width)
+    outgoing = jnp.dot(selector, normed_part, preferred_element_type=jnp.float32).astype(jnp.bfloat16)
     outgoing = outgoing.reshape(expert_count, capacity, -1)
     arrived = lax.all_to_all(outgoing, EXPERT, split_axis=0, concat_axis=0, tiled=True)
     arrived_cols = arrived.reshape(-1, arrived.shape[2])
@@ -91,7 +110,6 @@
     returned = lax.all_to_all(summed_rows, EXPERT, split_axis=0, concat_axis=0, tiled=True)
     back_rows = returned.reshape(expert_count * capacity, -1).astype(jnp.float32)
     mixture = jnp.dot(blending.T, back_rows, precision=lax.Precision.HIGHEST)
-    stream_cols = lax.dynamic_slice_in_dim(stream, offset, col_width, 1)
     return stream_cols + mixture
 
 

time: 236 us -> 245 us (1.038)
  starting transfers between devices: 50.9 us -> 61.6 us
  blocking collectives: 34.8 us -> 24.7 us
  local copies, waits for them, and re-layouts: 7.78 us -> 17.5 us
  waiting for transfers between devices: 116 us -> 112 us
    all_gather x1, waiting for transfers between devices: 0.01 us -> 29 us  [on_device(): value_cols = lax.all_gather(w_value_out, 'ey', axis=1, tiled=True)]
    all_to_all x1, waiting for transfers between devices: 48.7 us -> 20 us  [on_device(): lax.all_to_all(latent_copies, 'ez', split_axis=0, concat_axis=0, tiled=True)]
    all_gather x1, waiting for transfers between devices: 17.1 us -> 6.21 us  [on_device(): flat_rows = lax.all_gather(arrived_cols, 'head', axis=1, tiled=True)]
    psum x1, blocking collectives: 22 us -> 11.9 us  [on_device(): lax.psum(jnp.sum(stream_part * stream_part, axis=1, keepdims=True), 'head')]
    all_to_all x1 -> x2, waiting for transfers between devices: 12.6 us -> 19.2 us  [the longest x1 16.9 us: on_device(): lax.all_to_all(sending, ('head', 'ez'), split_axis=0, concat_axis=0, tile...]
    all_to_all x1 -> x2, starting transfers between devices: 11.6 us -> 17.4 us  [the longest x1 12.6 us: on_device(): lax.all_to_all(sending, ('head', 'ez'), split_axis=0, concat_axis=0, tile...]
    unnamed x11 -> x20, local copies, waits for them, and re-layouts: 1.48 us -> 7.27 us
    transpose x0 -> x4, local copies, waits for them, and re-layouts: none -> 3.98 us  [the longest x1 3.92 us: on_device(): gate_up.transpose(0, 1, 3, 2, 4)]
  transfers between devices with their start and end apart: 7 -> 8, of which waited for: 5 -> 7; matrix products, arithmetic and copies ran while one was open for 3% -> 9% of each run, Pallas kernels for 0% -> 0%
where the time goes in v10:
time: 245 us; the launch traced here: 243 us
  waiting for transfers between devices  112 us (46%)
  starting transfers between devices  61.6 us (25%)
  blocking collectives  24.7 us (10%)
  local copies, waits for them, and re-layouts  17.5 us (7%)
  between operations  13.7 us (6%)
  matrix products  10.8 us (4%)
  other arithmetic  2.69 us (1%)
    all_gather x1, waiting for transfers between devices, on_device(): value_cols = lax.all_gather(w_value_out, 'ey', axis=1, tiled=True)  29 us
    all_to_all x1, waiting for transfers between devices, on_device(): lax.all_to_all(latent_copies, 'ez', split_axis=0, concat_axis=0, tiled=True)  20 us
    all_to_all x1, waiting for transfers between devices, on_device(): lax.all_to_all(outgoing, EXPERT, split_axis=0, concat_axis=0, tiled=True)  19.5 us
    all_to_all x1, waiting for transfers between devices, on_device(): lax.all_to_all(summed_rows, EXPERT, split_axis=0, concat_axis=0, tiled=True)  17.8 us
    all_to_all x1, waiting for transfers between devices, on_device(): lax.all_to_all(sending, ('head', 'ez'), split_axis=0, concat_axis=0, tile...  16.9 us
    all_to_all x1, starting transfers between devices, on_device(): lax.all_to_all(summed_rows, EXPERT, split_axis=0, concat_axis=0, tiled=True)  15.9 us
    all_to_all x1, starting transfers between devices, on_device(): lax.all_to_all(latent_copies, 'ez', split_axis=0, concat_axis=0, tiled=True)  15.2 us
    all_gather x1, blocking collectives, on_device(): hidden_all = lax.all_gather(hidden, 'head', axis=1, tiled=True)  12.8 us
  transfers between devices with their start and end apart: 8, of which 7 were waited for; matrix products, arithmetic and copies ran while one was open for 9% of the time, Pallas kernels for 0%

profile of v10, /device:TPU:6, one launch (start us, length us, event | category | flops | bytes accessed | tf_op | source)
XLA Modules:
  0.0 243.3 jit_solution(2596459979954062128)
XLA Ops:
  6.5 0.7 all-gather.3.cloned.1.call-update
  7.3 0.5 copy-done
  7.8 1.2 fusion.20
  9.0 1.1 fusion.7
  10.1 0.2 fusion.18
  10.2 0.3 fusion.3
  10.6 1.1 broadcast_in_dim.34
  11.7 15.2 %all-to-all-start = ((bf16[16,8,4096]{2,1,0:T(8,128)(2,1)}), bf16[16,8,4096]{2,1,0:T(8,128)(2,1)S(1)}, u32[]{:S(2)}, u32[]{:S(2)}) async-start(bf16[16,8,4096]{2,1,0:T(8,128)(2,1)} %broadcast_in_dim.34), calls=%async_computation | async-start | bytes 2097152 | tf_op jit(solution)/shard_map/all_to_all | solution.py:47
  26.9 0.4 reshape.71
  27.4 0.1 eq.28
  27.5 0.1 fusion.13
  27.5 0.1 reduce_window_sum.11
  27.6 0.2 select_reduce_fusion.1
  27.8 0.1 reduce_sum.59
  27.9 29.0 %all-gather.3.cloned.1.call-done = bf16[4096,320]{0,1:T(8,128)(2,1)} async-done(((bf16[4096,80]{0,1:T(8,128)(2,1)}), bf16[4096,320]{0,1:T(8,128)(2,1)}) %all-gather.3.cloned.1.call-update) | async-done | bytes 2621456 | tf_op jit(solution)/shard_map/all_gather | solution.py:49
  56.8 20.0 %all-to-all-done = bf16[16,8,4096]{2,1,0:T(8,128)(2,1)S(1)} async-done(((bf16[16,8,4096]{2,1,0:T(8,128)(2,1)}), bf16[16,8,4096]{2,1,0:T(8,128)(2,1)S(1)}, u32[]{:S(2)}, u32[]{:S(2)}) %all-to-all-start) | async-done | bytes 1048608 | tf_op jit(solution)/shard_map/all_to_all | solution.py:47
  76.9 3.6 %convolution_bitcast_fusion = f32[8,16,8,40]{3,2,0,1:T(8,128)S(1)} fusion(bf16[8,40,4096,1]{2,1,0,3:T(8,128)(2,1)} %bitcast.97, bf16[16,8,4096]{2,1,0:T(8,128)(2,1)S(1)} %all-to-all-done), kind=kOutput, calls=%fused_computation.3 | convolution fusion | flops 335544320 | bytes 3833856 | tf_op jit(solution)/shard_map/dot_general | solution.py:50
  80.4 0.0 copy-start.3
  80.5 0.0 copy-start.1
  80.5 1.2 reshape.97
  81.7 12.6 %all-to-all-start.1 = ((f32[128,1,320]{2,1,0:T(1,128)}), f32[128,1,320]{2,1,0:T(1,128)S(1)}, u32[]{:S(2)}, u32[]{:S(2)}) async-start(f32[128,1,320]{2,1,0:T(1,128)} %reshape.97), calls=%async_computation.1 | async-start | bytes 393216 | tf_op jit(solution)/shard_map/all_to_all | solution.py:59
  94.3 0.1 copy.39
  94.4 0.1 constant_dynamic-slice_fusion
  94.5 0.1 reshape.84
  94.6 0.1 reshape.75
  94.8 0.1 mul.57
  94.8 0.1 convert_reduce_fusion
  94.9 16.9 %all-to-all-done.1 = f32[128,1,320]{2,1,0:T(1,128)S(1)} async-done(((f32[128,1,320]{2,1,0:T(1,128)}), f32[128,1,320]{2,1,0:T(1,128)S(1)}, u32[]{:S(2)}, u32[]{:S(2)}) %all-to-all-start.1) | async-done | bytes 163872 | tf_op jit(solution)/shard_map/all_to_all | solution.py:59
  111.9 0.6 broadcast.28
  112.4 1.1 reduce.5
  113.5 0.2 reshape.98
  113.8 0.1 fusion.10
  114.0 0.1 reshape.85
  114.0 11.9 %psum.7 = f32[8,1]{0,1:T(1,128)S(1)} all-reduce(f32[8,1]{0,1:T(1,128)S(1)} %bitcast.96), channel_id=1, replica_groups=mesh['head'=8,'ez'=16,'ey'=4] {'head'}, use_global_device_ids=true, to_apply=%region_8.9 | all-reduce | flops 8 | bytes 64 | tf_op jit(solution)/shard_map/psum | solution.py:68
  125.9 0.3 convolution_convert_fusion.1
  126.2 0.7 reshape.76
  126.9 6.3 %all-to-all-start.3 = ((bf16[64,2,640]{2,1,0:T(2,128)(2,1)}), bf16[64,2,640]{2,1,0:T(2,128)(2,1)S(1)}, u32[]{:S(2)}, u32[]{:S(2)}) async-start(bf16[64,2,640]{2,1,0:T(2,128)(2,1)} %reshape.76), calls=%async_computation.3 | async-start | bytes 327680 | tf_op jit(solution)/shard_map/all_to_all | solution.py:97
  133.2 0.0 all-gather.5.cloned.1.call-start
  133.3 0.1 copy.51
  133.4 19.5 %all-to-all-done.3 = bf16[64,2,640]{2,1,0:T(2,128)(2,1)S(1)} async-done(((bf16[64,2,640]{2,1,0:T(2,128)(2,1)}), bf16[64,2,640]{2,1,0:T(2,128)(2,1)S(1)}, u32[]{:S(2)}, u32[]{:S(2)}) %all-to-all-start.3) | async-done | bytes 163872 | tf_op jit(solution)/shard_map/all_to_all | solution.py:97
  152.9 0.7 reshape.77
  153.6 0.0 all-gather.5.cloned.1.call-update
  153.6 4.3 %copy.43 = bf16[1,2,96,5120]{2,3,1,0:T(8,128)(2,1)} copy(bf16[1,2,96,5120]{3,2,1,0:T(8,128)(2,1)} %param.22) | data formatting | bytes 3932160 | tf_op args[10]
  157.9 3.9 %copy.44 = bf16[2,96,8,16,40]{1,4,3,2,0:T(8,128)(2,1)} copy(bf16[2,96,8,16,40]{1,4,2,3,0:T(8,128)(2,1)} %bitcast.87) | data formatting | bytes 3932160 | tf_op jit(solution)/shard_map/transpose | solution.py:94
  161.9 1.1 copy.46
  162.9 6.8 %all-to-all-start.4 = ((bf16[96,8,640]{2,0,1:T(8,128)(2,1)}), bf16[96,8,640]{2,0,1:T(8,128)(2,1)S(1)}, u32[]{:S(2)}, u32[]{:S(2)}) async-start(bf16[96,8,640]{2,0,1:T(8,128)(2,1)} %copy.46), calls=%async_computation.4 | async-start | bytes 1966080 | tf_op jit(solution)/shard_map/all_to_all | solution.py:102
  169.7 0.7 reshape.99
  170.4 6.2 %all-gather.5.cloned.1.call-done = bf16[128,5120]{1,0:T(8,128)(2,1)} async-done(((bf16[128,640]{1,0:T(8,128)(2,1)}), bf16[128,5120]{1,0:T(8,128)(2,1)}) %all-gather.5.cloned.1.call-update) | async-done | bytes 1310736 | tf_op jit(solution)/shard_map/all_gather | solution.py:104
  176.7 3.2 %fusion.1 = f32[128,2,96]{0,2,1:T(8,128)S(1)} fusion(bf16[2,96,5120]{1,2,0:T(8,128)(2,1)} %bitcast.86, bf16[128,5120]{1,0:T(8,128)(2,1)} %all-gather.5.cloned.1.call-done), kind=kOutput, calls=%fused_computation.1 | convolution fusion | flops 251658240 | bytes 3375104 | tf_op jit(solution)/shard_map/rd,gfd->rgf/dot_general | solution.py:105
  179.9 12.8 %all_gather.11 = bf16[128,768]{0,1:T(8,128)(2,1)S(1)} all-gather(bf16[128,96]{0,1:T(8,128)(2,1)S(1)} %fusion.12), channel_id=1, replica_groups=mesh['head'=8,'ez'=16,'ey'=4] {'head'}, dimensions={1}, use_global_device_ids=true | all-gather | bytes 221184 | tf_op jit(solution)/shard_map/all_gather | solution.py:107
  192.7 0.0 all-to-all-done.4
  192.7 4.8 %all-to-all-start.2 = ((f32[8,1,640]{2,1,0:T(1,128)}), f32[8,1,640]{2,1,0:T(1,128)S(1)}, u32[]{:S(2)}, u32[]{:S(2)}) async-start(f32[8,1,640]{2,1,0:T(1,128)} %reshape.99), calls=%async_computation.2 | async-start | bytes 40960 | tf_op jit(solution)/shard_map/all_to_all | solution.py:75
  197.5 0.3 convolution_convert_fusion
  197.9 0.7 reshape.80
  198.6 2.2 all-to-all-done.2
  200.8 15.9 %all-to-all-start.5 = ((bf16[64,2,640]{2,1,0:T(2,128)(2,1)}), bf16[64,2,640]{2,1,0:T(2,128)(2,1)S(1)}, u32[]{:S(2)}, u32[]{:S(2)}) async-start(bf16[64,2,640]{2,1,0:T(2,128)(2,1)} %reshape.80), calls=%async_computation.5 | async-start | bytes 327680 | tf_op jit(solution)/shard_map/all_to_all | solution.py:110
  216.7 0.1 copy.40
  216.8 0.1 select_reduce_fusion
  216.9 0.7 reduce.6
  217.5 0.1 reshape.100
  217.7 0.1 reshape.74
  217.8 17.8 %all-to-all-done.5 = bf16[64,2,640]{2,1,0:T(2,128)(2,1)S(1)} async-done(((bf16[64,2,640]{2,1,0:T(2,128)(2,1)}), bf16[64,2,640]{2,1,0:T(2,128)(2,1)S(1)}, u32[]{:S(2)}, u32[]{:S(2)}) %all-to-all-start.5) | async-done | bytes 163872 | tf_op jit(solution)/shard_map/all_to_all | solution.py:110
  235.6 0.1 reshape.81
  235.7 0.8 convolution_add_fusion.1
  (24 shorter events, 0.3 us)
Async XLA Ops:
  6.5 1.2 copy-start
  6.5 50.3 %all-gather.3.cloned.1.call-start = ((), (), s32[]{:S(2)}) async-start(), calls=%async_computation.6 | async-start | bytes 3276800 | tf_op jit(solution)/shard_map/all_gather | solution.py:49
  9.0 17.9 %copy-start.2 = (bf16[8,5120]{1,0:T(8,128)(2,1)S(1)}, bf16[8,5120]{1,0:T(8,128)(2,1)}, u32[]{:S(2)}) copy-start(bf16[8,5120]{1,0:T(8,128)(2,1)} %param.18) | copy-start | bytes 245764
  9.0 18.4 %copy-start.4 = (s32[8,6]{1,0:T(8,128)S(1)}, s32[8,6]{1,0:T(8,128)}, u32[]{:S(2)}) copy-start(s32[8,6]{1,0:T(8,128)} %param.20) | copy-start | bytes 580
  11.7 65.2 %all-to-all-start = ((bf16[16,8,4096]{2,1,0:T(8,128)(2,1)}), bf16[16,8,4096]{2,1,0:T(8,128)(2,1)S(1)}, u32[]{:S(2)}, u32[]{:S(2)}) async-start(bf16[16,8,4096]{2,1,0:T(8,128)(2,1)} %broadcast_in_dim.34), calls=%async_computation | async-start | bytes 2097152 | tf_op jit(solution)/shard_map/all_to_all | solution.py:47
  80.4 14.2 %copy-start.3 = (f32[5120]{0:T(1024)S(1)}, f32[5120]{0:T(1024)}, u32[]{:S(2)}) copy-start(f32[5120]{0:T(1024)} %param.19) | copy-start | bytes 61444
  80.5 52.8 %copy-start.1 = (bf16[1,96,5120]{2,1,0:T(8,128)(2,1)S(1)}, bf16[1,96,5120]{2,1,0:T(8,128)(2,1)}, u32[]{:S(2)}) copy-start(bf16[1,96,5120]{2,1,0:T(8,128)(2,1)} %param.23) | copy-start | bytes 2949124
  81.7 30.2 %all-to-all-start.1 = ((f32[128,1,320]{2,1,0:T(1,128)}), f32[128,1,320]{2,1,0:T(1,128)S(1)}, u32[]{:S(2)}, u32[]{:S(2)}) async-start(f32[128,1,320]{2,1,0:T(1,128)} %reshape.97), calls=%async_computation.1 | async-start | bytes 393216 | tf_op jit(solution)/shard_map/all_to_all | solution.py:59
  126.9 25.9 %all-to-all-start.3 = ((bf16[64,2,640]{2,1,0:T(2,128)(2,1)}), bf16[64,2,640]{2,1,0:T(2,128)(2,1)S(1)}, u32[]{:S(2)}, u32[]{:S(2)}) async-start(bf16[64,2,640]{2,1,0:T(2,128)(2,1)} %reshape.76), calls=%async_computation.3 | async-start | bytes 327680 | tf_op jit(solution)/shard_map/all_to_all | solution.py:97
  133.2 43.4 %all-gather.5.cloned.1.call-start = ((), (), s32[]{:S(2)}) async-start(), calls=%async_computation.7 | async-start | bytes 1474560 | tf_op jit(solution)/shard_map/all_gather | solution.py:104
  162.9 29.7 %all-to-all-start.4 = ((bf16[96,8,640]{2,0,1:T(8,128)(2,1)}), bf16[96,8,640]{2,0,1:T(8,128)(2,1)S(1)}, u32[]{:S(2)}, u32[]{:S(2)}) async-start(bf16[96,8,640]{2,0,1:T(8,128)(2,1)} %copy.46), calls=%async_computation.4 | async-start | bytes 1966080 | tf_op jit(solution)/shard_map/all_to_all | solution.py:102
  176.7 40.0 %copy-start.5 = (f32[8,6]{1,0:T(8,128)S(1)}, f32[8,6]{1,0:T(8,128)}, u32[]{:S(2)}) copy-start(f32[8,6]{1,0:T(8,128)} %param.21) | copy-start | bytes 580
  192.7 8.1 %all-to-all-start.2 = ((f32[8,1,640]{2,1,0:T(1,128)}), f32[8,1,640]{2,1,0:T(1,128)S(1)}, u32[]{:S(2)}, u32[]{:S(2)}) async-start(f32[8,1,640]{2,1,0:T(1,128)} %reshape.99), calls=%async_computation.2 | async-start | bytes 40960 | tf_op jit(solution)/shard_map/all_to_all | solution.py:75
  200.8 34.8 %all-to-all-start.5 = ((bf16[64,2,640]{2,1,0:T(2,128)(2,1)}), bf16[64,2,640]{2,1,0:T(2,128)(2,1)S(1)}, u32[]{:S(2)}, u32[]{:S(2)}) async-start(bf16[64,2,640]{2,1,0:T(2,128)(2,1)} %reshape.80), calls=%async_computation.5 | async-start | bytes 327680 | tf_op jit(solution)/shard_map/all_to_all | solution.py:110
Sparse Core Ops, SparseCore 0:
  9.5 47.3 all-gather.2
  153.8 22.8 all-gather.4

commit v11 on v10

--- a/solution.py
+++ b/solution.py
@@ -47,6 +47,15 @@
     gathered = lax.all_to_all(latent_copies, "ez", split_axis=0, concat_axis=0, tiled=True)
     gathered = gathered.reshape(-1, flattened.shape[1])
     value_cols = lax.all_gather(w_value_out, "ey", axis=1, tiled=True)
+    width = resid.shape[1]
+    block = value_cols.shape[1]
+    head_count = lax.axis_size("head")
+    piece = block // head_count
+    gate_up = w_gate_up[0].reshape(
+        w_gate_up.shape[1], w_gate_up.shape[2], width // block, head_count, piece
+    )
+    gate_up = gate_up.transpose(0, 1, 3, 2, 4).reshape(w_gate_up.shape[1], w_gate_up.shape[2], width)
+    gathered, gate_up = lax.optimization_barrier((gathered, gate_up))
     column_terms = jnp.dot(gathered, value_cols, preferred_element_type=jnp.float32)
     head_count = lax.axis_size("head")
     head_index = lax.axis_index("head")
@@ -70,10 +79,6 @@
     normed_part = (stream_part * lax.rsqrt(mean_square + norm_epsilon) * strided(norm_gain)).astype(
         jnp.bfloat16
     )
-    halves = width // (head_count * block)
-    to_heads = stream_part.reshape(seq_local, head_count, halves, piece).transpose(1, 0, 2, 3)
-    from_heads = lax.all_to_all(to_heads, "head", split_axis=0, concat_axis=0, tiled=True)
-    stream_cols = from_heads.transpose(1, 2, 0, 3).reshape(seq_local, -1)
     expert_count = lax.axis_size("ez") * lax.axis_size("ey")
     top_count = route_ids.shape[1]
     capacity = max(2, -(-(seq_local * top_count) // expert_count))
@@ -88,17 +93,17 @@
     matches = target[None, :, :] == places[:, None, None]
     selector = jnp.sum(matches.astype(jnp.int32), axis=2).astype(jnp.bfloat16)
     blending = jnp.sum(jnp.where(matches, route_weights[None, :, :], 0.0), axis=2)
-    gate_up = w_gate_up[0].reshape(
-        w_gate_up.shape[1], w_gate_up.shape[2], width // block, head_count, piece
-    )
-    gate_up = gate_up.transpose(0, 1, 3, 2, 4).reshape(w_gate_up.shape[1], w_gate_up.shape[2], width)
     outgoing = jnp.dot(selector, normed_part, preferred_element_type=jnp.float32).astype(jnp.bfloat16)
     outgoing = outgoing.reshape(expert_count, capacity, -1)
     arrived = lax.all_to_all(outgoing, EXPERT, split_axis=0, concat_axis=0, tiled=True)
     arrived_cols = arrived.reshape(-1, arrived.shape[2])
     head_count = lax.axis_size("head")
     down_blocks = w_down[0].reshape(w_down.shape[1], head_count, -1)
-    arrived_cols, down_blocks = lax.optimization_barrier((arrived_cols, down_blocks))
+    halves = width // (head_count * block)
+    to_heads = stream_part.reshape(seq_local, head_count, halves, piece).transpose(1, 0, 2, 3)
+    arrived_cols, down_blocks, to_heads = lax.optimization_barrier((arrived_cols, down_blocks, to_heads))
+    from_heads = lax.all_to_all(to_heads, "head", split_axis=0, concat_axis=0, tiled=True)
+    stream_cols = from_heads.transpose(1, 2, 0, 3).reshape(seq_local, -1)
     down_cols = lax.all_to_all(down_blocks, "head", split_axis=1, concat_axis=0, tiled=True)
     down_cols = down_cols.reshape(-1, down_blocks.shape[2])
     flat_rows = lax.all_gather(arrived_cols, "head", axis=1, tiled=True)

time: 245 us -> 242 us (0.988)
  starting transfers between devices: 61.6 us -> 57.6 us
    all_gather x1, waiting for transfers between devices: 29 us -> 0.01 us  [on_device(): value_cols = lax.all_gather(w_value_out, 'ey', axis=1, tiled=True)]
    all_to_all x1, waiting for transfers between devices: 20 us -> 40 us  [on_device(): lax.all_to_all(latent_copies, 'ez', split_axis=0, concat_axis=0, tiled=True)]
    all_gather x1, waiting for transfers between devices: 6.21 us -> 15.5 us  [on_device(): flat_rows = lax.all_gather(arrived_cols, 'head', axis=1, tiled=True)]
    all_to_all x1, starting transfers between devices: 15.9 us -> 10.6 us  [on_device(): lax.all_to_all(summed_rows, EXPERT, split_axis=0, concat_axis=0, tiled=True)]
  transfers between devices with their start and end apart: 8 -> 8, of which waited for: 7 -> 6; matrix products, arithmetic and copies ran while one was open for 9% -> 7% of each run, Pallas kernels for 0% -> 0%
where the time goes in v11:
time: 242 us; the launch traced here: 241 us
  waiting for transfers between devices  113 us (47%)
  starting transfers between devices  57.6 us (24%)
  blocking collectives  25 us (10%)
  local copies, waits for them, and re-layouts  18.6 us (8%)
  between operations  13.7 us (6%)
  matrix products  9.98 us (4%)
  other arithmetic  2.68 us (1%)
    all_to_all x1, waiting for transfers between devices, on_device(): lax.all_to_all(latent_copies, 'ez', split_axis=0, concat_axis=0, tiled=True)  40 us
    all_to_all x1, waiting for transfers between devices, on_device(): lax.all_to_all(outgoing, EXPERT, split_axis=0, concat_axis=0, tiled=True)  19.7 us
    all_to_all x1, waiting for transfers between devices, on_device(): lax.all_to_all(summed_rows, EXPERT, split_axis=0, concat_axis=0, tiled=True)  17.8 us
    all_to_all x1, waiting for transfers between devices, on_device(): lax.all_to_all(sending, ('head', 'ez'), split_axis=0, concat_axis=0, tile...  17 us
    all_gather x1, waiting for transfers between devices, on_device(): flat_rows = lax.all_gather(arrived_cols, 'head', axis=1, tiled=True)  15.5 us
    all_to_all x1, starting transfers between devices, on_device(): lax.all_to_all(latent_copies, 'ez', split_axis=0, concat_axis=0, tiled=True)  15.2 us
    all_to_all x1, starting transfers between devices, on_device(): lax.all_to_all(sending, ('head', 'ez'), split_axis=0, concat_axis=0, tile...  14.1 us
    all_gather x1, blocking collectives, on_device(): hidden_all = lax.all_gather(hidden, 'head', axis=1, tiled=True)  13.2 us
  transfers between devices with their start and end apart: 8, of which 6 were waited for; matrix products, arithmetic and copies ran while one was open for 7% of the time, Pallas kernels for 0%

profile of v11, /device:TPU:6, one launch (start us, length us, event | category | flops | bytes accessed | tf_op | source)
XLA Modules:
  0.0 240.6 jit_solution(14795272573556648557)
XLA Ops:
  6.5 1.2 copy-done
  7.8 1.2 fusion.19
  9.0 1.1 fusion.7
  10.0 0.2 fusion.18
  10.2 0.3 fusion.3
  10.6 1.2 broadcast_in_dim.34
  11.7 15.2 %all-to-all-start = ((bf16[16,8,4096]{2,1,0:T(8,128)(2,1)}), bf16[16,8,4096]{2,1,0:T(8,128)(2,1)S(1)}, u32[]{:S(2)}, u32[]{:S(2)}) async-start(bf16[16,8,4096]{2,1,0:T(8,128)(2,1)} %broadcast_in_dim.34), calls=%async_computation | async-start | bytes 2097152 | tf_op jit(solution)/shard_map/all_to_all | solution.py:47
  26.9 0.0 all-gather.3.cloned.1.call-start
  27.0 0.7 all-gather.3.cloned.1.call-update
  27.7 0.4 reshape.72
  28.1 4.3 %copy.42 = bf16[1,2,96,5120]{2,3,1,0:T(8,128)(2,1)} copy(bf16[1,2,96,5120]{3,2,1,0:T(8,128)(2,1)} %param.22) | data formatting | bytes 3932160 | tf_op args[10]
  32.4 3.9 %copy.43 = bf16[2,96,8,16,40]{1,4,3,2,0:T(8,128)(2,1)} copy(bf16[2,96,8,16,40]{1,4,2,3,0:T(8,128)(2,1)} %bitcast.75) | data formatting | bytes 3932160 | tf_op jit(solution)/shard_map/transpose | solution.py:57
  36.4 0.1 constant_dynamic-slice_fusion
  36.5 0.1 reshape.85
  36.6 0.1 reshape.78
  36.7 0.1 mul.57
  36.8 0.1 eq.28
  36.9 40.0 %all-to-all-done = bf16[16,8,4096]{2,1,0:T(8,128)(2,1)S(1)} async-done(((bf16[16,8,4096]{2,1,0:T(8,128)(2,1)}), bf16[16,8,4096]{2,1,0:T(8,128)(2,1)S(1)}, u32[]{:S(2)}, u32[]{:S(2)}) %all-to-all-start) | async-done | bytes 1048608 | tf_op jit(solution)/shard_map/all_to_all | solution.py:47
  76.9 2.8 %fusion.20 = f32[128,320]{1,0:T(8,128)S(1)} fusion(bf16[128,4096]{1,0:T(8,128)(2,1)S(1)} %bitcast.76, bf16[4096,320]{0,1:T(8,128)(2,1)} %all-gather.3.cloned.1.call-done), kind=kOutput, calls=%fused_computation.45 | convolution fusion | flops 335544320 | bytes 3833856 | tf_op jit(solution)/shard_map/dot_general | solution.py:59
  79.7 0.2 reshape.75
  79.9 0.0 copy-start.1
  80.0 0.1 copy.45
  80.1 1.2 reshape.98
  81.2 14.1 %all-to-all-start.1 = ((f32[128,1,320]{2,1,0:T(1,128)}), f32[128,1,320]{2,1,0:T(1,128)S(1)}, u32[]{:S(2)}, u32[]{:S(2)}) async-start(f32[128,1,320]{2,1,0:T(1,128)} %reshape.98), calls=%async_computation.1 | async-start | bytes 393216 | tf_op jit(solution)/shard_map/all_to_all | solution.py:68
  95.4 0.1 fusion.12
  95.5 0.1 reduce_window_sum.11
  95.5 0.2 select_reduce_fusion.1
  95.7 0.1 reduce_sum.57
  95.8 0.1 copy.39
  95.9 0.1 convert_reduce_fusion
  96.0 17.0 %all-to-all-done.1 = f32[128,1,320]{2,1,0:T(1,128)S(1)} async-done(((f32[128,1,320]{2,1,0:T(1,128)}), f32[128,1,320]{2,1,0:T(1,128)S(1)}, u32[]{:S(2)}, u32[]{:S(2)}) %all-to-all-start.1) | async-done | bytes 163872 | tf_op jit(solution)/shard_map/all_to_all | solution.py:68
  113.0 0.6 broadcast.28
  113.5 1.1 reduce.5
  114.6 0.2 reshape.99
  114.9 0.1 fusion.9
  115.1 11.8 %psum.7 = f32[8,1]{0,1:T(1,128)S(1)} all-reduce(f32[8,1]{0,1:T(1,128)S(1)} %bitcast.87), channel_id=1, replica_groups=mesh['head'=8,'ez'=16,'ey'=4] {'head'}, use_global_device_ids=true, to_apply=%region_7.8 | all-reduce | flops 8 | bytes 64 | tf_op jit(solution)/shard_map/psum | solution.py:77
  126.9 0.1 reshape.86
  127.0 0.3 convolution_convert_fusion.1
  127.3 0.7 reshape.79
  128.0 5.0 %all-to-all-start.2 = ((bf16[64,2,640]{2,1,0:T(2,128)(2,1)}), bf16[64,2,640]{2,1,0:T(2,128)(2,1)S(1)}, u32[]{:S(2)}, u32[]{:S(2)}) async-start(bf16[64,2,640]{2,1,0:T(2,128)(2,1)} %reshape.79), calls=%async_computation.2 | async-start | bytes 327680 | tf_op jit(solution)/shard_map/all_to_all | solution.py:98
  133.0 0.0 all-gather.5.cloned.1.call-start
  133.1 0.1 copy.55
  133.2 19.7 %all-to-all-done.2 = bf16[64,2,640]{2,1,0:T(2,128)(2,1)S(1)} async-done(((bf16[64,2,640]{2,1,0:T(2,128)(2,1)}), bf16[64,2,640]{2,1,0:T(2,128)(2,1)S(1)}, u32[]{:S(2)}, u32[]{:S(2)}) %all-to-all-start.2) | async-done | bytes 163872 | tf_op jit(solution)/shard_map/all_to_all | solution.py:98
  153.0 0.7 reshape.80
  153.7 0.0 all-gather.5.cloned.1.call-update
  153.7 1.1 copy.50
  154.8 6.3 %all-to-all-start.4 = ((bf16[96,8,640]{2,0,1:T(8,128)(2,1)}), bf16[96,8,640]{2,0,1:T(8,128)(2,1)S(1)}, u32[]{:S(2)}, u32[]{:S(2)}) async-start(bf16[96,8,640]{2,0,1:T(8,128)(2,1)} %copy.50), calls=%async_computation.4 | async-start | bytes 1966080 | tf_op jit(solution)/shard_map/all_to_all | solution.py:107
  161.1 0.7 reshape.100
  161.9 15.5 %all-gather.5.cloned.1.call-done = bf16[128,5120]{1,0:T(8,128)(2,1)} async-done(((bf16[128,640]{1,0:T(8,128)(2,1)}), bf16[128,5120]{1,0:T(8,128)(2,1)}) %all-gather.5.cloned.1.call-update) | async-done | bytes 1310736 | tf_op jit(solution)/shard_map/all_gather | solution.py:109
  177.4 3.2 %fusion.1 = f32[128,2,96]{0,2,1:T(8,128)S(1)} fusion(bf16[2,96,5120]{1,2,0:T(8,128)(2,1)} %bitcast.74, bf16[128,5120]{1,0:T(8,128)(2,1)} %all-gather.5.cloned.1.call-done), kind=kOutput, calls=%fused_computation.1 | convolution fusion | flops 251658240 | bytes 3375104 | tf_op jit(solution)/shard_map/rd,gfd->rgf/dot_general | solution.py:110
  180.6 13.2 %all_gather.11 = bf16[128,768]{0,1:T(8,128)(2,1)S(1)} all-gather(bf16[128,96]{0,1:T(8,128)(2,1)S(1)} %fusion.11), channel_id=1, replica_groups=mesh['head'=8,'ez'=16,'ey'=4] {'head'}, dimensions={1}, use_global_device_ids=true | all-gather | bytes 221184 | tf_op jit(solution)/shard_map/all_gather | solution.py:112
  193.8 6.2 %all-to-all-start.3 = ((f32[8,1,640]{2,1,0:T(1,128)}), f32[8,1,640]{2,1,0:T(1,128)S(1)}, u32[]{:S(2)}, u32[]{:S(2)}) async-start(f32[8,1,640]{2,1,0:T(1,128)} %reshape.100), calls=%async_computation.3 | async-start | bytes 40960 | tf_op jit(solution)/shard_map/all_to_all | solution.py:105
  200.0 0.3 convolution_convert_fusion
  200.4 0.7 reshape.83
  201.1 2.2 all-to-all-done.3
  203.3 10.6 %all-to-all-start.5 = ((bf16[64,2,640]{2,1,0:T(2,128)(2,1)}), bf16[64,2,640]{2,1,0:T(2,128)(2,1)S(1)}, u32[]{:S(2)}, u32[]{:S(2)}) async-start(bf16[64,2,640]{2,1,0:T(2,128)(2,1)} %reshape.83), calls=%async_computation.5 | async-start | bytes 327680 | tf_op jit(solution)/shard_map/all_to_all | solution.py:115
  214.0 0.1 copy.48
  214.0 0.1 select_reduce_fusion
  214.1 0.7 reduce.6
  214.8 0.1 reshape.101
  214.9 0.1 reshape.81
  215.0 17.8 %all-to-all-done.5 = bf16[64,2,640]{2,1,0:T(2,128)(2,1)S(1)} async-done(((bf16[64,2,640]{2,1,0:T(2,128)(2,1)}), bf16[64,2,640]{2,1,0:T(2,128)(2,1)S(1)}, u32[]{:S(2)}, u32[]{:S(2)}) %all-to-all-start.5) | async-done | bytes 163872 | tf_op jit(solution)/shard_map/all_to_all | solution.py:115
  232.9 0.1 reshape.84
  232.9 0.8 convolution_add_fusion.1
  (25 shorter events, 0.3 us)
Async XLA Ops:
  6.5 1.2 copy-start
  10.0 17.7 %copy-start.2 = (bf16[8,5120]{1,0:T(8,128)(2,1)S(1)}, bf16[8,5120]{1,0:T(8,128)(2,1)}, u32[]{:S(2)}) copy-start(bf16[8,5120]{1,0:T(8,128)(2,1)} %param.18) | copy-start | bytes 245764
  11.7 65.2 %all-to-all-start = ((bf16[16,8,4096]{2,1,0:T(8,128)(2,1)}), bf16[16,8,4096]{2,1,0:T(8,128)(2,1)S(1)}, u32[]{:S(2)}, u32[]{:S(2)}) async-start(bf16[16,8,4096]{2,1,0:T(8,128)(2,1)} %broadcast_in_dim.34), calls=%async_computation | async-start | bytes 2097152 | tf_op jit(solution)/shard_map/all_to_all | solution.py:47
  26.9 50.0 %all-gather.3.cloned.1.call-start = ((), (), s32[]{:S(2)}) async-start(), calls=%async_computation.6 | async-start | bytes 3276800 | tf_op jit(solution)/shard_map/all_gather | solution.py:49
  32.4 4.2 %copy-start.3 = (f32[5120]{0:T(1024)S(1)}, f32[5120]{0:T(1024)}, u32[]{:S(2)}) copy-start(f32[5120]{0:T(1024)} %param.19) | copy-start | bytes 61444
  32.4 4.4 %copy-start.4 = (s32[8,6]{1,0:T(8,128)S(1)}, s32[8,6]{1,0:T(8,128)}, u32[]{:S(2)}) copy-start(s32[8,6]{1,0:T(8,128)} %param.20) | copy-start | bytes 580
  79.9 53.1 %copy-start.1 = (bf16[1,96,5120]{2,1,0:T(8,128)(2,1)S(1)}, bf16[1,96,5120]{2,1,0:T(8,128)(2,1)}, u32[]{:S(2)}) copy-start(bf16[1,96,5120]{2,1,0:T(8,128)(2,1)} %param.23) | copy-start | bytes 2949124
  81.2 31.7 %all-to-all-start.1 = ((f32[128,1,320]{2,1,0:T(1,128)}), f32[128,1,320]{2,1,0:T(1,128)S(1)}, u32[]{:S(2)}, u32[]{:S(2)}) async-start(f32[128,1,320]{2,1,0:T(1,128)} %reshape.98), calls=%async_computation.1 | async-start | bytes 393216 | tf_op jit(solution)/shard_map/all_to_all | solution.py:68
  128.0 24.9 %all-to-all-start.2 = ((bf16[64,2,640]{2,1,0:T(2,128)(2,1)}), bf16[64,2,640]{2,1,0:T(2,128)(2,1)S(1)}, u32[]{:S(2)}, u32[]{:S(2)}) async-start(bf16[64,2,640]{2,1,0:T(2,128)(2,1)} %reshape.79), calls=%async_computation.2 | async-start | bytes 327680 | tf_op jit(solution)/shard_map/all_to_all | solution.py:98
  133.0 44.4 %all-gather.5.cloned.1.call-start = ((), (), s32[]{:S(2)}) async-start(), calls=%async_computation.7 | async-start | bytes 1474560 | tf_op jit(solution)/shard_map/all_gather | solution.py:109
  154.8 39.0 %all-to-all-start.4 = ((bf16[96,8,640]{2,0,1:T(8,128)(2,1)}), bf16[96,8,640]{2,0,1:T(8,128)(2,1)S(1)}, u32[]{:S(2)}, u32[]{:S(2)}) async-start(bf16[96,8,640]{2,0,1:T(8,128)(2,1)} %copy.50), calls=%async_computation.4 | async-start | bytes 1966080 | tf_op jit(solution)/shard_map/all_to_all | solution.py:107
  161.9 52.1 %copy-start.5 = (f32[8,6]{1,0:T(8,128)S(1)}, f32[8,6]{1,0:T(8,128)}, u32[]{:S(2)}) copy-start(f32[8,6]{1,0:T(8,128)} %param.21) | copy-start | bytes 580
  193.8 9.5 %all-to-all-start.3 = ((f32[8,1,640]{2,1,0:T(1,128)}), f32[8,1,640]{2,1,0:T(1,128)S(1)}, u32[]{:S(2)}, u32[]{:S(2)}) async-start(f32[8,1,640]{2,1,0:T(1,128)} %reshape.100), calls=%async_computation.3 | async-start | bytes 40960 | tf_op jit(solution)/shard_map/all_to_all | solution.py:105
  203.3 29.5 %all-to-all-start.5 = ((bf16[64,2,640]{2,1,0:T(2,128)(2,1)}), bf16[64,2,640]{2,1,0:T(2,128)(2,1)S(1)}, u32[]{:S(2)}, u32[]{:S(2)}) async-start(bf16[64,2,640]{2,1,0:T(2,128)(2,1)} %reshape.83), calls=%async_computation.5 | async-start | bytes 327680 | tf_op jit(solution)/shard_map/all_to_all | solution.py:115
Sparse Core Ops, SparseCore 0:
  29.9 44.1 all-gather.2
  153.8 23.5 all-gather.4

commit v12 on v6

--- a/solution.py
+++ b/solution.py
@@ -50,9 +50,9 @@
     column_terms = jnp.einsum(
         "sk,jkc->sjc", gathered, value_blocks, preferred_element_type=jnp.float32
     ).reshape(gathered.shape[0], -1)
-    column_sums = lax.psum(column_terms, "head")
+    column_sums = lax.psum(column_terms.astype(jnp.bfloat16), "head")
     attention = lax.all_to_all(
-        column_sums.astype(jnp.bfloat16), "ez", split_axis=0, concat_axis=1, tiled=True
+        column_sums, "ez", split_axis=0, concat_axis=1, tiled=True
     )
     stream = resid.astype(jnp.float32) + attention.astype(jnp.float32)
     mean_square = jnp.mean(stream * stream, axis=1, keepdims=True)

time: 235 us -> 281 us (1.20)
  waiting for transfers between devices: 107 us -> 174 us
  blocking collectives: 34.8 us -> 12.8 us
    psum x0 -> x1, waiting for transfers between devices: none -> 67.9 us  [on_device(): column_sums = lax.psum(column_terms.astype(jnp.bfloat16), 'head')]
    psum x1 -> x0, blocking collectives: 22 us -> none  [on_device(): column_sums = lax.psum(column_terms, 'head')]
  transfers between devices with their start and end apart: 7 -> 8, of which waited for: 6 -> 7; matrix products, arithmetic and copies ran while one was open for 9% -> 7% of each run, Pallas kernels for 0% -> 0%
where the time goes in v12:
time: 281 us; the launch traced here: 280 us
  waiting for transfers between devices  174 us (62%)
  starting transfers between devices  51.7 us (18%)
  local copies, waits for them, and re-layouts  18 us (6%)
  between operations  13.3 us (5%)
  blocking collectives  12.8 us (5%)
  matrix products  9.05 us (3%)
    psum x1, waiting for transfers between devices, on_device(): column_sums = lax.psum(column_terms.astype(jnp.bfloat16), 'head')  67.9 us
    all_gather x1, waiting for transfers between devices, on_device(): value_blocks = lax.all_gather(w_value_out, 'ey', axis=0, tiled=False)  29.7 us
    all_to_all x1, waiting for transfers between devices, on_device(): lax.all_to_all(summed_rows, EXPERT, split_axis=0, concat_axis=0, tiled=True)  19.3 us
    all_to_all x1, waiting for transfers between devices, on_device(): lax.all_to_all(outgoing, EXPERT, split_axis=0, concat_axis=0, tiled=True)  17.1 us
    all_gather x1, waiting for transfers between devices, on_device(): flat_rows = lax.all_gather(arrived_cols, 'head', axis=1, tiled=True)  17.1 us
    all_to_all x1, starting transfers between devices, on_device(): lax.all_to_all(latent_copies, 'ez', split_axis=0, concat_axis=0, tiled=True)  15.2 us
    all_to_all x1, waiting for transfers between devices, on_device(): lax.all_to_all(column_sums, 'ez', split_axis=0, concat_axis=1, tiled=True)  12.9 us
    all_to_all x1, starting transfers between devices, on_device(): lax.all_to_all(summed_rows, EXPERT, split_axis=0, concat_axis=0, tiled=True)  12.8 us
  transfers between devices with their start and end apart: 8, of which 7 were waited for; matrix products, arithmetic and copies ran while one was open for 7% of the time, Pallas kernels for 0%

profile of v12, /device:TPU:6, one launch (start us, length us, event | category | flops | bytes accessed | tf_op | source)
XLA Modules:
  0.0 280.1 jit_solution(16904736965750733221)
XLA Ops:
  6.5 0.0 copy-start
  6.5 0.0 copy-start.1
  6.5 0.0 all-gather.6.cloned.1.call-start
  6.5 0.7 all-gather.6.cloned.1.call-update
  7.3 1.6 fusion.19
  8.9 1.1 fusion.8
  10.0 0.2 fusion.18
  10.1 0.0 copy-done.1
  10.1 0.0 copy-start.3
  10.1 0.3 fusion.4
  10.5 1.1 broadcast_in_dim.33
  11.6 15.2 %all-to-all-start = ((bf16[16,8,4096]{2,1,0:T(8,128)(2,1)}), bf16[16,8,4096]{2,1,0:T(8,128)(2,1)S(1)}, u32[]{:S(2)}, u32[]{:S(2)}) async-start(bf16[16,8,4096]{2,1,0:T(8,128)(2,1)} %broadcast_in_dim.33), calls=%async_computation | async-start | bytes 2097152 | tf_op jit(solution)/shard_map/all_to_all | solution.py:47
  26.8 0.0 all-reduce.2.cloned.1.call-start
  26.9 0.0 copy-done.3
  26.9 0.1 eq.28
  27.0 0.1 fusion.12
  27.0 0.1 reduce_window_sum.11
  27.1 29.7 %all-gather.6.cloned.1.call-done = bf16[16384,80]{0,1:T(8,128)(2,1)} async-done(((bf16[4096,80]{0,1:T(8,128)(2,1)}), bf16[16384,80]{0,1:T(8,128)(2,1)}) %all-gather.6.cloned.1.call-update) | async-done | bytes 2621456 | tf_op jit(solution)/shard_map/all_gather | solution.py:49
  56.8 5.5 %reshape.55 = bf16[4,4096,80]{1,0,2:T(4,128)(2,1)} reshape(bf16[16384,80]{0,1:T(8,128)(2,1)} %all-gather.6.cloned.1.call-done) | data formatting | bytes 5242880 | tf_op jit(solution)/shard_map/all_gather | solution.py:49
  62.3 4.7 %copy.24 = bf16[4,80,4096]{2,1,0:T(8,128)(2,1)} copy(bf16[4,80,4096]{2,0,1:T(4,128)(2,1)} %bitcast.50) | data formatting | bytes 5242880 | tf_op jit(solution)/shard_map/sk,jkc->sjc/dot_general | solution.py:50
  67.0 9.8 %all-to-all-done = bf16[16,8,4096]{2,1,0:T(8,128)(2,1)S(1)} async-done(((bf16[16,8,4096]{2,1,0:T(8,128)(2,1)}), bf16[16,8,4096]{2,1,0:T(8,128)(2,1)S(1)}, u32[]{:S(2)}, u32[]{:S(2)}) %all-to-all-start) | async-done | bytes 1048608 | tf_op jit(solution)/shard_map/all_to_all | solution.py:47
  76.8 0.0 copy-start.2
  76.8 2.6 convolution_convert_fusion.2
  79.4 0.7 copy.25
  80.2 0.0 all-reduce.2.cloned.1.call-update
  80.2 0.2 select_reduce_fusion.1
  80.4 0.1 reduce_sum.49
  80.5 67.9 %all-reduce.2.cloned.1.call-done = bf16[16,8,320]{2,1,0:T(8,128)(2,1)} async-done(((bf16[16,8,320]{2,1,0:T(8,128)(2,1)}), bf16[16,8,320]{2,1,0:T(8,128)(2,1)}) %all-reduce.2.cloned.1.call-update) | async-done | bytes 81936 | tf_op jit(solution)/shard_map/psum | solution.py:53
  148.3 11.8 %all-to-all-start.1 = ((bf16[16,8,320]{2,1,0:T(8,128)(2,1)}), bf16[16,8,320]{2,1,0:T(8,128)(2,1)S(1)}, u32[]{:S(2)}, u32[]{:S(2)}) async-start(bf16[16,8,320]{2,1,0:T(8,128)(2,1)} %all-reduce.2.cloned.1.call-done), calls=%async_computation.1 | async-start | bytes 196608 | tf_op jit(solution)/shard_map/all_to_all | solution.py:54
  160.2 0.1 copy.27
  160.3 0.8 dynamic-slice
  161.0 0.1 convert_reduce_fusion
  161.1 12.9 %all-to-all-done.1 = bf16[16,8,320]{2,1,0:T(8,128)(2,1)S(1)} async-done(((bf16[16,8,320]{2,1,0:T(8,128)(2,1)}), bf16[16,8,320]{2,1,0:T(8,128)(2,1)S(1)}, u32[]{:S(2)}, u32[]{:S(2)}) %all-to-all-start.1) | async-done | bytes 81952 | tf_op jit(solution)/shard_map/all_to_all | solution.py:54
  174.0 0.1 reshape.54
  174.1 0.0 copy-done.2
  174.2 0.2 multiply_reduce_fusion
  174.3 0.3 convolution_convert_fusion.1
  174.6 0.7 reshape.49
  175.4 6.8 %all-to-all-start.2 = ((bf16[64,2,640]{2,1,0:T(2,128)(2,1)}), bf16[64,2,640]{2,1,0:T(2,128)(2,1)S(1)}, u32[]{:S(2)}, u32[]{:S(2)}) async-start(bf16[64,2,640]{2,1,0:T(2,128)(2,1)} %reshape.49), calls=%async_computation.2 | async-start | bytes 327680 | tf_op jit(solution)/shard_map/all_to_all | solution.py:80
  182.2 0.0 all-gather.4.cloned.1.call-start
  182.3 1.3 copy.31
  183.6 17.1 %all-to-all-done.2 = bf16[64,2,640]{2,1,0:T(2,128)(2,1)S(1)} async-done(((bf16[64,2,640]{2,1,0:T(2,128)(2,1)}), bf16[64,2,640]{2,1,0:T(2,128)(2,1)S(1)}, u32[]{:S(2)}, u32[]{:S(2)}) %all-to-all-start.2) | async-done | bytes 163872 | tf_op jit(solution)/shard_map/all_to_all | solution.py:80
  200.7 0.7 reshape.50
  201.4 0.0 all-gather.4.cloned.1.call-update
  201.4 1.1 copy.29
  202.5 4.9 %all-to-all-start.3 = ((bf16[96,8,640]{2,0,1:T(8,128)(2,1)}), bf16[96,8,640]{2,0,1:T(8,128)(2,1)S(1)}, u32[]{:S(2)}, u32[]{:S(2)}) async-start(bf16[96,8,640]{2,0,1:T(8,128)(2,1)} %copy.29), calls=%async_computation.3 | async-start | bytes 1966080 | tf_op jit(solution)/shard_map/all_to_all | solution.py:85
  207.4 17.1 %all-gather.4.cloned.1.call-done = bf16[128,5120]{1,0:T(8,128)(2,1)} async-done(((bf16[128,640]{1,0:T(8,128)(2,1)}), bf16[128,5120]{1,0:T(8,128)(2,1)}) %all-gather.4.cloned.1.call-update) | async-done | bytes 1310736 | tf_op jit(solution)/shard_map/all_gather | solution.py:87
  224.5 0.0 copy-done
  224.5 2.0 fusion.1
  226.5 0.0 copy-start.4
  226.5 12.8 %all_gather.15 = bf16[128,768]{0,1:T(8,128)(2,1)S(1)} all-gather(bf16[128,96]{0,1:T(8,128)(2,1)S(1)} %fusion.11), channel_id=1, replica_groups=mesh['head'=8,'ez'=16,'ey'=4] {'head'}, dimensions={1}, use_global_device_ids=true | all-gather | bytes 221184 | tf_op jit(solution)/shard_map/all_gather | solution.py:90
  239.3 0.0 all-to-all-done.3
  239.3 0.3 convolution_convert_fusion
  239.7 0.7 reshape.52
  240.4 12.8 %all-to-all-start.4 = ((bf16[64,2,640]{2,1,0:T(2,128)(2,1)}), bf16[64,2,640]{2,1,0:T(2,128)(2,1)S(1)}, u32[]{:S(2)}, u32[]{:S(2)}) async-start(bf16[64,2,640]{2,1,0:T(2,128)(2,1)} %reshape.52), calls=%async_computation.4 | async-start | bytes 327680 | tf_op jit(solution)/shard_map/all_to_all | solution.py:93
  253.2 0.0 copy-done.4
  253.2 0.1 copy.28
  253.3 0.1 select_reduce_fusion
  253.4 19.3 %all-to-all-done.4 = bf16[64,2,640]{2,1,0:T(2,128)(2,1)S(1)} async-done(((bf16[64,2,640]{2,1,0:T(2,128)(2,1)}), bf16[64,2,640]{2,1,0:T(2,128)(2,1)S(1)}, u32[]{:S(2)}, u32[]{:S(2)}) %all-to-all-start.4) | async-done | bytes 163872 | tf_op jit(solution)/shard_map/all_to_all | solution.py:93
  272.7 0.1 reshape.53
  272.8 0.8 convolution_add_fusion.1
  (6 shorter events, 0.1 us)
Async XLA Ops:
  6.5 218.0 %copy-start = (bf16[1,2,96,5120]{3,2,1,0:T(8,128)(2,1)S(1)}, bf16[1,2,96,5120]{3,2,1,0:T(8,128)(2,1)}, u32[]{:S(2)}) copy-start(bf16[1,2,96,5120]{3,2,1,0:T(8,128)(2,1)} %param.22) | copy-start | bytes 5898244
  6.5 3.6 %copy-start.1 = (bf16[8,128,512]{2,1,0:T(8,128)(2,1)S(1)}, bf16[8,128,512]{2,1,0:T(8,128)(2,1)}, u32[]{:S(2)}) copy-start(bf16[8,128,512]{2,1,0:T(8,128)(2,1)} %param.14) | copy-start | bytes 3145732
  6.5 50.3 %all-gather.6.cloned.1.call-start = ((), (), s32[]{:S(2)}) async-start(), calls=%async_computation.7 | async-start | bytes 3276800 | tf_op jit(solution)/shard_map/all_gather | solution.py:49
  10.1 16.7 %copy-start.3 = (s32[8,6]{1,0:T(8,128)S(1)}, s32[8,6]{1,0:T(8,128)}, u32[]{:S(2)}) copy-start(s32[8,6]{1,0:T(8,128)} %param.20) | copy-start | bytes 580
  11.6 65.2 %all-to-all-start = ((bf16[16,8,4096]{2,1,0:T(8,128)(2,1)}), bf16[16,8,4096]{2,1,0:T(8,128)(2,1)S(1)}, u32[]{:S(2)}, u32[]{:S(2)}) async-start(bf16[16,8,4096]{2,1,0:T(8,128)(2,1)} %broadcast_in_dim.33), calls=%async_computation | async-start | bytes 2097152 | tf_op jit(solution)/shard_map/all_to_all | solution.py:47
  26.8 121.5 %all-reduce.2.cloned.1.call-start = ((), (), s32[]{:S(2)}) async-start(), calls=%async_computation.5 | async-start | bytes 196608 | tf_op jit(solution)/shard_map/psum | solution.py:53
  76.8 97.3 %copy-start.2 = (bf16[8,5120]{1,0:T(8,128)(2,1)S(1)}, bf16[8,5120]{1,0:T(8,128)(2,1)}, u32[]{:S(2)}) copy-start(bf16[8,5120]{1,0:T(8,128)(2,1)} %param.18) | copy-start | bytes 245764
  148.3 25.7 %all-to-all-start.1 = ((bf16[16,8,320]{2,1,0:T(8,128)(2,1)}), bf16[16,8,320]{2,1,0:T(8,128)(2,1)S(1)}, u32[]{:S(2)}, u32[]{:S(2)}) async-start(bf16[16,8,320]{2,1,0:T(8,128)(2,1)} %all-reduce.2.cloned.1.call-done), calls=%async_computation.1 | async-start | bytes 196608 | tf_op jit(solution)/shard_map/all_to_all | solution.py:54
  175.4 25.3 %all-to-all-start.2 = ((bf16[64,2,640]{2,1,0:T(2,128)(2,1)}), bf16[64,2,640]{2,1,0:T(2,128)(2,1)S(1)}, u32[]{:S(2)}, u32[]{:S(2)}) async-start(bf16[64,2,640]{2,1,0:T(2,128)(2,1)} %reshape.49), calls=%async_computation.2 | async-start | bytes 327680 | tf_op jit(solution)/shard_map/all_to_all | solution.py:80
  182.2 42.3 %all-gather.4.cloned.1.call-start = ((), (), s32[]{:S(2)}) async-start(), calls=%async_computation.6 | async-start | bytes 1474560 | tf_op jit(solution)/shard_map/all_gather | solution.py:87
  202.5 36.8 %all-to-all-start.3 = ((bf16[96,8,640]{2,0,1:T(8,128)(2,1)}), bf16[96,8,640]{2,0,1:T(8,128)(2,1)S(1)}, u32[]{:S(2)}, u32[]{:S(2)}) async-start(bf16[96,8,640]{2,0,1:T(8,128)(2,1)} %copy.29), calls=%async_computation.3 | async-start | bytes 1966080 | tf_op jit(solution)/shard_map/all_to_all | solution.py:85
  226.5 26.7 %copy-start.4 = (f32[8,6]{1,0:T(8,128)S(1)}, f32[8,6]{1,0:T(8,128)}, u32[]{:S(2)}) copy-start(f32[8,6]{1,0:T(8,128)} %param.21) | copy-start | bytes 580
  240.4 32.3 %all-to-all-start.4 = ((bf16[64,2,640]{2,1,0:T(2,128)(2,1)}), bf16[64,2,640]{2,1,0:T(2,128)(2,1)S(1)}, u32[]{:S(2)}, u32[]{:S(2)}) async-start(bf16[64,2,640]{2,1,0:T(2,128)(2,1)} %reshape.52), calls=%async_computation.4 | async-start | bytes 327680 | tf_op jit(solution)/shard_map/all_to_all | solution.py:93
Sparse Core Ops, SparseCore 0:
  9.5 47.2 all-gather.5
  80.3 67.9 all-reduce.1
  201.5 22.9 all-gather.3

commit v13 on v6

--- a/solution.py
+++ b/solution.py
@@ -76,9 +76,9 @@
     offset = lax.axis_index("head") * col_width
     normed_cols = lax.dynamic_slice_in_dim(normed, offset, col_width, 1)
     outgoing = jnp.dot(selector, normed_cols, preferred_element_type=jnp.float32).astype(jnp.bfloat16)
-    outgoing = outgoing.reshape(expert_count, capacity, -1)
+    outgoing = outgoing.reshape(expert_count, -1)
     arrived = lax.all_to_all(outgoing, EXPERT, split_axis=0, concat_axis=0, tiled=True)
-    arrived_cols = arrived.reshape(-1, arrived.shape[2])
+    arrived_cols = arrived.reshape(expert_count * capacity, -1)
     head_count = lax.axis_size("head")
     down_blocks = w_down[0].reshape(w_down.shape[1], head_count, -1)
     arrived_cols, down_blocks = lax.optimization_barrier((arrived_cols, down_blocks))
@@ -89,7 +89,7 @@
     hidden = (jax.nn.silu(projected[:, 0]) * projected[:, 1]).astype(jnp.bfloat16)
     hidden_all = lax.all_gather(hidden, "head", axis=1, tiled=True)
     summed_cols = jnp.dot(hidden_all, down_cols, preferred_element_type=jnp.float32).astype(jnp.bfloat16)
-    summed_rows = summed_cols.reshape(expert_count, capacity, -1)
+    summed_rows = summed_cols.reshape(expert_count, -1)
     returned = lax.all_to_all(summed_rows, EXPERT, split_axis=0, concat_axis=0, tiled=True)
     back_rows = returned.reshape(expert_count * capacity, -1).astype(jnp.float32)
     mixture = jnp.dot(blending.T, back_rows, precision=lax.Precision.HIGHEST)

time: 235 us -> 242 us (1.030)
  other arithmetic: 0.87 us -> 5.94 us
    all_to_all x0 -> x4, other arithmetic: none -> 5.07 us  [the longest x2 2.54 us: on_device(): lax.all_to_all(summed_rows, EXPERT, split_axis=0, concat_axis=0, tiled=True)]
where the time goes in v13:
time: 242 us; the launch traced here: 241 us
  waiting for transfers between devices  107 us (44%)
  starting transfers between devices  50.8 us (21%)
  blocking collectives  34.8 us (14%)
  local copies, waits for them, and re-layouts  19.5 us (8%)
  between operations  13.7 us (6%)
  matrix products  9.76 us (4%)
  other arithmetic  5.94 us (2%)
    all_gather x1, waiting for transfers between devices, on_device(): value_blocks = lax.all_gather(w_value_out, 'ey', axis=0, tiled=False)  29.5 us
    psum x1, blocking collectives, on_device(): column_sums = lax.psum(column_terms, 'head')  22 us
    all_to_all x1, waiting for transfers between devices, on_device(): lax.all_to_all(summed_rows, EXPERT, split_axis=0, concat_axis=0, tiled=True)  19.3 us
    all_to_all x1, waiting for transfers between devices, on_device(): lax.all_to_all(outgoing, EXPERT, split_axis=0, concat_axis=0, tiled=True)  17.8 us
    all_gather x1, waiting for transfers between devices, on_device(): flat_rows = lax.all_gather(arrived_cols, 'head', axis=1, tiled=True)  17.1 us
    all_to_all x1, starting transfers between devices, on_device(): lax.all_to_all(latent_copies, 'ez', split_axis=0, concat_axis=0, tiled=True)  15.2 us
    all_to_all x1, starting transfers between devices, on_device(): lax.all_to_all(summed_rows, EXPERT, split_axis=0, concat_axis=0, tiled=True)  12.8 us
    all_gather x1, blocking collectives, on_device(): hidden_all = lax.all_gather(hidden, 'head', axis=1, tiled=True)  12.8 us
  transfers between devices with their start and end apart: 7, of which 6 were waited for; matrix products, arithmetic and copies ran while one was open for 9% of the time, Pallas kernels for 0%

profile of v13, /device:TPU:6, one launch (start us, length us, event | category | flops | bytes accessed | tf_op | source)
XLA Modules:
  0.0 241.2 jit_solution(6365685893869408621)
XLA Ops:
  6.5 0.0 copy-start
  6.5 0.0 all-gather.6.cloned.1.call-start
  6.5 0.7 all-gather.6.cloned.1.call-update
  7.3 1.6 fusion.20
  8.9 1.1 fusion.8
  10.0 0.2 fusion.19
  10.1 0.0 copy-done.1
  10.1 0.3 fusion.4
  10.5 1.1 broadcast_in_dim.33
  11.6 15.2 %all-to-all-start = ((bf16[16,8,4096]{2,1,0:T(8,128)(2,1)}), bf16[16,8,4096]{2,1,0:T(8,128)(2,1)S(1)}, u32[]{:S(2)}, u32[]{:S(2)}) async-start(bf16[16,8,4096]{2,1,0:T(8,128)(2,1)} %broadcast_in_dim.33), calls=%async_computation | async-start | bytes 2097152 | tf_op jit(solution)/shard_map/all_to_all | solution.py:47
  26.8 0.0 copy-done.4
  26.8 0.1 eq.28
  26.9 0.1 fusion.13
  27.0 0.1 reduce_window_sum.11
  27.1 0.2 select_reduce_fusion.1
  27.2 0.1 reduce_sum.49
  27.3 29.5 %all-gather.6.cloned.1.call-done = bf16[16384,80]{0,1:T(8,128)(2,1)} async-done(((bf16[4096,80]{0,1:T(8,128)(2,1)}), bf16[16384,80]{0,1:T(8,128)(2,1)}) %all-gather.6.cloned.1.call-update) | async-done | bytes 2621456 | tf_op jit(solution)/shard_map/all_gather | solution.py:49
  56.8 5.5 %reshape.57 = bf16[4,4096,80]{1,0,2:T(4,128)(2,1)} reshape(bf16[16384,80]{0,1:T(8,128)(2,1)} %all-gather.6.cloned.1.call-done) | data formatting | bytes 5242880 | tf_op jit(solution)/shard_map/all_gather | solution.py:49
  62.3 4.7 %copy.32 = bf16[4,80,4096]{2,1,0:T(8,128)(2,1)} copy(bf16[4,80,4096]{2,0,1:T(4,128)(2,1)} %bitcast.50) | data formatting | bytes 5242880 | tf_op jit(solution)/shard_map/sk,jkc->sjc/dot_general | solution.py:50
  67.0 9.8 %all-to-all-done = bf16[16,8,4096]{2,1,0:T(8,128)(2,1)S(1)} async-done(((bf16[16,8,4096]{2,1,0:T(8,128)(2,1)}), bf16[16,8,4096]{2,1,0:T(8,128)(2,1)S(1)}, u32[]{:S(2)}, u32[]{:S(2)}) %all-to-all-start) | async-done | bytes 1048608 | tf_op jit(solution)/shard_map/all_to_all | solution.py:47
  76.8 2.6 %fusion.9 = f32[128,320]{0,1:T(8,128)S(1)} fusion(bf16[320,4096]{1,0:T(8,128)(2,1)} %bitcast.49, bf16[16,8,4096]{2,1,0:T(8,128)(2,1)S(1)} %all-to-all-done), kind=kOutput, calls=%fused_computation.14 | convolution fusion | flops 335544320 | bytes 3833856 | tf_op jit(solution)/shard_map/sk,jkc->sjc/dot_general | solution.py:50
  79.4 22.0 %all-reduce.1 = bf16[128,320]{0,1:T(8,128)(2,1)S(1)} all-reduce(f32[128,320]{0,1:T(8,128)S(1)} %fusion.9), channel_id=1, replica_groups=mesh['head'=8,'ez'=16,'ey'=4] {'head'}, use_global_device_ids=true, to_apply=%region_2.3 | all-reduce | flops 40960 | bytes 245760 | tf_op jit(solution)/shard_map/psum | solution.py:53
  101.4 0.7 copy.33
  102.2 10.2 %all-to-all-start.1 = ((bf16[16,8,320]{2,1,0:T(8,128)(2,1)}), bf16[16,8,320]{2,1,0:T(8,128)(2,1)S(1)}, u32[]{:S(2)}, u32[]{:S(2)}) async-start(bf16[16,8,320]{2,1,0:T(8,128)(2,1)} %bitcast.3), calls=%async_computation.1 | async-start | bytes 196608 | tf_op jit(solution)/shard_map/all_to_all | solution.py:54
  112.4 0.1 copy.35
  112.5 0.8 dynamic-slice
  113.3 0.1 convert_reduce_fusion
  113.3 12.6 %all-to-all-done.1 = bf16[16,8,320]{2,1,0:T(8,128)(2,1)S(1)} async-done(((bf16[16,8,320]{2,1,0:T(8,128)(2,1)}), bf16[16,8,320]{2,1,0:T(8,128)(2,1)S(1)}, u32[]{:S(2)}, u32[]{:S(2)}) %all-to-all-start.1) | async-done | bytes 81952 | tf_op jit(solution)/shard_map/all_to_all | solution.py:54
  126.0 0.1 reshape.56
  126.1 0.0 copy-done.3
  126.1 0.2 multiply_reduce_fusion
  126.3 0.6 copy-done.2
  126.9 0.3 convolution_convert_fusion.1
  127.2 0.1 all_to_all.46
  127.3 0.5 broadcast.38
  127.8 1.6 reduce.2
  129.4 0.7 reshape.61
  130.1 8.0 %all-to-all-start.2 = ((bf16[64,2,640]{2,1,0:T(2,128)(2,1)}), bf16[64,2,640]{2,1,0:T(2,128)(2,1)S(1)}, u32[]{:S(2)}, u32[]{:S(2)}) async-start(bf16[64,2,640]{2,1,0:T(2,128)(2,1)} %reshape.61), calls=%async_computation.2 | async-start | bytes 327680 | tf_op jit(solution)/shard_map/all_to_all | solution.py:80
  138.1 0.0 all-gather.4.cloned.1.call-start
  138.2 1.3 copy.41
  139.5 17.8 %all-to-all-done.2 = bf16[64,2,640]{2,1,0:T(2,128)(2,1)S(1)} async-done(((bf16[64,2,640]{2,1,0:T(2,128)(2,1)}), bf16[64,2,640]{2,1,0:T(2,128)(2,1)S(1)}, u32[]{:S(2)}, u32[]{:S(2)}) %all-to-all-start.2) | async-done | bytes 163872 | tf_op jit(solution)/shard_map/all_to_all | solution.py:80
  157.3 0.1 reshape.62
  157.5 0.9 reduce
  158.4 0.7 reshape.53
  159.1 0.0 all-gather.4.cloned.1.call-update
  159.2 1.1 copy.38
  160.3 4.5 %all-to-all-start.3 = ((bf16[96,8,640]{2,0,1:T(8,128)(2,1)}), bf16[96,8,640]{2,0,1:T(8,128)(2,1)S(1)}, u32[]{:S(2)}, u32[]{:S(2)}) async-start(bf16[96,8,640]{2,0,1:T(8,128)(2,1)} %copy.38), calls=%async_computation.3 | async-start | bytes 1966080 | tf_op jit(solution)/shard_map/all_to_all | solution.py:85
  164.8 17.1 %all-gather.4.cloned.1.call-done = bf16[128,5120]{1,0:T(8,128)(2,1)} async-done(((bf16[128,640]{1,0:T(8,128)(2,1)}), bf16[128,5120]{1,0:T(8,128)(2,1)}) %all-gather.4.cloned.1.call-update) | async-done | bytes 1310736 | tf_op jit(solution)/shard_map/all_gather | solution.py:87
  181.8 2.0 fusion.1
  183.8 0.0 copy-start.5
  183.9 12.8 %all_gather.15 = bf16[128,768]{0,1:T(8,128)(2,1)S(1)} all-gather(bf16[128,96]{0,1:T(8,128)(2,1)S(1)} %fusion.12), channel_id=1, replica_groups=mesh['head'=8,'ez'=16,'ey'=4] {'head'}, dimensions={1}, use_global_device_ids=true | all-gather | bytes 221184 | tf_op jit(solution)/shard_map/all_gather | solution.py:90
  196.7 0.0 all-to-all-done.3
  196.7 0.3 convolution_convert_fusion
  197.0 0.1 all_to_all.47
  197.1 1.6 reduce.3
  198.7 0.7 reshape.63
  199.4 12.8 %all-to-all-start.4 = ((bf16[64,2,640]{2,1,0:T(2,128)(2,1)}), bf16[64,2,640]{2,1,0:T(2,128)(2,1)S(1)}, u32[]{:S(2)}, u32[]{:S(2)}) async-start(bf16[64,2,640]{2,1,0:T(2,128)(2,1)} %reshape.63), calls=%async_computation.4 | async-start | bytes 327680 | tf_op jit(solution)/shard_map/all_to_all | solution.py:93
  212.2 0.1 copy.36
  212.3 0.1 select_reduce_fusion
  212.4 19.3 %all-to-all-done.4 = bf16[64,2,640]{2,1,0:T(2,128)(2,1)S(1)} async-done(((bf16[64,2,640]{2,1,0:T(2,128)(2,1)}), bf16[64,2,640]{2,1,0:T(2,128)(2,1)S(1)}, u32[]{:S(2)}, u32[]{:S(2)}) %all-to-all-start.4) | async-done | bytes 163872 | tf_op jit(solution)/shard_map/all_to_all | solution.py:93
  231.7 0.1 reshape.64
  231.8 0.9 reduce.1
  232.8 0.1 reshape.55
  232.8 1.5 convolution_add_fusion.1
  (12 shorter events, 0.1 us)
Async XLA Ops:
  6.5 175.3 %copy-start = (bf16[1,2,96,5120]{3,2,1,0:T(8,128)(2,1)S(1)}, bf16[1,2,96,5120]{3,2,1,0:T(8,128)(2,1)}, u32[]{:S(2)}) copy-start(bf16[1,2,96,5120]{3,2,1,0:T(8,128)(2,1)} %param.22) | copy-start | bytes 5898244
  6.5 3.6 %copy-start.1 = (bf16[8,128,512]{2,1,0:T(8,128)(2,1)S(1)}, bf16[8,128,512]{2,1,0:T(8,128)(2,1)}, u32[]{:S(2)}) copy-start(bf16[8,128,512]{2,1,0:T(8,128)(2,1)} %param.14) | copy-start | bytes 3145732
  6.5 50.3 %all-gather.6.cloned.1.call-start = ((), (), s32[]{:S(2)}) async-start(), calls=%async_computation.6 | async-start | bytes 3276800 | tf_op jit(solution)/shard_map/all_gather | solution.py:49
  10.4 16.4 %copy-start.4 = (s32[8,6]{1,0:T(8,128)S(1)}, s32[8,6]{1,0:T(8,128)}, u32[]{:S(2)}) copy-start(s32[8,6]{1,0:T(8,128)} %param.20) | copy-start | bytes 580
  11.6 65.2 %all-to-all-start = ((bf16[16,8,4096]{2,1,0:T(8,128)(2,1)}), bf16[16,8,4096]{2,1,0:T(8,128)(2,1)S(1)}, u32[]{:S(2)}, u32[]{:S(2)}) async-start(bf16[16,8,4096]{2,1,0:T(8,128)(2,1)} %broadcast_in_dim.33), calls=%async_computation | async-start | bytes 2097152 | tf_op jit(solution)/shard_map/all_to_all | solution.py:47
  76.8 49.3 %copy-start.3 = (bf16[8,5120]{1,0:T(8,128)(2,1)S(1)}, bf16[8,5120]{1,0:T(8,128)(2,1)}, u32[]{:S(2)}) copy-start(bf16[8,5120]{1,0:T(8,128)(2,1)} %param.18) | copy-start | bytes 245764
  102.2 23.7 %all-to-all-start.1 = ((bf16[16,8,320]{2,1,0:T(8,128)(2,1)}), bf16[16,8,320]{2,1,0:T(8,128)(2,1)S(1)}, u32[]{:S(2)}, u32[]{:S(2)}) async-start(bf16[16,8,320]{2,1,0:T(8,128)(2,1)} %bitcast.3), calls=%async_computation.1 | async-start | bytes 196608 | tf_op jit(solution)/shard_map/all_to_all | solution.py:54
  126.2 0.7 copy-start.2
  130.1 27.3 %all-to-all-start.2 = ((bf16[64,2,640]{2,1,0:T(2,128)(2,1)}), bf16[64,2,640]{2,1,0:T(2,128)(2,1)S(1)}, u32[]{:S(2)}, u32[]{:S(2)}) async-start(bf16[64,2,640]{2,1,0:T(2,128)(2,1)} %reshape.61), calls=%async_computation.2 | async-start | bytes 327680 | tf_op jit(solution)/shard_map/all_to_all | solution.py:80
  138.1 43.7 %all-gather.4.cloned.1.call-start = ((), (), s32[]{:S(2)}) async-start(), calls=%async_computation.5 | async-start | bytes 1474560 | tf_op jit(solution)/shard_map/all_gather | solution.py:87
  160.3 36.4 %all-to-all-start.3 = ((bf16[96,8,640]{2,0,1:T(8,128)(2,1)}), bf16[96,8,640]{2,0,1:T(8,128)(2,1)S(1)}, u32[]{:S(2)}, u32[]{:S(2)}) async-start(bf16[96,8,640]{2,0,1:T(8,128)(2,1)} %copy.38), calls=%async_computation.3 | async-start | bytes 1966080 | tf_op jit(solution)/shard_map/all_to_all | solution.py:85
  183.8 28.4 %copy-start.5 = (f32[8,6]{1,0:T(8,128)S(1)}, f32[8,6]{1,0:T(8,128)}, u32[]{:S(2)}) copy-start(f32[8,6]{1,0:T(8,128)} %param.21) | copy-start | bytes 580
  199.4 32.3 %all-to-all-start.4 = ((bf16[64,2,640]{2,1,0:T(2,128)(2,1)}), bf16[64,2,640]{2,1,0:T(2,128)(2,1)S(1)}, u32[]{:S(2)}, u32[]{:S(2)}) async-start(bf16[64,2,640]{2,1,0:T(2,128)(2,1)} %reshape.63), calls=%async_computation.4 | async-start | bytes 327680 | tf_op jit(solution)/shard_map/all_to_all | solution.py:93
Sparse Core Ops, SparseCore 0:
  9.5 47.2 all-gather.5
  159.3 22.4 all-gather.3
